TPU v7x, 256 devices: a whole 4x4x8 slice. The times are simulated.
256 devices in a mesh: section: 4 (over z_lo, core), seq: 64 (over y, x, z_hi).
Axes of the slice: x: 4, y: 4, z: 8 (z_hi: 4, z_lo: 2; z = z_hi * 2 + z_lo), core: 2. Of those that a mesh axis runs over, the one named last changes fastest.
Arguments:
- q_img: bfloat16 [8192, 3072], P('seq', 'section'), may hold values from -6 to 6
- k_img: bfloat16 [8192, 3072], P('seq', 'section'), may hold values from -6 to 6
- v_img: bfloat16 [8192, 3072], P('seq', 'section'), may hold values from -6 to 6
- q_txt: bfloat16 [256, 3072], P('seq', 'section'), may hold values from -6 to 6
- k_txt: bfloat16 [256, 3072], P('seq', 'section'), may hold values from -6 to 6
- v_txt: bfloat16 [256, 3072], P('seq', 'section'), may hold values from -6 to 6
- norm_gains: float32 [4, 128], replicated, may hold values from 1.2 to 2
- block_map: int32 [24, 64, 64], P('section', 'seq'), may hold values 0 or 1
Outputs:
- image_out: bfloat16 [2048, 4, 3072], P('seq', 'section')
- text_out: bfloat16 [256, 3072], P('seq', 'section')
All inputs are finite; a program needn't handle non-finite values. No bound on the sum of `block_map` on one device may be relied on, other than what follows from the above.
Results may differ from a plain program's by a relative error of at most 0.011.
Values may be sent and summed in bfloat16 or wider, within the bound.
No kernel may reach another device: no remote copies, remote signals or barrier semaphores. Data moves between devices by JAX's collectives and lax.ppermute only.
A program may use at most 256 MiB of HBM per device.

v0:
```python
import jax
import jax.numpy as jnp
from jax import lax
from jax.sharding import PartitionSpec as P

BLOCK = 128


def normed(values, gain, heads):
    rows = values.shape[0]
    floats = values.astype(jnp.float32).reshape(rows, heads, gain.shape[0])
    power = jnp.mean(floats * floats, axis=-1, keepdims=True)
    return (floats * lax.rsqrt(power + 1e-06) * gain).astype(jnp.bfloat16)


def make_keep(flags, query_shards, shards, first, rows, text_rows):
    heads = flags.shape[0]
    key_blocks = rows // BLOCK
    stride = rows + text_rows
    picked = lax.dynamic_slice_in_dim(flags, first * key_blocks, shards * key_blocks, 2)
    picked = picked.reshape(heads, query_shards, key_blocks, shards, key_blocks)
    image_mask = jnp.broadcast_to(
        picked[:, :, :, None, :, :, None] > 0,
        (heads, query_shards, key_blocks, BLOCK, shards, key_blocks, BLOCK),
    )
    image_mask = image_mask.reshape(heads, query_shards, rows, shards, rows)
    keep = jnp.pad(
        image_mask, ((0, 0), (0, 0), (0, text_rows), (0, 0), (0, text_rows)), constant_values=True
    )
    return keep.reshape(heads, query_shards * stride, shards, stride)


def accumulate(queries, flags, query_shards, rows, text_rows, carry, pieces, start):
    numer, denom = carry
    piece_keys, piece_values = pieces
    heads = queries.shape[1]
    head_size = queries.shape[2]
    stride = rows + text_rows
    shards = piece_keys.shape[0] // stride
    first = start // stride
    keys_four = piece_keys.reshape(shards, stride, heads, head_size)
    values_four = piece_values.reshape(shards, stride, heads, head_size)
    scores = jnp.einsum(
        "qhd,skhd->hqsk", queries, keys_four, preferred_element_type=jnp.float32
    ) * head_size ** (-0.5)
    keep = make_keep(flags, query_shards, shards, first, rows, text_rows)
    weights = jnp.where(keep, jnp.exp(scores), jnp.float32(0.0))
    denom = denom + jnp.sum(weights, axis=(2, 3))
    numer = numer + jnp.einsum(
        "hqsk,skhd->hqd",
        weights.astype(jnp.bfloat16),
        values_four,
        preferred_element_type=jnp.float32,
    )
    return (numer, denom)


def body(q_img, k_img, v_img, q_txt, k_txt, v_txt, norm_gains, block_map):
    rows, width = q_img.shape
    head_size = norm_gains.shape[1]
    heads = width // head_size
    text_rows = q_txt.shape[0]
    stride = rows + text_rows
    queries = jnp.concatenate(
        [normed(q_img, norm_gains[0], heads), normed(q_txt, norm_gains[2], heads)], axis=0
    )
    keys_image = normed(k_img, norm_gains[1], heads).reshape(rows, width)
    keys_text = normed(k_txt, norm_gains[3], heads).reshape(text_rows, width)
    local_keys = jnp.concatenate([keys_image, keys_text], axis=0)
    local_values = jnp.concatenate([v_img, v_txt], axis=0)
    start_state = (
        jnp.zeros((heads, stride, head_size), jnp.float32),
        jnp.zeros((heads, stride), jnp.float32),
    )

    def fold_step(carry, pieces, start):
        return accumulate(queries, block_map, 1, rows, text_rows, carry, pieces, start)

    whole_keys, whole_values = (
        lax.all_gather(local_keys, "seq", axis=0, tiled=True),
        lax.all_gather(local_values, "seq", axis=0, tiled=True),
    )
    count_seq = lax.axis_size("seq")
    grouped = 1
    while (
        grouped * 2 <= count_seq
        and count_seq % (grouped * 2) == 0
        and (grouped * 2 * stride <= 1024)
    ):
        grouped = grouped * 2
    span = grouped * stride

    def step_over(index, carry):
        offset = index * span
        piece_keys = lax.dynamic_slice_in_dim(whole_keys, offset, span, 0)
        piece_values = lax.dynamic_slice_in_dim(whole_values, offset, span, 0)
        return fold_step(carry, (piece_keys, piece_values), offset)

    numer, denom = lax.fori_loop(0, count_seq // grouped, step_over, start_state)
    result = numer / denom[..., None]
    merged = result.transpose(1, 0, 2).reshape(stride, width).astype(jnp.bfloat16)
    image_part = merged[:rows]
    text_out = merged[rows:]
    sections = lax.axis_size("section")
    image_out = lax.all_to_all(
        image_part.reshape(rows // sections, sections, width),
        "section",
        split_axis=1,
        concat_axis=2,
        tiled=True,
    )
    return (image_out, text_out)


def solution(mesh):
    placed = (
        P("seq", "section"),
        P("seq", "section"),
        P("seq", "section"),
        P("seq", "section"),
        P("seq", "section"),
        P("seq", "section"),
        P(),
        P("section", "seq", None),
    )
    return jax.shard_map(
        body,
        mesh=mesh,
        in_specs=placed,
        out_specs=(P("seq", "section", None), P("seq", "section")),
        check_vma=False,
    )
```

profile of v0, /device:TPU:1, one launch (start us, length us, event | category | flops | bytes accessed | tf_op | source)
XLA Modules:
  0.0 707.2 jit_solution(929896019080219932)
XLA Ops:
  14.1 138.3 %all-gather.5.cloned.1.call-done = bf16[64,132,768]{2,1,0:T(8,128)(2,1)} async-done(((bf16[1,132,768]{2,1,0:T(8,128)(2,1)}), bf16[64,132,768]{2,1,0:T(8,128)(2,1)}) %all-gather.5.cloned.1.call-update) | async-done | bytes 12976144 | tf_op jit(solution)/shard_map/all_gather | solution.py:80
  152.4 16.0 %reshape.141 = bf16[8448,768]{1,0:T(8,128)(2,1)} reshape(bf16[64,132,768]{2,1,0:T(8,128)(2,1)} %all-gather.5.cloned.1.call-done) | data formatting | bytes 25952256
  168.4 131.9 %all-gather.7.cloned.1.call-done = bf16[64,132,768]{2,1,0:T(8,128)(2,1)} async-done(((bf16[1,132,768]{2,1,0:T(8,128)(2,1)}), bf16[64,132,768]{2,1,0:T(8,128)(2,1)}) %all-gather.7.cloned.1.call-update) | async-done | bytes 12976144 | tf_op jit(solution)/shard_map/all_gather | solution.py:81
  300.3 16.1 %reshape.143 = bf16[8448,768]{1,0:T(8,128)(2,1)} reshape(bf16[64,132,768]{2,1,0:T(8,128)(2,1)} %all-gather.7.cloned.1.call-done) | data formatting | bytes 25952256
  316.4 363.8 %while.18 = (s32[]{:T(128)}, f32[6,132,128]{2,1,0:T(8,128)}, f32[6,132]{1,0:T(8,128)S(1)}, s32[6,1,64]{0,2,1:T(8,128)S(1)}, bf16[8448,768]{1,0:T(8,128)(2,1)}, /...) while((s32[]{:T(128)}, f32[6,132,128]{2,1,0:T(8,128)}, ...), condition=%wide.region_6.7_spmd.clone, body=%wide.region_4.6_spmd.clone.sunk | while | flops 215982384 | bytes 21925776 | solution.py:99
  323.2 4.7 copy.123
  345.9 4.7 copy.123
  368.6 4.7 copy.123
  379.3 3.3 fusion.36
  391.4 4.7 copy.123
  414.1 4.7 copy.123
  436.8 4.7 copy.123
  459.6 4.7 copy.123
  482.3 4.7 copy.123
  505.1 4.7 copy.123
  527.8 4.7 copy.123
  550.6 4.7 copy.123
  573.3 4.7 copy.123
  596.1 4.7 copy.123
  618.8 4.7 copy.123
  641.6 4.7 copy.123
  664.3 4.7 copy.123
  682.4 12.9 %all-to-all-start = ((bf16[32,4,768]{2,0,1:T(8,128)(2,1)}), bf16[32,4,768]{2,0,1:T(8,128)(2,1)S(1)}, u32[]{:S(2)}, u32[]{:S(2)}) async-start(bf16[32,4,768]{2,0,1:T(8,128)(2,1)} %copy.97), calls=%async_computation | async-start | bytes 393216 | tf_op jit(solution)/shard_map/all_to_all | solution.py:105
  695.9 3.5 all-to-all-done
  (259 shorter events, 294.4 us)
Async XLA Ops:
  7.2 5.1 copy-start.1
  7.2 5.1 copy-start.3
  7.2 5.8 copy-start.4
  7.2 6.0 copy-start.2
  7.2 145.2 %all-gather.5.cloned.1.call-start = ((), (), s32[]{:S(2)}) async-start(), calls=%async_computation.1 | async-start | bytes 13578240 | tf_op jit(solution)/shard_map/all_gather | solution.py:80
  11.1 2.9 copy-start.5
  12.2 288.1 %all-gather.7.cloned.1.call-start = ((), (), s32[]{:S(2)}) async-start(), calls=%async_computation.2 | async-start | bytes 13578240 | tf_op jit(solution)/shard_map/all_gather | solution.py:81
  333.9 3.2 copy-start
  356.5 3.3 copy-start
  379.3 3.3 copy-start
  402.0 3.3 copy-start
  424.7 3.3 copy-start
  447.5 3.3 copy-start
  470.2 3.3 copy-start
  493.0 3.3 copy-start
  515.7 3.3 copy-start
  538.5 3.3 copy-start
  561.2 3.3 copy-start
  584.0 3.3 copy-start
  606.7 3.3 copy-start
  629.5 3.3 copy-start
  652.2 3.3 copy-start
  674.9 3.3 copy-start
  682.4 17.0 %all-to-all-start = ((bf16[32,4,768]{2,0,1:T(8,128)(2,1)}), bf16[32,4,768]{2,0,1:T(8,128)(2,1)S(1)}, u32[]{:S(2)}, u32[]{:S(2)}) async-start(bf16[32,4,768]{2,0,1:T(8,128)(2,1)} %copy.97), calls=%async_computation | async-start | bytes 393216 | tf_op jit(solution)/shard_map/all_to_all | solution.py:105
Sparse Core Ops, SparseCore 0:
  12.3 140.0 all-gather.4
  155.7 144.5 all-gather.6
where the time goes:
time: 711 us; the launch traced here: 707 us
  waiting for transfers between devices  274 us (39%)
  local copies, waits for them, and re-layouts  229 us (32%)
  matrix products  89.9 us (13%)
  other arithmetic  86 us (12%)
  between operations  14.3 us (2%)
  starting transfers between devices  13 us (2%)
    all_gather x1, waiting for transfers between devices, body(): lax.all_gather(local_keys, 'seq', axis=0, tiled=True)  138 us
    all_gather x1, waiting for transfers between devices, body(): lax.all_gather(local_values, 'seq', axis=0, tiled=True)  132 us
    while x48, local copies, waits for them, and re-layouts  75.5 us
    dot_general x16, matrix products, accumulate(): jnp.einsum('hqsk,skhd->hqd', weights.astype(jnp.bfloat16), values_four, p...  52.2 us
    convert_element_type x16, other arithmetic, accumulate(): weights.astype(jnp.bfloat16)  50.4 us
    reshape x16, local copies, waits for them, and re-layouts, accumulate(): values_four = piece_values.reshape(shards, stride, heads, head_size)  44.4 us
    dynamic_slice x16, local copies, waits for them, and re-layouts, step_over(): piece_values = lax.dynamic_slice_in_dim(whole_values, offset, span, 0)  38.4 us
    dot_general x16, matrix products, accumulate(): jnp.einsum('qhd,skhd->hqsk', queries, keys_four, preferred_element_type=j...  37.6 us
  transfers between devices with their start and end apart: 3, of which 3 were waited for; matrix products, arithmetic and copies ran while one was open for 3% of the time, Pallas kernels for 0%

commit v1 on v0

v1 whole, which is shorter than its diff:
```python
import jax
import jax.numpy as jnp
from jax import lax
from jax.sharding import Mesh, PartitionSpec as P

BLOCK = 128
QUERY_GROUP = 4


def normed(values, gain, heads):
    rows = values.shape[0]
    floats = values.astype(jnp.float32).reshape(rows, heads, gain.shape[0])
    power = jnp.mean(floats * floats, axis=-1, keepdims=True)
    return (floats * lax.rsqrt(power + 1e-06) * gain).astype(jnp.bfloat16)


def body(q_img, k_img, v_img, q_txt, k_txt, v_txt, norm_gains, block_map):
    rows, width = q_img.shape
    head_size = norm_gains.shape[1]
    heads = width // head_size
    text_rows = q_txt.shape[0]
    stride = rows + text_rows
    groups_q = lax.axis_size("qq")
    groups_k = lax.axis_size("kk")
    own_q = lax.axis_index("qq")

    queries = jnp.concatenate(
        [normed(q_img, norm_gains[0], heads), normed(q_txt, norm_gains[2], heads)], axis=0
    )
    keys = jnp.concatenate(
        [normed(k_img, norm_gains[1], heads), normed(k_txt, norm_gains[3], heads)], axis=0
    )
    values = jnp.concatenate([v_img, v_txt], axis=0).reshape(stride, heads, head_size)
    pair = jnp.stack([keys, values], axis=1)

    all_q = lax.all_gather(queries, "qq", axis=0, tiled=True)
    all_kv = lax.all_gather(pair, "kk", axis=0, tiled=True)
    flags = lax.all_gather(block_map, "qq", axis=1, tiled=True)
    flags = flags.reshape(heads, groups_q, groups_k, groups_q)
    flags = lax.dynamic_index_in_dim(flags, own_q, axis=3, keepdims=False)

    all_k = all_kv[:, 0]
    all_v = all_kv[:, 1]
    scores = jnp.einsum(
        "qhd,khd->hqk", all_q, all_k, preferred_element_type=jnp.float32
    ) * head_size ** (-0.5)
    scores = scores.reshape(heads, groups_q, stride, groups_k, stride)
    image_q = jnp.arange(stride) < rows
    text_pair = ~(image_q[:, None, None] & image_q[None, None, :])
    keep = (flags[:, :, None, :, None] > 0) | text_pair[None, None]
    weights = jnp.where(keep, jnp.exp(scores), jnp.float32(0.0))
    denom = jnp.sum(weights, axis=(3, 4)).reshape(heads, groups_q * stride)
    weights = weights.reshape(heads, groups_q * stride, groups_k * stride)
    numer = jnp.einsum(
        "hqk,khd->hqd",
        weights.astype(jnp.bfloat16),
        all_v,
        preferred_element_type=jnp.float32,
    )
    numer = lax.psum_scatter(numer, "qq", scatter_dimension=1, tiled=True)
    denom = lax.psum_scatter(denom, "qq", scatter_dimension=1, tiled=True)
    result = numer / denom[..., None]
    merged = result.transpose(1, 0, 2).reshape(stride, width).astype(jnp.bfloat16)
    image_part = merged[:rows]
    text_out = merged[rows:]
    sections = lax.axis_size("section")
    image_out = lax.all_to_all(
        image_part.reshape(rows // sections, sections, width),
        "section",
        split_axis=1,
        concat_axis=2,
        tiled=True,
    )
    return (image_out, text_out)


def solution(mesh):
    sections, seq = mesh.devices.shape
    grid = Mesh(
        mesh.devices.reshape(sections, seq // QUERY_GROUP, QUERY_GROUP),
        ("section", "kk", "qq"),
    )
    rows = ("kk", "qq")
    placed = (
        P(rows, "section"),
        P(rows, "section"),
        P(rows, "section"),
        P(rows, "section"),
        P(rows, "section"),
        P(rows, "section"),
        P(),
        P("section", rows, None),
    )
    return jax.shard_map(
        body,
        mesh=grid,
        in_specs=placed,
        out_specs=(P(rows, "section", None), P(rows, "section")),
        check_vma=False,
    )
```

time: 711 us -> 253 us (0.36)
  waiting for transfers between devices: 274 us -> 75.2 us
  local copies, waits for them, and re-layouts: 229 us -> 75.7 us
  other arithmetic: 86 us -> 3.64 us
  matrix products: 89.9 us -> 27.2 us
  blocking collectives: 0 us -> 50.5 us
  starting transfers between devices: 13 us -> 4.24 us
    all_gather x2 -> x1, waiting for transfers between devices: 270 us -> 0.01 us  [body(): all_kv = lax.all_gather(pair, 'kk', axis=0, tiled=True)]
    while x48 -> x0, local copies, waits for them, and re-layouts: 75.5 us -> none
    reshape x48 -> x1, local copies, waits for them, and re-layouts: 75.3 us -> 0.13 us  [body(): flags = flags.reshape(heads, groups_q, groups_k, groups_q)]
    unnamed x2 -> x3, waiting for transfers between devices: 0.03 us -> 71.7 us
    dot_general x32 -> x2, matrix products: 89.9 us -> 27.2 us  [the longest x1 15.3 us: body(): jnp.einsum('qhd,khd->hqk', all_q, all_k, preferred_element_type=jnp.float32)]
    or x0 -> x4, local copies, waits for them, and re-layouts: none -> 51.5 us  [body(): keep = (flags[:, :, None, :, None] > 0) | text_pair[None, None]]
    convert_element_type x16 -> x0, other arithmetic: 50.4 us -> none  [accumulate(): weights.astype(jnp.bfloat16)]
    dynamic_slice x16 -> x0, local copies, waits for them, and re-layouts: 38.4 us -> none  [step_over(): piece_values = lax.dynamic_slice_in_dim(whole_values, offset, span, 0)]
  transfers between devices with their start and end apart: 3 -> 3, of which waited for: 3 -> 2; matrix products, arithmetic and copies ran while one was open for 3% -> 22% of each run, Pallas kernels for 0% -> 0%
where the time goes in v1:
time: 253 us; the launch traced here: 251 us
  local copies, waits for them, and re-layouts  75.7 us (30%)
  waiting for transfers between devices  75.2 us (30%)
  blocking collectives  50.5 us (20%)
  matrix products  27.2 us (11%)
  between operations  14.9 us (6%)
  starting transfers between devices  4.24 us (2%)
  other arithmetic  3.64 us (1%)
    unnamed x3, waiting for transfers between devices  71.7 us
    or x4, local copies, waits for them, and re-layouts, body(): keep = (flags[:, :, None, :, None] > 0) | text_pair[None, None]  51.5 us
    all_gather x1, blocking collectives, body(): all_q = lax.all_gather(queries, 'qq', axis=0, tiled=True)  20.9 us
    all_gather x1, blocking collectives, body(): flags = lax.all_gather(block_map, 'qq', axis=1, tiled=True)  15.4 us
    dot_general x1, matrix products, body(): jnp.einsum('qhd,khd->hqk', all_q, all_k, preferred_element_type=jnp.float32)  15.3 us
    unnamed x1, blocking collectives  14.3 us
    slice x1, local copies, waits for them, and re-layouts, body(): all_v = all_kv[:, 1]  13.8 us
    dot_general x1, matrix products, body(): jnp.einsum('hqk,khd->hqd', weights.astype(jnp.bfloat16), all_v, preferred...  11.9 us
  transfers between devices with their start and end apart: 3, of which 2 were waited for; matrix products, arithmetic and copies ran while one was open for 22% of the time, Pallas kernels for 0%

profile of v1, /device:TPU:1, one launch (start us, length us, event | category | flops | bytes accessed | tf_op | source)
XLA Modules:
  0.0 251.3 jit_solution(8729990873441594041)
XLA Ops:
  7.2 0.8 slice_bitcast_fusion.4
  8.1 0.8 copy.36
  9.0 0.8 copy.33
  9.9 1.1 copy.35
  11.1 1.1 copy.32
  12.2 1.0 pad_maximum_fusion.2
  13.9 1.2 copy.38
  15.2 1.0 copy.34
  16.2 15.4 %all_gather.9 = s32[6,4,64]{2,0,1:T(8,128)S(1)} all-gather(s32[6,1,64]{2,0,1:T(8,128)S(1)} %copy.30), channel_id=1, replica_groups=mesh['section'=4,'kk'=16,'qq'=4] {'qq'}, dimensions={1}, use_global_device_ids=true | all-gather | bytes 7680 | tf_op jit(solution)/shard_map/all_gather | solution.py:38
  31.7 0.6 fusion.11
  32.3 5.4 %or.21 = pred[6,4,132,16,132]{4,3,2,1,0:T(8,128)(4,1)} broadcast(pred[6,4,16]{2,1,0:T(4,128)(4,1)S(1)} %fusion.11), dimensions={0,1,3} | broadcast | bytes 6691200 | tf_op jit(solution)/shard_map/or | solution.py:50
  37.7 39.4 %or.22 = pred[6,528,2112]{2,1,0:T(8,128)(4,1)} reshape(pred[6,4,132,16,132]{4,3,2,1,0:T(8,128)(4,1)} %or.21) | data formatting | bytes 13381632 | tf_op jit(solution)/shard_map/or | solution.py:50
  77.7 6.1 %or.24 = pred[528,2112]{1,0:T(8,128)(4,1)S(1)} reshape(pred[4,132,16,132]{3,2,1,0:T(8,128)(4,1)S(1)} %or.23) | data formatting | bytes 2230272 | tf_op jit(solution)/shard_map/or | solution.py:50
  83.9 20.9 %all_gather.10 = bf16[528,6,128]{2,1,0:T(8,128)(2,1)S(1)} all-gather(bf16[132,6,128]{2,1,0:T(8,128)(2,1)} %copy.34), channel_id=1, replica_groups=mesh['section'=4,'kk'=16,'qq'=4] {'qq'}, dimensions={0}, use_global_device_ids=true | all-gather | bytes 1013760 | tf_op jit(solution)/shard_map/all_gather | solution.py:36
  104.8 13.8 %fusion.12 = (bf16[2112,1,6,128]{3,1,2,0:T(2,128)(2,1)}, bf16[2112,1,6,128]{3,1,2,0:T(2,128)(2,1)}) fusion(bf16[2112,2,6,128]{3,1,2,0:T(2,128)(2,1)} %all-gather.2.cloned.1.call-done), kind=kLoop, calls=%fused_computation.41 | loop fusion | bytes 12976128 | tf_op jit(solution)/shard_map/slice | solution.py:43
  118.6 15.3 %fusion.13 = (f32[6,528]{1,0:T(8,128)S(1)}, bf16[6,528,2112]{2,1,0:T(8,128)(2,1)}) fusion(bf16[2112,1,6,128]{3,1,2,0:T(2,128)(2,1)} %get-tuple-element.3, bf16[528,6,128]{2,1,0:T(8,128)(2,1)S(1)} %all_gather.10, pred[6,528,2112]{2,1,0:T(8,128)(4,1)} %or.22, pred[528,2112]{1,0:T(8,128)(4,1)S(1)} %or.24), kind=kOutput, calls=%fused_computation.42 | convolution fusion | flops 1746299776 | bytes 25255296 | tf_op jit(solution)/shard_map/qhd,khd->hqk/dot_general | solution.py:44
  133.9 11.9 %fusion = f32[6,528,128]{2,1,0:T(8,128)} fusion(bf16[6,528,2112]{2,1,0:T(8,128)(2,1)} %get-tuple-element.9, bf16[2112,1,6,128]{3,1,2,0:T(2,128)(2,1)} %get-tuple-element.2), kind=kOutput, calls=%fused_computation.1 | convolution fusion | flops 1712848896 | bytes 18247680 | tf_op jit(solution)/shard_map/hqk,khd->hqd/dot_general | solution.py:54
  147.1 14.3 %all-reduce.1 = f32[6,528]{1,0:T(8,128)S(1)} all-reduce(f32[6,528]{1,0:T(8,128)S(1)} %get-tuple-element.8), channel_id=3, replica_groups=mesh['section'=4,'kk'=16,'qq'=4] {'qq'}, use_global_device_ids=true, to_apply=%region_6.7.clone | all-reduce | flops 3168 | bytes 25344
  161.4 71.6 %all-reduce.4.cloned.1.call-done = f32[6,528,128]{2,1,0:T(8,128)} async-done(((f32[6,528,128]{2,1,0:T(8,128)}), f32[6,528,128]{2,1,0:T(8,128)}) %all-reduce.4.cloned.1.call-update) | async-done | bytes 1622032
  233.0 1.2 fusion.10
  234.5 0.7 copy.43
  235.2 4.2 %all-to-all-start = ((bf16[32,4,768]{2,0,1:T(8,128)(2,1)}), bf16[32,4,768]{2,0,1:T(8,128)(2,1)S(1)}, u32[]{:S(2)}, u32[]{:S(2)}) async-start(bf16[32,4,768]{2,0,1:T(8,128)(2,1)} %copy.43), calls=%async_computation | async-start | bytes 393216 | tf_op jit(solution)/shard_map/all_to_all | solution.py:67
  240.0 3.5 %all-to-all-done = bf16[32,4,768]{2,0,1:T(8,128)(2,1)S(1)} async-done(((bf16[32,4,768]{2,0,1:T(8,128)(2,1)}), bf16[32,4,768]{2,0,1:T(8,128)(2,1)S(1)}, u32[]{:S(2)}, u32[]{:S(2)}) %all-to-all-start) | async-done | bytes 196640 | tf_op jit(solution)/shard_map/all_to_all | solution.py:67
  243.6 0.8 all_to_all.10
  (36 shorter events, 3.6 us)
Async XLA Ops:
  7.2 9.0 %copy-start = (s32[6,1,64]{2,1,0:T(1,128)S(1)}, s32[6,1,64]{2,1,0:T(1,128)}, u32[]{:S(2)}) copy-start(s32[6,1,64]{2,1,0:T(1,128)} %param.15) | copy-start | bytes 4612
  7.2 97.6 %all-gather.2.cloned.1.call-start = ((), (), s32[]{:S(2)}) async-start(), calls=%async_computation.1 | async-start | bytes 6893568 | tf_op jit(solution)/shard_map/all_gather | solution.py:37
  15.1 217.9 %all-reduce.4.cloned.1.call-start = ((), (), s32[]{:S(2)}) async-start(), calls=%async_computation.2 | async-start | bytes 3244032
  133.9 11.9 %copy-start.1 = (u32[256]{0:T(256)S(1)}, u32[256]{0:T(256)}, u32[]{:S(2)}) copy-start(u32[256]{0:T(256)} %constant.33) | copy-start | bytes 3076
  235.2 8.3 %all-to-all-start = ((bf16[32,4,768]{2,0,1:T(8,128)(2,1)}), bf16[32,4,768]{2,0,1:T(8,128)(2,1)S(1)}, u32[]{:S(2)}, u32[]{:S(2)}) async-start(bf16[32,4,768]{2,0,1:T(8,128)(2,1)} %copy.43), calls=%async_computation | async-start | bytes 393216 | tf_op jit(solution)/shard_map/all_to_all | solution.py:67
Sparse Core Ops, SparseCore 0:
  15.2 70.7 all-gather.1
  145.9 87.0 all-reduce.3

commit v2 on v1

v2 whole, which is shorter than its diff:
```python
import jax
import jax.numpy as jnp
from jax import lax
from jax.experimental import pallas as pl
from jax.experimental.pallas import tpu as pltpu
from jax.sharding import Mesh, PartitionSpec as P

BLOCK = 128
QUERY_GROUP = 4


def normed(values, gain, heads):
    rows = values.shape[0]
    floats = values.astype(jnp.float32).reshape(rows, heads, gain.shape[0])
    power = jnp.mean(floats * floats, axis=-1, keepdims=True)
    return (floats * lax.rsqrt(power + 1e-06) * gain).astype(jnp.bfloat16)


def attend_kernel(qi_ref, qt_ref, ki_ref, kt_ref, vi_ref, vt_ref, fl_ref, ni_ref, nt_ref, di_ref, dt_ref):
    head_size = qi_ref.shape[1]
    scale = head_size ** (-0.5)
    q_blocks = qi_ref.shape[0] // BLOCK
    dims = (((1,), (1,)), ((), ()))
    keys_img = ki_ref[...]
    keys_txt = kt_ref[...]
    vals_img = vi_ref[...]
    vals_txt = vt_ref[...]

    def one(q, flags):
        s_img = lax.dot_general(q, keys_img, dims, preferred_element_type=jnp.float32) * scale
        s_txt = lax.dot_general(q, keys_txt, dims, preferred_element_type=jnp.float32) * scale
        e_img = jnp.exp(s_img)
        if flags is not None:
            e_img = jnp.where(flags > 0, e_img, jnp.float32(0.0))
        e_txt = jnp.exp(s_txt)
        den = jnp.sum(e_img, axis=1, keepdims=True) + jnp.sum(e_txt, axis=1, keepdims=True)
        num = jnp.dot(e_img.astype(jnp.bfloat16), vals_img, preferred_element_type=jnp.float32)
        num = num + jnp.dot(e_txt.astype(jnp.bfloat16), vals_txt, preferred_element_type=jnp.float32)
        return num, den

    for a in range(q_blocks):
        rows = slice(a * BLOCK, (a + 1) * BLOCK)
        num, den = one(qi_ref[rows, :], fl_ref[0, a:a + 1, :])
        ni_ref[rows, :] = num
        di_ref[rows, :] = jnp.broadcast_to(den, num.shape)
    num, den = one(qt_ref[...], None)
    nt_ref[...] = num
    dt_ref[...] = jnp.broadcast_to(den, num.shape)


def attend(qi, qt, ki, kt, vi, vt, fl, heads, head_size):
    def cols(rows):
        return pl.BlockSpec((rows, head_size), lambda h: (0, h))

    n_qi, n_qt, n_ki, n_kt = qi.shape[0], qt.shape[0], ki.shape[0], kt.shape[0]
    width = heads * head_size
    return pl.pallas_call(
        attend_kernel,
        grid=(heads,),
        in_specs=[
            cols(n_qi), cols(n_qt), cols(n_ki), cols(n_kt), cols(n_ki), cols(n_kt),
            pl.BlockSpec((1,) + fl.shape[1:], lambda h: (h, 0, 0)),
        ],
        out_specs=[cols(n_qi), cols(n_qt), cols(n_qi), cols(n_qt)],
        out_shape=[
            jax.ShapeDtypeStruct((n_qi, width), jnp.float32),
            jax.ShapeDtypeStruct((n_qt, width), jnp.float32),
            jax.ShapeDtypeStruct((n_qi, width), jnp.float32),
            jax.ShapeDtypeStruct((n_qt, width), jnp.float32),
        ],
        compiler_params=pltpu.CompilerParams(vmem_limit_bytes=48 * 1024 * 1024),
    )(qi, qt, ki, kt, vi, vt, fl)


def body(q_img, k_img, v_img, q_txt, k_txt, v_txt, norm_gains, block_map):
    rows, width = q_img.shape
    head_size = norm_gains.shape[1]
    heads = width // head_size
    text_rows = q_txt.shape[0]
    stride = rows + text_rows
    groups_q = lax.axis_size("qq")
    groups_k = lax.axis_size("kk")
    own_q = lax.axis_index("qq")

    queries = jnp.concatenate(
        [normed(q_img, norm_gains[0], heads), normed(q_txt, norm_gains[2], heads)], axis=0
    ).reshape(stride, width)
    keys = jnp.concatenate(
        [normed(k_img, norm_gains[1], heads), normed(k_txt, norm_gains[3], heads)], axis=0
    ).reshape(stride, width)
    values = jnp.concatenate([v_img, v_txt], axis=0)
    pair = jnp.stack([keys, values], axis=0)

    all_q = lax.all_gather(queries, "qq", axis=0, tiled=True)
    all_kv = lax.all_gather(pair, "kk", axis=1, tiled=True)
    flags = lax.all_gather(block_map, "qq", axis=1, tiled=True)
    flags = flags.reshape(heads, groups_q, groups_k, groups_q)
    flags = lax.dynamic_index_in_dim(flags, own_q, axis=3, keepdims=False)
    flags = jnp.repeat(flags, BLOCK, axis=2)

    all_q = all_q.reshape(groups_q, stride, width)
    qi = all_q[:, :rows].reshape(groups_q * rows, width)
    qt = all_q[:, rows:].reshape(groups_q * text_rows, width)
    all_kv = all_kv.reshape(2, groups_k, stride, width)
    ki = all_kv[0, :, :rows].reshape(groups_k * rows, width)
    kt = all_kv[0, :, rows:].reshape(groups_k * text_rows, width)
    vi = all_kv[1, :, :rows].reshape(groups_k * rows, width)
    vt = all_kv[1, :, rows:].reshape(groups_k * text_rows, width)

    ni, nt, di, dt = attend(qi, qt, ki, kt, vi, vt, flags, heads, head_size)
    numer = jnp.concatenate(
        [ni.reshape(groups_q, rows, width), nt.reshape(groups_q, text_rows, width)], axis=1
    )
    denom = jnp.concatenate(
        [di[:, ::head_size].reshape(groups_q, rows, heads),
         dt[:, ::head_size].reshape(groups_q, text_rows, heads)], axis=1
    )
    packed = jnp.concatenate([numer, denom], axis=2)
    packed = lax.all_to_all(packed, "qq", split_axis=0, concat_axis=0, tiled=True)
    packed = jnp.sum(packed, axis=0)
    numer = packed[:, :width].reshape(stride, heads, head_size)
    denom = packed[:, width:]
    result = numer / denom[..., None]
    merged = result.reshape(stride, width).astype(jnp.bfloat16)
    image_part = merged[:rows]
    text_out = merged[rows:]
    sections = lax.axis_size("section")
    image_out = lax.all_to_all(
        image_part.reshape(rows // sections, sections, width),
        "section",
        split_axis=1,
        concat_axis=2,
        tiled=True,
    )
    return (image_out, text_out)


def solution(mesh):
    sections, seq = mesh.devices.shape
    grid = Mesh(
        mesh.devices.reshape(sections, seq // QUERY_GROUP, QUERY_GROUP),
        ("section", "kk", "qq"),
    )
    rows = ("kk", "qq")
    placed = (
        P(rows, "section"),
        P(rows, "section"),
        P(rows, "section"),
        P(rows, "section"),
        P(rows, "section"),
        P(rows, "section"),
        P(),
        P("section", rows, None),
    )
    return jax.shard_map(
        body,
        mesh=grid,
        in_specs=placed,
        out_specs=(P(rows, "section", None), P(rows, "section")),
        check_vma=False,
    )
```

time: 253 us -> 197 us (0.78)
  local copies, waits for them, and re-layouts: 75.7 us -> 36.9 us
  waiting for transfers between devices: 75.2 us -> 39.1 us
  blocking collectives: 50.5 us -> 85.2 us
  matrix products: 27.2 us -> 0 us
  Pallas kernels: 0 us -> 12.6 us
    unnamed x3 -> x1, waiting for transfers between devices: 71.7 us -> 0.02 us
    all_to_all x0 -> x1, blocking collectives: none -> 51.9 us  [body(): lax.all_to_all(packed, 'qq', split_axis=0, concat_axis=0, tiled=True)]
    or x4 -> x0, local copies, waits for them, and re-layouts: 51.5 us -> none  [body(): keep = (flags[:, :, None, :, None] > 0) | text_pair[None, None]]
    all_gather x1, waiting for transfers between devices: 0.01 us -> 35.6 us  [body(): all_kv = lax.all_gather(pair, 'kk', axis=1, tiled=True)]
    dot_general x2 -> x0, matrix products: 27.2 us -> none  [the longest x1 15.3 us: body(): jnp.einsum('qhd,khd->hqk', all_q, all_k, preferred_element_type=jnp.float32)]
    unnamed x1 -> x0, blocking collectives: 14.3 us -> none
    pallas_call x0 -> x1, Pallas kernels: none -> 12.6 us  [attend(): pl.pallas_call(attend_kernel, grid=(heads,), in_specs=[cols(n_qi), cols(n...]
    unnamed x9 -> x22, local copies, waits for them, and re-layouts: 2.84 us -> 12.6 us
  transfers between devices with their start and end apart: 3 -> 2, of which waited for: 2 -> 2; matrix products, arithmetic and copies ran while one was open for 22% -> 1% of each run, Pallas kernels for 0% -> 0%
where the time goes in v2:
time: 197 us
  blocking collectives  85.2 us (43%)
  waiting for transfers between devices  39.1 us (20%)
  local copies, waits for them, and re-layouts  36.9 us (19%)
  between operations  14.4 us (7%)
  Pallas kernels  12.6 us (6%)
  starting transfers between devices  5.84 us (3%)
  other arithmetic  2.73 us (1%)
    all_to_all x1, blocking collectives, body(): lax.all_to_all(packed, 'qq', split_axis=0, concat_axis=0, tiled=True)  51.9 us
    all_gather x1, waiting for transfers between devices, body(): all_kv = lax.all_gather(pair, 'kk', axis=1, tiled=True)  35.6 us
    all_gather x1, blocking collectives, body(): all_q = lax.all_gather(queries, 'qq', axis=0, tiled=True)  22.1 us
    slice x1, local copies, waits for them, and re-layouts, body(): vi = all_kv[1, :, :rows].reshape(groups_k * rows, width)  13.8 us
    unnamed x22, local copies, waits for them, and re-layouts  12.6 us
    pallas_call x1, Pallas kernels, attend(): pl.pallas_call(attend_kernel, grid=(heads,), in_specs=[cols(n_qi), cols(n...  12.6 us
    all_gather x1, blocking collectives, body(): flags = lax.all_gather(block_map, 'qq', axis=1, tiled=True)  11.1 us
    all_to_all x1, starting transfers between devices, body(): lax.all_to_all(image_part.reshape(rows // sections, sections, width), 'se...  5.8 us
  transfers between devices with their start and end apart: 2, of which 2 were waited for; matrix products, arithmetic and copies ran while one was open for 1% of the time, Pallas kernels for 0%

profile of v2, /device:TPU:1, one launch (start us, length us, event | category | flops | bytes accessed | tf_op | source)
XLA Modules:
  0.0 196.7 jit_solution(13568408285397253579)
XLA Ops:
  7.2 0.8 slice_bitcast_fusion.1
  8.0 0.7 convert_multiply_fusion.5
  8.9 0.7 fusion.9
  9.8 1.1 copy.82
  10.9 1.1 copy.84
  12.0 0.9 copy.85
  13.4 1.2 copy.86
  15.7 22.1 %all-gather = bf16[4,132,768]{2,1,0:T(8,128)(2,1)S(1)} all-gather(bf16[1,132,768]{2,1,0:T(8,128)(2,1)S(1)} %copy.81), channel_id=1, replica_groups=mesh['section'=4,'kk'=16,'qq'=4] {'qq'}, dimensions={0}, use_global_device_ids=true | all-gather | bytes 1013760 | tf_op jit(solution)/shard_map/all_gather | solution.py:94
  37.9 11.1 %all_gather.11 = s32[6,4,64]{2,0,1:T(8,128)S(1)} all-gather(s32[6,1,64]{2,0,1:T(8,128)S(1)} %copy.88), channel_id=1, replica_groups=mesh['section'=4,'kk'=16,'qq'=4] {'qq'}, dimensions={1}, use_global_device_ids=true | all-gather | bytes 7680 | tf_op jit(solution)/shard_map/all_gather | solution.py:96
  49.2 0.6 dynamic-slice_reduce_fusion
  50.0 35.6 %all-gather.3.cloned.1.call-done = bf16[2,2112,768]{2,0,1:T(2,128)(2,1)} async-done(((bf16[2,132,768]{2,0,1:T(2,128)(2,1)}), bf16[2,2112,768]{2,0,1:T(2,128)(2,1)}) %all-gather.3.cloned.1.call-update) | async-done | bytes 6488080 | tf_op jit(solution)/shard_map/all_gather | solution.py:95
  85.6 2.0 slice_reduce_fusion
  87.5 13.8 %fusion.10 = (bf16[1,16,128,768]{3,0,2,1:T(2,128)(2,1)}, bf16[1,16,128,768]{3,0,2,1:T(2,128)(2,1)}) fusion(bf16[2,16,132,768]{3,0,2,1:T(2,128)(2,1)} %bitcast.54), kind=kLoop, calls=%fused_computation.40 | loop fusion | bytes 12582912 | tf_op jit(solution)/shard_map/slice | solution.py:107
  101.4 5.3 %copy.95 = bf16[1,16,128,768]{3,2,1,0:T(8,128)(2,1)} copy(bf16[1,16,128,768]{3,0,2,1:T(2,128)(2,1)} %get-tuple-element.12) | data formatting | bytes 6291456
  106.7 2.5 %copy.93 = bf16[1,16,128,768]{3,2,1,0:T(8,128)(2,1)} copy(bf16[1,16,128,768]{3,0,2,1:T(2,128)(2,1)S(1)} %copy-done.1) | data formatting | bytes 6291456
  109.2 12.6 %shard_map.95 = (f32[512,768]{1,0:T(8,128)S(1)}, f32[16,768]{1,0:T(8,128)S(1)}, f32[512,768]{1,0:T(8,128)S(1)}, f32[16,768]{1,0:T(8,128)S(1)}) custom-call(bf16[512,768]{1,0:T(8,128)(2,1)S(1)} %bitcast.51, bf16[16,768]{1,0:T(8,128)(2,1)S(1)} %reshape.117.qt_ref, bf16[2048,768]{1,0:T(8,128)(2,1)} %bitcast.56, bf16[64,768]{1,0:T(8,128)(2,1)S(1)} %reshape_squeeze.13.kt_ref, ...), custom_call_target="tpu_custom_call" | custom-call | tf_op jit(solution)/shard_map/pallas_call | solution.py:57
  121.8 1.1 copy-done
  123.0 2.6 %slice.58 = f32[512,6]{1,0:T(8,128)S(1)} slice(f32[512,768]{1,0:T(8,128)} %copy-done), slice={[0:512:1], [0:768:128]} | slice | bytes 24576 | tf_op jit(solution)/shard_map/slice | solution.py:115
  125.7 51.9 %all_to_all.17 = f32[4,132,774]{2,1,0:T(8,128)S(1)} all-to-all(f32[4,132,774]{2,1,0:T(8,128)S(1)} %maximum_maximum_fusion), channel_id=1, replica_groups=mesh['section'=4,'kk'=16,'qq'=4] {'qq'}, dimensions={0} | all-to-all | bytes 3269376 | tf_op jit(solution)/shard_map/all_to_all | solution.py:119
  178.3 0.7 copy.90
  179.0 5.8 %all-to-all-start.1 = ((bf16[32,4,768]{2,0,1:T(8,128)(2,1)}), bf16[32,4,768]{2,0,1:T(8,128)(2,1)S(1)}, u32[]{:S(2)}, u32[]{:S(2)}) async-start(bf16[32,4,768]{2,0,1:T(8,128)(2,1)} %copy.90), calls=%async_computation.1 | async-start | bytes 393216 | tf_op jit(solution)/shard_map/all_to_all | solution.py:128
  184.8 0.6 slice.73
  185.4 3.5 %all-to-all-done.1 = bf16[32,4,768]{2,0,1:T(8,128)(2,1)S(1)} async-done(((bf16[32,4,768]{2,0,1:T(8,128)(2,1)}), bf16[32,4,768]{2,0,1:T(8,128)(2,1)S(1)}, u32[]{:S(2)}, u32[]{:S(2)}) %all-to-all-start.1) | async-done | bytes 196640 | tf_op jit(solution)/shard_map/all_to_all | solution.py:128
  189.1 0.8 all_to_all.14
  (60 shorter events, 3.3 us)
Async XLA Ops:
  7.2 78.4 %all-gather.3.cloned.1.call-start = ((), (), s32[]{:S(2)}) async-start(), calls=%async_computation.2 | async-start | bytes 6893568 | tf_op jit(solution)/shard_map/all_gather | solution.py:95
  13.1 1.5 copy-start.3
  13.1 1.9 copy-start.2
  15.5 22.4 %copy-start.4 = (s32[6,1,64]{2,1,0:T(1,128)S(1)}, s32[6,1,64]{2,1,0:T(1,128)}, u32[]{:S(2)}) copy-start(s32[6,1,64]{2,1,0:T(1,128)} %param.15) | copy-start | bytes 4612
  101.4 5.4 %copy-start.1 = (bf16[1,16,128,768]{3,0,2,1:T(2,128)(2,1)S(1)}, bf16[1,16,128,768]{3,0,2,1:T(2,128)(2,1)}, u32[]{:S(2)}) copy-start(bf16[1,16,128,768]{3,0,2,1:T(2,128)(2,1)} %get-tuple-element.13) | copy-start | bytes 9437188
  121.7 1.2 copy-start
  179.0 9.9 %all-to-all-start.1 = ((bf16[32,4,768]{2,0,1:T(8,128)(2,1)}), bf16[32,4,768]{2,0,1:T(8,128)(2,1)S(1)}, u32[]{:S(2)}, u32[]{:S(2)}) async-start(bf16[32,4,768]{2,0,1:T(8,128)(2,1)} %copy.90), calls=%async_computation.1 | async-start | bytes 393216 | tf_op jit(solution)/shard_map/all_to_all | solution.py:128
Sparse Core Ops, SparseCore 0:
  14.7 70.8 all-gather.2

commit v3 on v2

--- a/solution.py
+++ b/solution.py
@@ -17,13 +17,13 @@
 
 
 def attend_kernel(qi_ref, qt_ref, ki_ref, kt_ref, vi_ref, vt_ref, fl_ref, ni_ref, nt_ref, di_ref, dt_ref):
-    head_size = qi_ref.shape[1]
+    head_size = qi_ref.shape[-1]
     scale = head_size ** (-0.5)
-    q_blocks = qi_ref.shape[0] // BLOCK
+    q_blocks = qi_ref.shape[0]
     dims = (((1,), (1,)), ((), ()))
-    keys_img = ki_ref[...]
+    keys_img = ki_ref[0].reshape(-1, head_size)
     keys_txt = kt_ref[...]
-    vals_img = vi_ref[...]
+    vals_img = vi_ref[0].reshape(-1, head_size)
     vals_txt = vt_ref[...]
 
     def one(q, flags):
@@ -40,7 +40,7 @@
 
     for a in range(q_blocks):
         rows = slice(a * BLOCK, (a + 1) * BLOCK)
-        num, den = one(qi_ref[rows, :], fl_ref[0, a:a + 1, :])
+        num, den = one(qi_ref[a], fl_ref[0, a:a + 1, :])
         ni_ref[rows, :] = num
         di_ref[rows, :] = jnp.broadcast_to(den, num.shape)
     num, den = one(qt_ref[...], None)
@@ -48,17 +48,27 @@
     dt_ref[...] = jnp.broadcast_to(den, num.shape)
 
 
-def attend(qi, qt, ki, kt, vi, vt, fl, heads, head_size):
+def attend(qi, qt, kv, kt, vt, fl, heads, head_size):
+    groups_q = qi.shape[0]
+    groups_k = kv.shape[1]
+    n_qi = groups_q * BLOCK
+    n_ki = groups_k * BLOCK
+    n_qt, n_kt = qt.shape[0], kt.shape[0]
+    width = heads * head_size
+
     def cols(rows):
         return pl.BlockSpec((rows, head_size), lambda h: (0, h))
 
-    n_qi, n_qt, n_ki, n_kt = qi.shape[0], qt.shape[0], ki.shape[0], kt.shape[0]
-    width = heads * head_size
     return pl.pallas_call(
         attend_kernel,
         grid=(heads,),
         in_specs=[
-            cols(n_qi), cols(n_qt), cols(n_ki), cols(n_kt), cols(n_ki), cols(n_kt),
+            pl.BlockSpec((groups_q, BLOCK, head_size), lambda h: (0, 0, h)),
+            cols(n_qt),
+            pl.BlockSpec((1, groups_k, BLOCK, head_size), lambda h: (0, 0, 0, h)),
+            cols(n_kt),
+            pl.BlockSpec((1, groups_k, BLOCK, head_size), lambda h: (1, 0, 0, h)),
+            cols(n_kt),
             pl.BlockSpec((1,) + fl.shape[1:], lambda h: (h, 0, 0)),
         ],
         out_specs=[cols(n_qi), cols(n_qt), cols(n_qi), cols(n_qt)],
@@ -69,7 +79,7 @@
             jax.ShapeDtypeStruct((n_qt, width), jnp.float32),
         ],
         compiler_params=pltpu.CompilerParams(vmem_limit_bytes=48 * 1024 * 1024),
-    )(qi, qt, ki, kt, vi, vt, fl)
+    )(qi, qt, kv, kt, kv, vt, fl)
 
 
 def body(q_img, k_img, v_img, q_txt, k_txt, v_txt, norm_gains, block_map):
@@ -84,11 +94,11 @@
 
     queries = jnp.concatenate(
         [normed(q_img, norm_gains[0], heads), normed(q_txt, norm_gains[2], heads)], axis=0
-    ).reshape(stride, width)
+    ).reshape(1, stride, width)
     keys = jnp.concatenate(
         [normed(k_img, norm_gains[1], heads), normed(k_txt, norm_gains[3], heads)], axis=0
-    ).reshape(stride, width)
-    values = jnp.concatenate([v_img, v_txt], axis=0)
+    ).reshape(1, stride, width)
+    values = jnp.concatenate([v_img, v_txt], axis=0).reshape(1, stride, width)
     pair = jnp.stack([keys, values], axis=0)
 
     all_q = lax.all_gather(queries, "qq", axis=0, tiled=True)
@@ -98,16 +108,11 @@
     flags = lax.dynamic_index_in_dim(flags, own_q, axis=3, keepdims=False)
     flags = jnp.repeat(flags, BLOCK, axis=2)
 
-    all_q = all_q.reshape(groups_q, stride, width)
-    qi = all_q[:, :rows].reshape(groups_q * rows, width)
     qt = all_q[:, rows:].reshape(groups_q * text_rows, width)
-    all_kv = all_kv.reshape(2, groups_k, stride, width)
-    ki = all_kv[0, :, :rows].reshape(groups_k * rows, width)
     kt = all_kv[0, :, rows:].reshape(groups_k * text_rows, width)
-    vi = all_kv[1, :, :rows].reshape(groups_k * rows, width)
     vt = all_kv[1, :, rows:].reshape(groups_k * text_rows, width)
 
-    ni, nt, di, dt = attend(qi, qt, ki, kt, vi, vt, flags, heads, head_size)
+    ni, nt, di, dt = attend(all_q, qt, all_kv, kt, vt, flags, heads, head_size)
     numer = jnp.concatenate(
         [ni.reshape(groups_q, rows, width), nt.reshape(groups_q, text_rows, width)], axis=1
     )
@@ -115,11 +120,13 @@
         [di[:, ::head_size].reshape(groups_q, rows, heads),
          dt[:, ::head_size].reshape(groups_q, text_rows, heads)], axis=1
     )
-    packed = jnp.concatenate([numer, denom], axis=2)
+    denom_hi = denom.astype(jnp.bfloat16)
+    denom_lo = (denom - denom_hi.astype(jnp.float32)).astype(jnp.bfloat16)
+    packed = jnp.concatenate([numer.astype(jnp.bfloat16), denom_hi, denom_lo], axis=2)
     packed = lax.all_to_all(packed, "qq", split_axis=0, concat_axis=0, tiled=True)
-    packed = jnp.sum(packed, axis=0)
+    packed = jnp.sum(packed.astype(jnp.float32), axis=0)
     numer = packed[:, :width].reshape(stride, heads, head_size)
-    denom = packed[:, width:]
+    denom = packed[:, width:width + heads] + packed[:, width + heads:]
     result = numer / denom[..., None]
     merged = result.reshape(stride, width).astype(jnp.bfloat16)
     image_part = merged[:rows]

time: 197 us -> 152 us (0.77)
  local copies, waits for them, and re-layouts: 36.9 us -> 11 us
  blocking collectives: 85.2 us -> 63.5 us
  waiting for transfers between devices: 39.1 us -> 41.2 us
    all_to_all x1, blocking collectives: 51.9 us -> 31.5 us  [body(): lax.all_to_all(packed, 'qq', split_axis=0, concat_axis=0, tiled=True)]
    slice x3 -> x0, local copies, waits for them, and re-layouts: 13.8 us -> none  [the longest x1 13.8 us: body(): vi = all_kv[1, :, :rows].reshape(groups_k * rows, width)]
    unnamed x22, local copies, waits for them, and re-layouts: 12.6 us -> 1.62 us
    all_gather x1, blocking collectives: 22.1 us -> 16.7 us  [body(): all_q = lax.all_gather(queries, 'qq', axis=0, tiled=True)]
    all_gather x1, blocking collectives: 11.1 us -> 15.4 us  [body(): flags = lax.all_gather(block_map, 'qq', axis=1, tiled=True)]
    all_gather x1, waiting for transfers between devices: 35.6 us -> 37.7 us  [body(): all_kv = lax.all_gather(pair, 'kk', axis=1, tiled=True)]
  transfers between devices with their start and end apart: 2 -> 2, of which waited for: 2 -> 2; matrix products, arithmetic and copies ran while one was open for 1% -> 2% of each run, Pallas kernels for 0% -> 0%
where the time goes in v3:
time: 152 us
  blocking collectives  63.5 us (42%)
  waiting for transfers between devices  41.2 us (27%)
  between operations  14.5 us (10%)
  Pallas kernels  12.7 us (8%)
  local copies, waits for them, and re-layouts  11 us (7%)
  starting transfers between devices  5.59 us (4%)
  other arithmetic  3.65 us (2%)
    all_gather x1, waiting for transfers between devices, body(): all_kv = lax.all_gather(pair, 'kk', axis=1, tiled=True)  37.7 us
    all_to_all x1, blocking collectives, body(): lax.all_to_all(packed, 'qq', split_axis=0, concat_axis=0, tiled=True)  31.5 us
    all_gather x1, blocking collectives, body(): all_q = lax.all_gather(queries, 'qq', axis=0, tiled=True)  16.7 us
    all_gather x1, blocking collectives, body(): flags = lax.all_gather(block_map, 'qq', axis=1, tiled=True)  15.4 us
    pallas_call x1, Pallas kernels, attend(): pl.pallas_call(attend_kernel, grid=(heads,), in_specs=[pl.BlockSpec((grou...  12.7 us
    all_to_all x1, starting transfers between devices, body(): lax.all_to_all(image_part.reshape(rows // sections, sections, width), 'se...  5.55 us
    all_to_all x1, waiting for transfers between devices, body(): lax.all_to_all(image_part.reshape(rows // sections, sections, width), 'se...  3.5 us
  transfers between devices with their start and end apart: 2, of which 2 were waited for; matrix products, arithmetic and copies ran while one was open for 2% of the time, Pallas kernels for 0%

profile of v3, /device:TPU:1, one launch (start us, length us, event | category | flops | bytes accessed | tf_op | source)
XLA Modules:
  0.0 152.1 jit_solution(10905724519995546228)
XLA Ops:
  7.3 0.8 slice_bitcast_fusion.1
  8.1 0.7 convert_multiply_fusion.5
  9.0 1.0 convert_multiply_fusion.1
  10.2 0.2 copy.47
  10.5 0.8 pad_maximum_fusion.1
  11.4 15.4 %all_gather.11 = s32[6,4,64]{2,0,1:T(8,128)S(1)} all-gather(s32[6,1,64]{2,0,1:T(8,128)S(1)} %copy.48), channel_id=1, replica_groups=mesh['section'=4,'kk'=16,'qq'=4] {'qq'}, dimensions={1}, use_global_device_ids=true | all-gather | bytes 7680 | tf_op jit(solution)/shard_map/all_gather | solution.py:106
  27.0 0.6 dynamic-slice_reduce_fusion
  27.9 0.2 copy.44
  28.4 0.2 fusion.2
  28.8 16.7 %all_gather.9.qi_ref = bf16[4,132,768]{2,1,0:T(8,128)(2,1)S(1)} all-gather(bf16[1,132,768]{2,1,0:T(8,128)(2,1)S(1)} %copy.45), channel_id=1, replica_groups=mesh['section'=4,'kk'=16,'qq'=4] {'qq'}, dimensions={0}, use_global_device_ids=true | all-gather | bytes 1013760 | tf_op jit(solution)/shard_map/all_gather | solution.py:104
  45.5 37.7 %all-gather.2.cloned.1.call-done.ki_ref.vi_ref = bf16[2,16,132,768]{3,2,1,0:T(8,128)(2,1)} async-done(((bf16[2,1,132,768]{3,2,1,0:T(8,128)(2,1)}), bf16[2,16,132,768]{3,2,1,0:T(8,128)(2,1)}) %all-gather.2.cloned.1.call-update) | async-done | bytes 6488080 | tf_op jit(solution)/shard_map/all_gather | solution.py:105
  83.2 1.1 fusion.13
  84.4 12.7 %shard_map.95 = (f32[512,768]{1,0:T(8,128)S(1)}, f32[16,768]{1,0:T(8,128)S(1)}, f32[512,768]{1,0:T(8,128)S(1)}, f32[16,768]{1,0:T(8,128)S(1)}) custom-call(bf16[4,132,768]{2,1,0:T(8,128)(2,1)S(1)} %all_gather.9.qi_ref, bf16[16,768]{1,0:T(8,128)(2,1)S(1)} %reshape.122.qt_ref, bf16[2,16,132,768]{3,2,1,0:T(8,128)(2,1)} %all-gather.2.cloned.1.call-done.ki_ref.vi_ref, ...), custom_call_target="tpu_custom_call" | custom-call | tf_op jit(solution)/shard_map/pallas_call | solution.py:62
  97.1 1.1 copy-done
  98.4 2.6 %slice.49 = f32[512,6]{1,0:T(8,128)S(1)} slice(f32[512,768]{1,0:T(8,128)} %copy-done), slice={[0:512:1], [0:768:128]} | slice | bytes 24576 | tf_op jit(solution)/shard_map/slice | solution.py:120
  101.2 0.2 copy.52
  101.4 0.2 copy.53
  101.7 31.5 %all_to_all.17 = bf16[4,132,780]{2,1,0:T(8,128)(2,1)S(1)} all-to-all(bf16[4,132,780]{2,1,0:T(8,128)(2,1)S(1)} %pad_maximum_fusion), channel_id=1, replica_groups=mesh['section'=4,'kk'=16,'qq'=4] {'qq'}, dimensions={0} | all-to-all | bytes 1647360 | tf_op jit(solution)/shard_map/all_to_all | solution.py:126
  133.4 0.2 div.27
  133.9 0.7 copy.54
  134.6 5.5 %all-to-all-start.1 = ((bf16[32,4,768]{2,0,1:T(8,128)(2,1)}), bf16[32,4,768]{2,0,1:T(8,128)(2,1)S(1)}, u32[]{:S(2)}, u32[]{:S(2)}) async-start(bf16[32,4,768]{2,0,1:T(8,128)(2,1)} %copy.54), calls=%async_computation.1 | async-start | bytes 393216 | tf_op jit(solution)/shard_map/all_to_all | solution.py:135
  140.2 0.6 slice.63
  140.8 3.5 %all-to-all-done.1 = bf16[32,4,768]{2,0,1:T(8,128)(2,1)S(1)} async-done(((bf16[32,4,768]{2,0,1:T(8,128)(2,1)}), bf16[32,4,768]{2,0,1:T(8,128)(2,1)S(1)}, u32[]{:S(2)}, u32[]{:S(2)}) %all-to-all-start.1) | async-done | bytes 196640 | tf_op jit(solution)/shard_map/all_to_all | solution.py:135
  144.4 0.8 all_to_all.14
  (68 shorter events, 2.8 us)
Async XLA Ops:
  7.2 3.2 %copy-start.4 = (bf16[4,768]{1,0:T(4,128)(2,1)S(1)}, bf16[4,768]{1,0:T(4,128)(2,1)}, u32[]{:S(2)}) copy-start(bf16[4,768]{1,0:T(4,128)(2,1)} %param.12) | copy-start | bytes 18436
  7.2 3.3 %copy-start.1 = (bf16[128,768]{1,0:T(8,128)(2,1)S(1)}, bf16[128,768]{1,0:T(8,128)(2,1)}, u32[]{:S(2)}) copy-start(bf16[128,768]{1,0:T(8,128)(2,1)} %param.9) | copy-start | bytes 589828
  7.2 3.2 %copy-start.6 = (bf16[4,768]{1,0:T(4,128)(2,1)S(1)}, bf16[4,768]{1,0:T(4,128)(2,1)}, u32[]{:S(2)}) copy-start(bf16[4,768]{1,0:T(4,128)(2,1)} %param.13) | copy-start | bytes 18436
  7.2 3.2 %copy-start.2 = (bf16[128,768]{1,0:T(8,128)(2,1)S(1)}, bf16[128,768]{1,0:T(8,128)(2,1)}, u32[]{:S(2)}) copy-start(bf16[128,768]{1,0:T(8,128)(2,1)} %param.10) | copy-start | bytes 589828
  7.2 76.0 %all-gather.2.cloned.1.call-start = ((), (), s32[]{:S(2)}) async-start(), calls=%async_computation.2 | async-start | bytes 7102464 | tf_op jit(solution)/shard_map/all_gather | solution.py:105
  10.1 1.2 copy-start.7
  10.2 16.6 %copy-start.5 = (bf16[4,768]{1,0:T(4,128)(2,1)S(1)}, bf16[4,768]{1,0:T(4,128)(2,1)}, u32[]{:S(2)}) copy-start(bf16[4,768]{1,0:T(4,128)(2,1)} %param.11) | copy-start | bytes 18436
  10.4 17.7 %copy-start.3 = (bf16[128,768]{1,0:T(8,128)(2,1)S(1)}, bf16[128,768]{1,0:T(8,128)(2,1)}, u32[]{:S(2)}) copy-start(bf16[128,768]{1,0:T(8,128)(2,1)} %param.8) | copy-start | bytes 589828
  97.0 1.2 copy-start
  134.6 9.6 %all-to-all-start.1 = ((bf16[32,4,768]{2,0,1:T(8,128)(2,1)}), bf16[32,4,768]{2,0,1:T(8,128)(2,1)S(1)}, u32[]{:S(2)}, u32[]{:S(2)}) async-start(bf16[32,4,768]{2,0,1:T(8,128)(2,1)} %copy.54), calls=%async_computation.1 | async-start | bytes 393216 | tf_op jit(solution)/shard_map/all_to_all | solution.py:135
Sparse Core Ops, SparseCore 0:
  11.5 71.7 all-gather.1

commit v4 on v3

--- a/solution.py
+++ b/solution.py
@@ -7,6 +7,7 @@
 
 BLOCK = 128
 QUERY_GROUP = 4
+CHUNKS = 3
 
 
 def normed(values, gain, heads):
@@ -48,28 +49,27 @@
     dt_ref[...] = jnp.broadcast_to(den, num.shape)
 
 
-def attend(qi, qt, kv, kt, vt, fl, heads, head_size):
+def attend(qi, qt, kv, kt, vt, fl, first, heads, head_size):
     groups_q = qi.shape[0]
     groups_k = kv.shape[1]
     n_qi = groups_q * BLOCK
-    n_ki = groups_k * BLOCK
     n_qt, n_kt = qt.shape[0], kt.shape[0]
     width = heads * head_size
 
-    def cols(rows):
-        return pl.BlockSpec((rows, head_size), lambda h: (0, h))
+    def cols(rows, offset=0):
+        return pl.BlockSpec((rows, head_size), lambda h: (0, h + offset))
 
     return pl.pallas_call(
         attend_kernel,
         grid=(heads,),
         in_specs=[
-            pl.BlockSpec((groups_q, BLOCK, head_size), lambda h: (0, 0, h)),
-            cols(n_qt),
+            pl.BlockSpec((groups_q, BLOCK, head_size), lambda h: (0, 0, h + first)),
+            cols(n_qt, first),
             pl.BlockSpec((1, groups_k, BLOCK, head_size), lambda h: (0, 0, 0, h)),
             cols(n_kt),
             pl.BlockSpec((1, groups_k, BLOCK, head_size), lambda h: (1, 0, 0, h)),
             cols(n_kt),
-            pl.BlockSpec((1,) + fl.shape[1:], lambda h: (h, 0, 0)),
+            pl.BlockSpec((1,) + fl.shape[1:], lambda h: (h + first, 0, 0)),
         ],
         out_specs=[cols(n_qi), cols(n_qt), cols(n_qi), cols(n_qt)],
         out_shape=[
@@ -91,10 +91,16 @@
     groups_q = lax.axis_size("qq")
     groups_k = lax.axis_size("kk")
     own_q = lax.axis_index("qq")
+    sections = lax.axis_size("section")
+    chunk = heads // CHUNKS
 
+    map_row = block_map.reshape(1, -1).astype(jnp.bfloat16)
+    map_row = jnp.pad(map_row, ((0, 0), (0, width - map_row.shape[1])))
     queries = jnp.concatenate(
-        [normed(q_img, norm_gains[0], heads), normed(q_txt, norm_gains[2], heads)], axis=0
-    ).reshape(1, stride, width)
+        [normed(q_img, norm_gains[0], heads).reshape(rows, width),
+         normed(q_txt, norm_gains[2], heads).reshape(text_rows, width),
+         map_row], axis=0
+    ).reshape(1, stride + 1, width)
     keys = jnp.concatenate(
         [normed(k_img, norm_gains[1], heads), normed(k_txt, norm_gains[3], heads)], axis=0
     ).reshape(1, stride, width)
@@ -102,43 +108,47 @@
     pair = jnp.stack([keys, values], axis=0)
 
     all_q = lax.all_gather(queries, "qq", axis=0, tiled=True)
-    all_kv = lax.all_gather(pair, "kk", axis=1, tiled=True)
-    flags = lax.all_gather(block_map, "qq", axis=1, tiled=True)
-    flags = flags.reshape(heads, groups_q, groups_k, groups_q)
+    flags = all_q[:, stride, :block_map.size].reshape(groups_q, heads, groups_k, groups_q)
     flags = lax.dynamic_index_in_dim(flags, own_q, axis=3, keepdims=False)
-    flags = jnp.repeat(flags, BLOCK, axis=2)
+    flags = jnp.repeat(flags.transpose(1, 0, 2), BLOCK, axis=2)
+    qt = all_q[:, rows:stride].reshape(groups_q * text_rows, width)
 
-    qt = all_q[:, rows:].reshape(groups_q * text_rows, width)
-    kt = all_kv[0, :, rows:].reshape(groups_k * text_rows, width)
-    vt = all_kv[1, :, rows:].reshape(groups_k * text_rows, width)
-
-    ni, nt, di, dt = attend(all_q, qt, all_kv, kt, vt, flags, heads, head_size)
-    numer = jnp.concatenate(
-        [ni.reshape(groups_q, rows, width), nt.reshape(groups_q, text_rows, width)], axis=1
-    )
-    denom = jnp.concatenate(
-        [di[:, ::head_size].reshape(groups_q, rows, heads),
-         dt[:, ::head_size].reshape(groups_q, text_rows, heads)], axis=1
-    )
-    denom_hi = denom.astype(jnp.bfloat16)
-    denom_lo = (denom - denom_hi.astype(jnp.float32)).astype(jnp.bfloat16)
-    packed = jnp.concatenate([numer.astype(jnp.bfloat16), denom_hi, denom_lo], axis=2)
-    packed = lax.all_to_all(packed, "qq", split_axis=0, concat_axis=0, tiled=True)
-    packed = jnp.sum(packed.astype(jnp.float32), axis=0)
-    numer = packed[:, :width].reshape(stride, heads, head_size)
-    denom = packed[:, width:width + heads] + packed[:, width + heads:]
-    result = numer / denom[..., None]
-    merged = result.reshape(stride, width).astype(jnp.bfloat16)
-    image_part = merged[:rows]
-    text_out = merged[rows:]
-    sections = lax.axis_size("section")
-    image_out = lax.all_to_all(
-        image_part.reshape(rows // sections, sections, width),
-        "section",
-        split_axis=1,
-        concat_axis=2,
-        tiled=True,
-    )
+    image_parts = []
+    text_parts = []
+    for c in range(CHUNKS):
+        span = slice(c * chunk * head_size, (c + 1) * chunk * head_size)
+        all_kv = lax.all_gather(pair[..., span], "kk", axis=1, tiled=True)
+        kt = all_kv[0, :, rows:].reshape(groups_k * text_rows, chunk * head_size)
+        vt = all_kv[1, :, rows:].reshape(groups_k * text_rows, chunk * head_size)
+        ni, nt, di, dt = attend(all_q, qt, all_kv, kt, vt, flags, c * chunk, chunk, head_size)
+        numer = jnp.concatenate(
+            [ni.reshape(groups_q, rows, -1), nt.reshape(groups_q, text_rows, -1)], axis=1
+        )
+        denom = jnp.concatenate(
+            [di[:, ::head_size].reshape(groups_q, rows, chunk),
+             dt[:, ::head_size].reshape(groups_q, text_rows, chunk)], axis=1
+        )
+        denom_hi = denom.astype(jnp.bfloat16)
+        denom_lo = (denom - denom_hi.astype(jnp.float32)).astype(jnp.bfloat16)
+        packed = jnp.concatenate([numer.astype(jnp.bfloat16), denom_hi, denom_lo], axis=2)
+        packed = lax.all_to_all(packed, "qq", split_axis=0, concat_axis=0, tiled=True)
+        packed = jnp.sum(packed.astype(jnp.float32), axis=0)
+        part_width = chunk * head_size
+        numer = packed[:, :part_width].reshape(stride, chunk, head_size)
+        denom = packed[:, part_width:part_width + chunk] + packed[:, part_width + chunk:]
+        result = numer / denom[..., None]
+        merged = result.reshape(stride, part_width).astype(jnp.bfloat16)
+        text_parts.append(merged[rows:])
+        image_part = lax.all_to_all(
+            merged[:rows].reshape(rows // sections, sections, part_width),
+            "section",
+            split_axis=1,
+            concat_axis=2,
+            tiled=True,
+        )
+        image_parts.append(image_part.reshape(rows // sections, 1, sections, part_width))
+    image_out = jnp.stack(image_parts, axis=3).reshape(rows // sections, 1, sections * width)
+    text_out = jnp.concatenate(text_parts, axis=1)
     return (image_out, text_out)
 
 

time: 152 us -> 244 us (1.61)
  waiting for transfers between devices: 41.2 us -> 134 us
  blocking collectives: 63.5 us -> 22.1 us
  starting transfers between devices: 5.59 us -> 33.3 us
  local copies, waits for them, and re-layouts: 11 us -> 20.9 us
    all_gather x1 -> x3, waiting for transfers between devices: 37.7 us -> 106 us  [body(): all_kv = lax.all_gather(pair[..., span], 'kk', axis=1, tiled=True)]
    all_to_all x1 -> x0, blocking collectives: 31.5 us -> none  [body(): lax.all_to_all(packed, 'qq', split_axis=0, concat_axis=0, tiled=True)]
    all_to_all x1 -> x6, starting transfers between devices: 5.55 us -> 33.2 us  [the longest x3 18.1 us: body(): lax.all_to_all(packed, 'qq', split_axis=0, concat_axis=0, tiled=True)]
    all_to_all x1 -> x6, waiting for transfers between devices: 3.5 us -> 26.4 us  [the longest x3 19.1 us: body(): lax.all_to_all(packed, 'qq', split_axis=0, concat_axis=0, tiled=True)]
    all_gather x1 -> x0, blocking collectives: 15.4 us -> none  [body(): flags = lax.all_gather(block_map, 'qq', axis=1, tiled=True)]
    all_gather x1, blocking collectives: 16.7 us -> 22.1 us  [body(): all_q = lax.all_gather(queries, 'qq', axis=0, tiled=True)]
    unnamed x22 -> x30, local copies, waits for them, and re-layouts: 1.62 us -> 5.53 us
    slice x6 -> x18, local copies, waits for them, and re-layouts: 4.33 us -> 7.54 us  [the longest x3 3.81 us: body(): di[:, ::head_size].reshape(groups_q, rows, chunk)]
  transfers between devices with their start and end apart: 2 -> 9, of which waited for: 2 -> 8; matrix products, arithmetic and copies ran while one was open for 2% -> 7% of each run, Pallas kernels for 0% -> 5%
where the time goes in v4:
time: 244 us; the launch traced here: 243 us
  waiting for transfers between devices  134 us (55%)
  starting transfers between devices  33.3 us (14%)
  blocking collectives  22.1 us (9%)
  local copies, waits for them, and re-layouts  20.9 us (9%)
  between operations  14.4 us (6%)
  Pallas kernels  12.6 us (5%)
  other arithmetic  5.62 us (2%)
    all_gather x3, waiting for transfers between devices, body(): all_kv = lax.all_gather(pair[..., span], 'kk', axis=1, tiled=True)  106 us
    all_gather x1, blocking collectives, body(): all_q = lax.all_gather(queries, 'qq', axis=0, tiled=True)  22.1 us
    all_to_all x3, waiting for transfers between devices, body(): lax.all_to_all(packed, 'qq', split_axis=0, concat_axis=0, tiled=True)  19.1 us
    all_to_all x3, starting transfers between devices, body(): lax.all_to_all(packed, 'qq', split_axis=0, concat_axis=0, tiled=True)  18.1 us
    all_to_all x3, starting transfers between devices, body(): lax.all_to_all(merged[:rows].reshape(rows // sections, sections, part_wid...  15.1 us
    pallas_call x3, Pallas kernels, attend(): pl.pallas_call(attend_kernel, grid=(heads,), in_specs=[pl.BlockSpec((grou...  12.6 us
    all_to_all x3, waiting for transfers between devices, body(): lax.all_to_all(merged[:rows].reshape(rows // sections, sections, part_wid...  7.34 us
    unnamed x30, local copies, waits for them, and re-layouts  5.53 us
  transfers between devices with their start and end apart: 9, of which 8 were waited for; matrix products, arithmetic and copies ran while one was open for 7% of the time, Pallas kernels for 5%

profile of v4, /device:TPU:1, one launch (start us, length us, event | category | flops | bytes accessed | tf_op | source)
XLA Modules:
  0.0 243.2 jit_solution(4015571120171503146)
XLA Ops:
  13.5 22.1 %all-gather.1.qi_ref = bf16[4,133,768]{2,1,0:T(8,128)(2,1)S(1)} all-gather(bf16[1,133,768]{2,1,0:T(8,128)(2,1)S(1)} %copy.107), channel_id=2, replica_groups=mesh['section'=4,'kk'=16,'qq'=4] {'qq'}, dimensions={0}, use_global_device_ids=true | all-gather | bytes 1021440 | tf_op jit(solution)/shard_map/all_gather | solution.py:110
  36.4 27.0 %all-gather.6.cloned.1.call-done.ki_ref.vi_ref = bf16[2,16,132,256]{3,2,1,0:T(8,128)(2,1)} async-done(((bf16[2,1,132,256]{3,2,1,0:T(8,128)(2,1)}), bf16[2,16,132,256]{3,2,1,0:T(8,128)(2,1)}) %all-gather.6.cloned.1.call-update) | async-done | bytes 2162704 | tf_op jit(solution)/shard_map/all_gather | solution.py:120
  64.4 1.6 copy-done.2
  66.0 4.2 %shard_map.95 = (f32[512,256]{1,0:T(8,128)S(1)}, f32[16,256]{1,0:T(8,128)S(1)}, f32[512,256]{1,0:T(8,128)S(1)}, f32[16,256]{1,0:T(8,128)S(1)}) custom-call(bf16[4,133,768]{2,1,0:T(8,128)(2,1)S(1)} %all-gather.1.qi_ref, bf16[16,768]{1,0:T(8,128)(2,1)S(1)} %reshape.176.qt_ref, bf16[2,16,132,256]{3,2,1,0:T(8,128)(2,1)S(1)} %copy-done.2, ...), custom_call_target="tpu_custom_call" | custom-call | tf_op jit(solution)/shard_map/pallas_call | solution.py:62
  70.2 1.3 slice.117
  73.2 6.7 %all-to-all-start = ((bf16[4,132,260]{2,1,0:T(8,128)(2,1)}), bf16[4,132,260]{2,1,0:T(8,128)(2,1)S(1)}, u32[]{:S(2)}, u32[]{:S(2)}) async-start(bf16[4,132,260]{2,1,0:T(8,128)(2,1)} %pad_maximum_fusion.1), calls=%async_computation | async-start | bytes 835584 | tf_op jit(solution)/shard_map/all_to_all | solution.py:134
  79.9 35.8 %all-gather.8.cloned.1.call-done.ki_ref.vi_ref = bf16[2,16,132,256]{3,2,1,0:T(8,128)(2,1)} async-done(((bf16[2,1,132,256]{3,2,1,0:T(8,128)(2,1)}), bf16[2,16,132,256]{3,2,1,0:T(8,128)(2,1)}) %all-gather.8.cloned.1.call-update) | async-done | bytes 2162704 | tf_op jit(solution)/shard_map/all_gather | solution.py:120
  116.6 1.6 copy-done.1
  118.2 4.2 %shard_map.96 = (f32[512,256]{1,0:T(8,128)S(1)}, f32[16,256]{1,0:T(8,128)S(1)}, f32[512,256]{1,0:T(8,128)S(1)}, f32[16,256]{1,0:T(8,128)S(1)}) custom-call(bf16[4,133,768]{2,1,0:T(8,128)(2,1)S(1)} %all-gather.1.qi_ref, bf16[16,768]{1,0:T(8,128)(2,1)S(1)} %reshape.176.qt_ref, bf16[2,16,132,256]{3,2,1,0:T(8,128)(2,1)S(1)} %copy-done.1, ...), custom_call_target="tpu_custom_call" | custom-call | tf_op jit(solution)/shard_map/pallas_call | solution.py:62
  122.4 1.3 slice.126
  124.2 43.6 %all-gather.10.cloned.1.call-done.ki_ref.vi_ref = bf16[2,16,132,256]{3,2,1,0:T(8,128)(2,1)} async-done(((bf16[2,1,132,256]{3,2,1,0:T(8,128)(2,1)}), bf16[2,16,132,256]{3,2,1,0:T(8,128)(2,1)}) %all-gather.10.cloned.1.call-update) | async-done | bytes 2162704 | tf_op jit(solution)/shard_map/all_gather | solution.py:120
  169.0 1.6 copy-done
  170.6 4.2 %shard_map.97 = (f32[512,256]{1,0:T(8,128)S(1)}, f32[16,256]{1,0:T(8,128)S(1)}, f32[512,256]{1,0:T(8,128)S(1)}, f32[16,256]{1,0:T(8,128)S(1)}) custom-call(bf16[4,133,768]{2,1,0:T(8,128)(2,1)S(1)} %all-gather.1.qi_ref, bf16[16,768]{1,0:T(8,128)(2,1)S(1)} %reshape.176.qt_ref, bf16[2,16,132,256]{3,2,1,0:T(8,128)(2,1)S(1)} %copy-done, ...), custom_call_target="tpu_custom_call" | custom-call | tf_op jit(solution)/shard_map/pallas_call | solution.py:62
  174.8 1.3 slice.135
  177.7 6.7 %all-to-all-start.2 = ((bf16[4,132,260]{2,1,0:T(8,128)(2,1)}), bf16[4,132,260]{2,1,0:T(8,128)(2,1)S(1)}, u32[]{:S(2)}, u32[]{:S(2)}) async-start(bf16[4,132,260]{2,1,0:T(8,128)(2,1)} %pad_maximum_fusion.2), calls=%async_computation.2 | async-start | bytes 835584 | tf_op jit(solution)/shard_map/all_to_all | solution.py:134
  185.8 9.7 %all-to-all-done.2 = bf16[4,132,260]{2,1,0:T(8,128)(2,1)S(1)} async-done(((bf16[4,132,260]{2,1,0:T(8,128)(2,1)}), bf16[4,132,260]{2,1,0:T(8,128)(2,1)S(1)}, u32[]{:S(2)}, u32[]{:S(2)}) %all-to-all-start.2) | async-done | bytes 274592 | tf_op jit(solution)/shard_map/all_to_all | solution.py:134
  195.5 4.6 %all-to-all-start.4 = ((bf16[4,132,260]{2,1,0:T(8,128)(2,1)}), bf16[4,132,260]{2,1,0:T(8,128)(2,1)S(1)}, u32[]{:S(2)}, u32[]{:S(2)}) async-start(bf16[4,132,260]{2,1,0:T(8,128)(2,1)} %pad_maximum_fusion.3), calls=%async_computation.4 | async-start | bytes 835584 | tf_op jit(solution)/shard_map/all_to_all | solution.py:134
  201.3 9.4 %all-to-all-done.4 = bf16[4,132,260]{2,1,0:T(8,128)(2,1)S(1)} async-done(((bf16[4,132,260]{2,1,0:T(8,128)(2,1)}), bf16[4,132,260]{2,1,0:T(8,128)(2,1)S(1)}, u32[]{:S(2)}, u32[]{:S(2)}) %all-to-all-start.4) | async-done | bytes 274592 | tf_op jit(solution)/shard_map/all_to_all | solution.py:134
  210.7 6.8 %all-to-all-start.1 = ((bf16[32,4,256]{2,0,1:T(8,128)(2,1)}), bf16[32,4,256]{2,0,1:T(8,128)(2,1)S(1)}, u32[]{:S(2)}, u32[]{:S(2)}) async-start(bf16[32,4,256]{2,0,1:T(8,128)(2,1)} %copy.115), calls=%async_computation.1 | async-start | bytes 131072 | tf_op jit(solution)/shard_map/all_to_all | solution.py:142
  218.7 2.2 all-to-all-done.1
  220.8 4.1 %all-to-all-start.3 = ((bf16[32,4,256]{2,0,1:T(8,128)(2,1)}), bf16[32,4,256]{2,0,1:T(8,128)(2,1)S(1)}, u32[]{:S(2)}, u32[]{:S(2)}) async-start(bf16[32,4,256]{2,0,1:T(8,128)(2,1)} %copy.120), calls=%async_computation.3 | async-start | bytes 131072 | tf_op jit(solution)/shard_map/all_to_all | solution.py:142
  225.7 2.5 %all-to-all-done.3 = bf16[32,4,256]{2,0,1:T(8,128)(2,1)S(1)} async-done(((bf16[32,4,256]{2,0,1:T(8,128)(2,1)}), bf16[32,4,256]{2,0,1:T(8,128)(2,1)S(1)}, u32[]{:S(2)}, u32[]{:S(2)}) %all-to-all-start.3) | async-done | bytes 65568 | tf_op jit(solution)/shard_map/all_to_all | solution.py:142
  228.2 4.1 %all-to-all-start.5 = ((bf16[32,4,256]{2,0,1:T(8,128)(2,1)}), bf16[32,4,256]{2,0,1:T(8,128)(2,1)S(1)}, u32[]{:S(2)}, u32[]{:S(2)}) async-start(bf16[32,4,256]{2,0,1:T(8,128)(2,1)} %copy.125), calls=%async_computation.5 | async-start | bytes 131072 | tf_op jit(solution)/shard_map/all_to_all | solution.py:142
  232.9 2.7 %all-to-all-done.5 = bf16[32,4,256]{2,0,1:T(8,128)(2,1)S(1)} async-done(((bf16[32,4,256]{2,0,1:T(8,128)(2,1)}), bf16[32,4,256]{2,0,1:T(8,128)(2,1)S(1)}, u32[]{:S(2)}, u32[]{:S(2)}) %all-to-all-start.5) | async-done | bytes 65568 | tf_op jit(solution)/shard_map/all_to_all | solution.py:142
  (143 shorter events, 19.4 us)
Async XLA Ops:
  7.2 2.6 %copy-start.3 = (bf16[128,768]{1,0:T(8,128)(2,1)S(1)}, bf16[128,768]{1,0:T(8,128)(2,1)}, u32[]{:S(2)}) copy-start(bf16[128,768]{1,0:T(8,128)(2,1)} %param.9) | copy-start | bytes 589828
  7.2 2.3 copy-start.6
  7.2 2.6 %copy-start.4 = (bf16[128,768]{1,0:T(8,128)(2,1)S(1)}, bf16[128,768]{1,0:T(8,128)(2,1)}, u32[]{:S(2)}) copy-start(bf16[128,768]{1,0:T(8,128)(2,1)} %param.10) | copy-start | bytes 589828
  7.2 2.6 %copy-start.8 = (bf16[4,768]{1,0:T(4,128)(2,1)S(1)}, bf16[4,768]{1,0:T(4,128)(2,1)}, u32[]{:S(2)}) copy-start(bf16[4,768]{1,0:T(4,128)(2,1)} %param.13) | copy-start | bytes 18436
  7.2 56.3 %all-gather.6.cloned.1.call-start = ((), (), s32[]{:S(2)}) async-start(), calls=%async_computation.6 | async-start | bytes 2367488 | tf_op jit(solution)/shard_map/all_gather | solution.py:120
  9.3 2.9 %copy-start.5 = (bf16[128,768]{1,0:T(8,128)(2,1)S(1)}, bf16[128,768]{1,0:T(8,128)(2,1)}, u32[]{:S(2)}) copy-start(bf16[128,768]{1,0:T(8,128)(2,1)} %param.8) | copy-start | bytes 589828
  9.7 2.7 %copy-start.7 = (bf16[4,768]{1,0:T(4,128)(2,1)S(1)}, bf16[4,768]{1,0:T(4,128)(2,1)}, u32[]{:S(2)}) copy-start(bf16[4,768]{1,0:T(4,128)(2,1)} %param.11) | copy-start | bytes 18436
  9.8 3.1 %copy-start.9 = (s32[6,1,64]{2,1,0:T(1,128)S(1)}, s32[6,1,64]{2,1,0:T(1,128)}, u32[]{:S(2)}) copy-start(s32[6,1,64]{2,1,0:T(1,128)} %param.15) | copy-start | bytes 4612
  10.7 105.0 %all-gather.8.cloned.1.call-start = ((), (), s32[]{:S(2)}) async-start(), calls=%async_computation.7 | async-start | bytes 2367488 | tf_op jit(solution)/shard_map/all_gather | solution.py:120
  11.4 156.4 %all-gather.10.cloned.1.call-start = ((), (), s32[]{:S(2)}) async-start(), calls=%async_computation.8 | async-start | bytes 2367488 | tf_op jit(solution)/shard_map/all_gather | solution.py:120
  64.4 1.6 copy-start.2
  73.2 104.6 %all-to-all-start = ((bf16[4,132,260]{2,1,0:T(8,128)(2,1)}), bf16[4,132,260]{2,1,0:T(8,128)(2,1)S(1)}, u32[]{:S(2)}, u32[]{:S(2)}) async-start(bf16[4,132,260]{2,1,0:T(8,128)(2,1)} %pad_maximum_fusion.1), calls=%async_computation | async-start | bytes 835584 | tf_op jit(solution)/shard_map/all_to_all | solution.py:134
  116.6 1.6 copy-start.1
  169.0 1.6 copy-start
  177.7 17.7 %all-to-all-start.2 = ((bf16[4,132,260]{2,1,0:T(8,128)(2,1)}), bf16[4,132,260]{2,1,0:T(8,128)(2,1)S(1)}, u32[]{:S(2)}, u32[]{:S(2)}) async-start(bf16[4,132,260]{2,1,0:T(8,128)(2,1)} %pad_maximum_fusion.2), calls=%async_computation.2 | async-start | bytes 835584 | tf_op jit(solution)/shard_map/all_to_all | solution.py:134
  195.5 15.2 %all-to-all-start.4 = ((bf16[4,132,260]{2,1,0:T(8,128)(2,1)}), bf16[4,132,260]{2,1,0:T(8,128)(2,1)S(1)}, u32[]{:S(2)}, u32[]{:S(2)}) async-start(bf16[4,132,260]{2,1,0:T(8,128)(2,1)} %pad_maximum_fusion.3), calls=%async_computation.4 | async-start | bytes 835584 | tf_op jit(solution)/shard_map/all_to_all | solution.py:134
  210.7 10.1 %all-to-all-start.1 = ((bf16[32,4,256]{2,0,1:T(8,128)(2,1)}), bf16[32,4,256]{2,0,1:T(8,128)(2,1)S(1)}, u32[]{:S(2)}, u32[]{:S(2)}) async-start(bf16[32,4,256]{2,0,1:T(8,128)(2,1)} %copy.115), calls=%async_computation.1 | async-start | bytes 131072 | tf_op jit(solution)/shard_map/all_to_all | solution.py:142
  220.8 7.4 %all-to-all-start.3 = ((bf16[32,4,256]{2,0,1:T(8,128)(2,1)}), bf16[32,4,256]{2,0,1:T(8,128)(2,1)S(1)}, u32[]{:S(2)}, u32[]{:S(2)}) async-start(bf16[32,4,256]{2,0,1:T(8,128)(2,1)} %copy.120), calls=%async_computation.3 | async-start | bytes 131072 | tf_op jit(solution)/shard_map/all_to_all | solution.py:142
  228.2 7.4 %all-to-all-start.5 = ((bf16[32,4,256]{2,0,1:T(8,128)(2,1)}), bf16[32,4,256]{2,0,1:T(8,128)(2,1)S(1)}, u32[]{:S(2)}, u32[]{:S(2)}) async-start(bf16[32,4,256]{2,0,1:T(8,128)(2,1)} %copy.125), calls=%async_computation.5 | async-start | bytes 131072 | tf_op jit(solution)/shard_map/all_to_all | solution.py:142
Sparse Core Ops, SparseCore 0:
  11.1 52.3 all-gather.5
  66.0 49.6 all-gather.7
  118.1 49.6 all-gather.9

commit v5 on v3

--- a/solution.py
+++ b/solution.py
@@ -6,7 +6,9 @@
 from jax.sharding import Mesh, PartitionSpec as P
 
 BLOCK = 128
-QUERY_GROUP = 4
+SIDE = 4
+QUERY_AXES = "x"
+KEY_AXES = ("y", "zh")
 
 
 def normed(values, gain, heads):
@@ -88,27 +90,33 @@
     heads = width // head_size
     text_rows = q_txt.shape[0]
     stride = rows + text_rows
-    groups_q = lax.axis_size("qq")
-    groups_k = lax.axis_size("kk")
-    own_q = lax.axis_index("qq")
+    groups_q = lax.axis_size(QUERY_AXES)
+    groups_k = lax.axis_size(KEY_AXES)
+    own_x = lax.axis_index("x")
+    size_x = lax.axis_size("x")
+    size_y = lax.axis_size("y")
 
+    map_row = block_map.reshape(1, -1).astype(jnp.bfloat16)
+    map_row = jnp.pad(map_row, ((0, 0), (0, width - map_row.shape[1])))
     queries = jnp.concatenate(
-        [normed(q_img, norm_gains[0], heads), normed(q_txt, norm_gains[2], heads)], axis=0
-    ).reshape(1, stride, width)
+        [normed(q_img, norm_gains[0], heads).reshape(rows, width),
+         normed(q_txt, norm_gains[2], heads).reshape(text_rows, width),
+         map_row], axis=0
+    ).reshape(1, stride + 1, width)
     keys = jnp.concatenate(
         [normed(k_img, norm_gains[1], heads), normed(k_txt, norm_gains[3], heads)], axis=0
     ).reshape(1, stride, width)
     values = jnp.concatenate([v_img, v_txt], axis=0).reshape(1, stride, width)
     pair = jnp.stack([keys, values], axis=0)
 
-    all_q = lax.all_gather(queries, "qq", axis=0, tiled=True)
-    all_kv = lax.all_gather(pair, "kk", axis=1, tiled=True)
-    flags = lax.all_gather(block_map, "qq", axis=1, tiled=True)
-    flags = flags.reshape(heads, groups_q, groups_k, groups_q)
-    flags = lax.dynamic_index_in_dim(flags, own_q, axis=3, keepdims=False)
+    all_q = lax.all_gather(queries, QUERY_AXES, axis=0, tiled=True)
+    all_kv = lax.all_gather(pair, KEY_AXES, axis=1, tiled=True)
+    flags = all_q[:, stride, :block_map.size].reshape(groups_q, heads, size_y, size_x, -1)
+    flags = lax.dynamic_index_in_dim(flags, own_x, axis=3, keepdims=False)
+    flags = flags.reshape(groups_q, heads, groups_k).transpose(1, 0, 2)
     flags = jnp.repeat(flags, BLOCK, axis=2)
 
-    qt = all_q[:, rows:].reshape(groups_q * text_rows, width)
+    qt = all_q[:, rows:stride].reshape(groups_q * text_rows, width)
     kt = all_kv[0, :, rows:].reshape(groups_k * text_rows, width)
     vt = all_kv[1, :, rows:].reshape(groups_k * text_rows, width)
 
@@ -123,7 +131,7 @@
     denom_hi = denom.astype(jnp.bfloat16)
     denom_lo = (denom - denom_hi.astype(jnp.float32)).astype(jnp.bfloat16)
     packed = jnp.concatenate([numer.astype(jnp.bfloat16), denom_hi, denom_lo], axis=2)
-    packed = lax.all_to_all(packed, "qq", split_axis=0, concat_axis=0, tiled=True)
+    packed = lax.all_to_all(packed, QUERY_AXES, split_axis=0, concat_axis=0, tiled=True)
     packed = jnp.sum(packed.astype(jnp.float32), axis=0)
     numer = packed[:, :width].reshape(stride, heads, head_size)
     denom = packed[:, width:width + heads] + packed[:, width + heads:]
@@ -145,10 +153,10 @@
 def solution(mesh):
     sections, seq = mesh.devices.shape
     grid = Mesh(
-        mesh.devices.reshape(sections, seq // QUERY_GROUP, QUERY_GROUP),
-        ("section", "kk", "qq"),
+        mesh.devices.reshape(sections, seq // (SIDE * SIDE), SIDE, SIDE),
+        ("section", "y", "x", "zh"),
     )
-    rows = ("kk", "qq")
+    rows = ("y", "x", "zh")
     placed = (
         P(rows, "section"),
         P(rows, "section"),

time: 152 us -> 170 us (1.12)
  waiting for transfers between devices: 41.2 us -> 84.1 us
  blocking collectives: 63.5 us -> 29.4 us
  starting transfers between devices: 5.59 us -> 13.8 us
    all_gather x1, waiting for transfers between devices: 37.7 us -> 80.6 us  [body(): all_kv = lax.all_gather(pair, KEY_AXES, axis=1, tiled=True)]
    all_gather x2 -> x1, blocking collectives: 32.1 us -> 13 us  [body(): all_q = lax.all_gather(queries, QUERY_AXES, axis=0, tiled=True)]
    all_to_all x1, blocking collectives: 31.5 us -> 16.4 us  [body(): lax.all_to_all(packed, QUERY_AXES, split_axis=0, concat_axis=0, tiled=True)]
    all_to_all x1, starting transfers between devices: 5.55 us -> 13.7 us  [body(): lax.all_to_all(image_part.reshape(rows // sections, sections, width), 'se...]
where the time goes in v5:
time: 170 us; the launch traced here: 169 us
  waiting for transfers between devices  84.1 us (49%)
  blocking collectives  29.4 us (17%)
  between operations  14.5 us (9%)
  starting transfers between devices  13.8 us (8%)
  Pallas kernels  12.7 us (7%)
  local copies, waits for them, and re-layouts  10.9 us (6%)
  other arithmetic  3.71 us (2%)
    all_gather x1, waiting for transfers between devices, body(): all_kv = lax.all_gather(pair, KEY_AXES, axis=1, tiled=True)  80.6 us
    all_to_all x1, blocking collectives, body(): lax.all_to_all(packed, QUERY_AXES, split_axis=0, concat_axis=0, tiled=True)  16.4 us
    all_to_all x1, starting transfers between devices, body(): lax.all_to_all(image_part.reshape(rows // sections, sections, width), 'se...  13.7 us
    all_gather x1, blocking collectives, body(): all_q = lax.all_gather(queries, QUERY_AXES, axis=0, tiled=True)  13 us
    pallas_call x1, Pallas kernels, attend(): pl.pallas_call(attend_kernel, grid=(heads,), in_specs=[pl.BlockSpec((grou...  12.7 us
    all_to_all x1, waiting for transfers between devices, body(): lax.all_to_all(image_part.reshape(rows // sections, sections, width), 'se...  3.49 us
  transfers between devices with their start and end apart: 2, of which 2 were waited for; matrix products, arithmetic and copies ran while one was open for 2% of the time, Pallas kernels for 0%

profile of v5, /device:TPU:1, one launch (start us, length us, event | category | flops | bytes accessed | tf_op | source)
XLA Modules:
  0.0 169.1 jit_solution(10593089338361749512)
XLA Ops:
  7.3 0.8 slice_bitcast_fusion.1
  8.1 0.7 convert_multiply_fusion.5
  9.0 1.0 convert_multiply_fusion.1
  10.5 0.8 pad_maximum_fusion.1
  11.5 0.2 convert_element_type.83
  11.9 0.2 copy.45
  12.3 0.2 fusion.3
  12.7 13.0 %all-gather.1.qi_ref = bf16[4,133,768]{2,1,0:T(8,128)(2,1)S(1)} all-gather(bf16[1,133,768]{2,1,0:T(8,128)(2,1)S(1)} %copy.46), channel_id=2, replica_groups=mesh['section'=4,'y'=4,'x'=4,'zh'=4] {'x'}, dimensions={0}, use_global_device_ids=true | all-gather | bytes 1021440 | tf_op jit(solution)/shard_map/all_gather | solution.py:112
  25.8 0.2 reshape_squeeze.11
  26.1 0.2 dynamic-slice_reduce_fusion
  26.5 80.6 %all-gather.4.cloned.1.call-done.ki_ref.vi_ref = bf16[2,16,132,768]{3,2,1,0:T(8,128)(2,1)} async-done(((bf16[2,1,132,768]{3,2,1,0:T(8,128)(2,1)}), bf16[2,16,132,768]{3,2,1,0:T(8,128)(2,1)}) %all-gather.4.cloned.1.call-update) | async-done | bytes 6488080 | tf_op jit(solution)/shard_map/all_gather | solution.py:113
  107.1 1.1 fusion.15
  108.2 12.7 %shard_map.95 = (f32[512,768]{1,0:T(8,128)S(1)}, f32[16,768]{1,0:T(8,128)S(1)}, f32[512,768]{1,0:T(8,128)S(1)}, f32[16,768]{1,0:T(8,128)S(1)}) custom-call(bf16[4,133,768]{2,1,0:T(8,128)(2,1)S(1)} %all-gather.1.qi_ref, bf16[16,768]{1,0:T(8,128)(2,1)S(1)} %reshape.126.qt_ref, bf16[2,16,132,768]{3,2,1,0:T(8,128)(2,1)} %all-gather.4.cloned.1.call-done.ki_ref.vi_ref, ...), custom_call_target="tpu_custom_call" | custom-call | tf_op jit(solution)/shard_map/pallas_call | solution.py:64
  121.0 1.1 copy-done
  122.3 2.6 %slice.53 = f32[512,6]{1,0:T(8,128)S(1)} slice(f32[512,768]{1,0:T(8,128)} %copy-done), slice={[0:512:1], [0:768:128]} | slice | bytes 24576 | tf_op jit(solution)/shard_map/slice | solution.py:128
  125.2 0.2 copy.52
  125.3 0.2 copy.53
  125.7 16.4 %all_to_all.17 = bf16[4,132,780]{2,1,0:T(8,128)(2,1)S(1)} all-to-all(bf16[4,132,780]{2,1,0:T(8,128)(2,1)S(1)} %pad_maximum_fusion), channel_id=1, replica_groups=mesh['section'=4,'y'=4,'x'=4,'zh'=4] {'x'}, dimensions={0} | all-to-all | bytes 1647360 | tf_op jit(solution)/shard_map/all_to_all | solution.py:134
  142.3 0.2 div.27
  142.8 0.7 copy.54
  143.5 13.7 %all-to-all-start.1 = ((bf16[32,4,768]{2,0,1:T(8,128)(2,1)}), bf16[32,4,768]{2,0,1:T(8,128)(2,1)S(1)}, u32[]{:S(2)}, u32[]{:S(2)}) async-start(bf16[32,4,768]{2,0,1:T(8,128)(2,1)} %copy.54), calls=%async_computation.1 | async-start | bytes 393216 | tf_op jit(solution)/shard_map/all_to_all | solution.py:143
  157.2 0.6 slice.68
  157.8 3.5 %all-to-all-done.1 = bf16[32,4,768]{2,0,1:T(8,128)(2,1)S(1)} async-done(((bf16[32,4,768]{2,0,1:T(8,128)(2,1)}), bf16[32,4,768]{2,0,1:T(8,128)(2,1)S(1)}, u32[]{:S(2)}, u32[]{:S(2)}) %all-to-all-start.1) | async-done | bytes 196640 | tf_op jit(solution)/shard_map/all_to_all | solution.py:143
  161.5 0.8 all_to_all.14
  (70 shorter events, 3.0 us)
Async XLA Ops:
  7.2 3.2 %copy-start.4 = (bf16[4,768]{1,0:T(4,128)(2,1)S(1)}, bf16[4,768]{1,0:T(4,128)(2,1)}, u32[]{:S(2)}) copy-start(bf16[4,768]{1,0:T(4,128)(2,1)} %param.12) | copy-start | bytes 18436
  7.2 3.3 %copy-start.1 = (bf16[128,768]{1,0:T(8,128)(2,1)S(1)}, bf16[128,768]{1,0:T(8,128)(2,1)}, u32[]{:S(2)}) copy-start(bf16[128,768]{1,0:T(8,128)(2,1)} %param.9) | copy-start | bytes 589828
  7.2 3.2 %copy-start.6 = (bf16[4,768]{1,0:T(4,128)(2,1)S(1)}, bf16[4,768]{1,0:T(4,128)(2,1)}, u32[]{:S(2)}) copy-start(bf16[4,768]{1,0:T(4,128)(2,1)} %param.13) | copy-start | bytes 18436
  7.2 3.2 %copy-start.2 = (bf16[128,768]{1,0:T(8,128)(2,1)S(1)}, bf16[128,768]{1,0:T(8,128)(2,1)}, u32[]{:S(2)}) copy-start(bf16[128,768]{1,0:T(8,128)(2,1)} %param.10) | copy-start | bytes 589828
  7.2 99.9 %all-gather.4.cloned.1.call-start = ((), (), s32[]{:S(2)}) async-start(), calls=%async_computation.2 | async-start | bytes 7102464 | tf_op jit(solution)/shard_map/all_gather | solution.py:113
  10.1 1.2 copy-start.5
  10.2 1.4 copy-start.7
  10.2 1.8 %copy-start.3 = (bf16[128,768]{1,0:T(8,128)(2,1)S(1)}, bf16[128,768]{1,0:T(8,128)(2,1)}, u32[]{:S(2)}) copy-start(bf16[128,768]{1,0:T(8,128)(2,1)} %param.8) | copy-start | bytes 589828
  121.0 1.2 copy-start
  143.5 17.8 %all-to-all-start.1 = ((bf16[32,4,768]{2,0,1:T(8,128)(2,1)}), bf16[32,4,768]{2,0,1:T(8,128)(2,1)S(1)}, u32[]{:S(2)}, u32[]{:S(2)}) async-start(bf16[32,4,768]{2,0,1:T(8,128)(2,1)} %copy.54), calls=%async_computation.1 | async-start | bytes 393216 | tf_op jit(solution)/shard_map/all_to_all | solution.py:143
Sparse Core Ops, SparseCore 0:
  11.5 95.5 all-gather.3

commit v6 on v5

--- a/solution.py
+++ b/solution.py
@@ -7,8 +7,8 @@
 
 BLOCK = 128
 SIDE = 4
-QUERY_AXES = "x"
-KEY_AXES = ("y", "zh")
+QUERY_AXES = ("x_lo", "zh")
+KEY_AXES = ("y", "x_hi")
 
 
 def normed(values, gain, heads):
@@ -92,9 +92,6 @@
     stride = rows + text_rows
     groups_q = lax.axis_size(QUERY_AXES)
     groups_k = lax.axis_size(KEY_AXES)
-    own_x = lax.axis_index("x")
-    size_x = lax.axis_size("x")
-    size_y = lax.axis_size("y")
 
     map_row = block_map.reshape(1, -1).astype(jnp.bfloat16)
     map_row = jnp.pad(map_row, ((0, 0), (0, width - map_row.shape[1])))
@@ -111,8 +108,15 @@
 
     all_q = lax.all_gather(queries, QUERY_AXES, axis=0, tiled=True)
     all_kv = lax.all_gather(pair, KEY_AXES, axis=1, tiled=True)
-    flags = all_q[:, stride, :block_map.size].reshape(groups_q, heads, size_y, size_x, -1)
-    flags = lax.dynamic_index_in_dim(flags, own_x, axis=3, keepdims=False)
+    seq_axes = ("y", "x_hi", "x_lo", "zh")
+    flags = all_q[:, stride, :block_map.size].reshape(
+        (groups_q, heads) + tuple(lax.axis_size(n) for n in seq_axes)
+    )
+    kept = [n for n in seq_axes]
+    for name in QUERY_AXES:
+        place = 2 + kept.index(name)
+        flags = lax.dynamic_index_in_dim(flags, lax.axis_index(name), axis=place, keepdims=False)
+        kept.remove(name)
     flags = flags.reshape(groups_q, heads, groups_k).transpose(1, 0, 2)
     flags = jnp.repeat(flags, BLOCK, axis=2)
 
@@ -152,11 +156,12 @@
 
 def solution(mesh):
     sections, seq = mesh.devices.shape
+    side = SIDE
     grid = Mesh(
-        mesh.devices.reshape(sections, seq // (SIDE * SIDE), SIDE, SIDE),
-        ("section", "y", "x", "zh"),
+        mesh.devices.reshape(sections, seq // (side * side), 2, side // 2, side),
+        ("section", "y", "x_hi", "x_lo", "zh"),
     )
-    rows = ("y", "x", "zh")
+    rows = ("y", "x_hi", "x_lo", "zh")
     placed = (
         P(rows, "section"),
         P(rows, "section"),

time: 170 us -> 240 us (1.41)
  waiting for transfers between devices: 84.1 us -> 126 us
  blocking collectives: 29.4 us -> 52.9 us
  starting transfers between devices: 13.8 us -> 5.5 us
  local copies, waits for them, and re-layouts: 10.9 us -> 19 us
  other arithmetic: 3.71 us -> 7.08 us
    all_gather x0 -> x1, waiting for transfers between devices: none -> 52.7 us  [body(): all_q = lax.all_gather(queries, QUERY_AXES, axis=0, tiled=True)]
    all_to_all x1, blocking collectives: 16.4 us -> 52.9 us  [body(): lax.all_to_all(packed, QUERY_AXES, split_axis=0, concat_axis=0, tiled=True)]
    all_gather x1 -> x0, blocking collectives: 13 us -> none  [body(): all_q = lax.all_gather(queries, QUERY_AXES, axis=0, tiled=True)]
    all_gather x1, waiting for transfers between devices: 80.6 us -> 70 us  [body(): all_kv = lax.all_gather(pair, KEY_AXES, axis=1, tiled=True)]
    all_to_all x1, starting transfers between devices: 13.7 us -> 5.42 us  [body(): lax.all_to_all(image_part.reshape(rows // sections, sections, width), 'se...]
    unnamed x22 -> x20, local copies, waits for them, and re-layouts: 1.75 us -> 4.47 us
  transfers between devices with their start and end apart: 2 -> 3, of which waited for: 2 -> 3; matrix products, arithmetic and copies ran while one was open for 2% -> 2% of each run, Pallas kernels for 0% -> 0%
where the time goes in v6:
time: 240 us
  waiting for transfers between devices  126 us (52%)
  blocking collectives  52.9 us (22%)
  local copies, waits for them, and re-layouts  19 us (8%)
  Pallas kernels  14.6 us (6%)
  between operations  14.4 us (6%)
  other arithmetic  7.08 us (3%)
  starting transfers between devices  5.5 us (2%)
    all_gather x1, waiting for transfers between devices, body(): all_kv = lax.all_gather(pair, KEY_AXES, axis=1, tiled=True)  70 us
    all_to_all x1, blocking collectives, body(): lax.all_to_all(packed, QUERY_AXES, split_axis=0, concat_axis=0, tiled=True)  52.9 us
    all_gather x1, waiting for transfers between devices, body(): all_q = lax.all_gather(queries, QUERY_AXES, axis=0, tiled=True)  52.7 us
    pallas_call x1, Pallas kernels, attend(): pl.pallas_call(attend_kernel, grid=(heads,), in_specs=[pl.BlockSpec((grou...  14.6 us
    all_to_all x1, starting transfers between devices, body(): lax.all_to_all(image_part.reshape(rows // sections, sections, width), 'se...  5.42 us
  transfers between devices with their start and end apart: 3, of which 3 were waited for; matrix products, arithmetic and copies ran while one was open for 2% of the time, Pallas kernels for 0%

profile of v6, /device:TPU:1, one launch (start us, length us, event | category | flops | bytes accessed | tf_op | source)
XLA Modules:
  0.0 239.7 jit_solution(2552947753397860231)
XLA Ops:
  7.2 0.7 convert_reduce_fusion.1
  8.0 0.8 slice_bitcast_fusion.1
  8.8 0.7 convert_multiply_fusion.7
  9.9 0.7 fusion.11
  10.8 1.1 copy.43
  12.3 0.8 copy.46
  14.0 0.8 pad_maximum_fusion.1
  14.8 52.7 %all-gather.7.cloned.1.call-done.qi_ref = bf16[8,133,768]{2,1,0:T(8,128)(2,1)} async-done(((bf16[1,133,768]{2,1,0:T(8,128)(2,1)}), bf16[8,133,768]{2,1,0:T(8,128)(2,1)}) %all-gather.7.cloned.1.call-update) | async-done | bytes 1634320 | tf_op jit(solution)/shard_map/all_gather | solution.py:109
  67.5 0.9 slice.60
  68.4 0.8 slice.63
  69.6 70.0 %all-gather.5.cloned.1.call-done.ki_ref.vi_ref = bf16[2,8,132,768]{3,2,1,0:T(8,128)(2,1)} async-done(((bf16[2,1,132,768]{3,2,1,0:T(8,128)(2,1)}), bf16[2,8,132,768]{3,2,1,0:T(8,128)(2,1)}) %all-gather.5.cloned.1.call-update) | async-done | bytes 3244048 | tf_op jit(solution)/shard_map/all_gather | solution.py:110
  139.6 1.0 fusion.15
  140.6 1.4 copy-done
  142.0 14.6 %shard_map.95 = (f32[1024,768]{1,0:T(8,128)S(1)}, f32[32,768]{1,0:T(8,128)S(1)}, f32[1024,768]{1,0:T(8,128)}, f32[32,768]{1,0:T(8,128)S(1)}) custom-call(bf16[8,133,768]{2,1,0:T(8,128)(2,1)S(1)} %copy-done, bf16[32,768]{1,0:T(8,128)(2,1)S(1)} %reshape.128.qt_ref, bf16[2,8,132,768]{3,2,1,0:T(8,128)(2,1)} %all-gather.5.cloned.1.call-done.ki_ref.vi_ref, ...), custom_call_target="tpu_custom_call" | custom-call | tf_op jit(solution)/shard_map/pallas_call | solution.py:64
  157.3 1.0 slice.54
  158.4 4.6 %slice.53 = f32[1024,6]{1,0:T(8,128)} slice(f32[1024,768]{1,0:T(8,128)} %get-tuple-element.8), slice={[0:1024:1], [0:768:128]} | slice | bytes 49152 | tf_op jit(solution)/shard_map/slice | solution.py:132
  163.1 1.2 copy.50
  164.3 1.3 convert.8
  166.2 1.7 pad_maximum_fusion
  167.9 52.9 %all_to_all.17 = bf16[8,132,780]{2,1,0:T(8,128)(2,1)S(1)} all-to-all(bf16[8,132,780]{2,1,0:T(8,128)(2,1)S(1)} %pad_maximum_fusion), channel_id=1, replica_groups=mesh['section'=4,'y'=4,'x_hi'=2,'x_lo'=2,'zh'=4] {'x_lo','zh'}, dimensions={0} | all-to-all | bytes 3294720 | tf_op jit(solution)/shard_map/all_to_all | solution.py:138
  221.7 0.7 copy.54
  222.4 5.4 %all-to-all-start.1 = ((bf16[32,4,768]{2,0,1:T(8,128)(2,1)}), bf16[32,4,768]{2,0,1:T(8,128)(2,1)S(1)}, u32[]{:S(2)}, u32[]{:S(2)}) async-start(bf16[32,4,768]{2,0,1:T(8,128)(2,1)} %copy.54), calls=%async_computation.1 | async-start | bytes 393216 | tf_op jit(solution)/shard_map/all_to_all | solution.py:147
  228.4 3.5 %all-to-all-done.1 = bf16[32,4,768]{2,0,1:T(8,128)(2,1)S(1)} async-done(((bf16[32,4,768]{2,0,1:T(8,128)(2,1)}), bf16[32,4,768]{2,0,1:T(8,128)(2,1)S(1)}, u32[]{:S(2)}, u32[]{:S(2)}) %all-to-all-start.1) | async-done | bytes 196640 | tf_op jit(solution)/shard_map/all_to_all | solution.py:147
  232.0 0.8 all_to_all.14
  (66 shorter events, 5.1 us)
Async XLA Ops:
  7.2 6.1 %copy-start.4 = (bf16[4,768]{1,0:T(4,128)(2,1)S(1)}, bf16[4,768]{1,0:T(4,128)(2,1)}, u32[]{:S(2)}) copy-start(bf16[4,768]{1,0:T(4,128)(2,1)} %param.12) | copy-start | bytes 18436
  7.2 6.2 %copy-start.2 = (bf16[128,768]{1,0:T(8,128)(2,1)S(1)}, bf16[128,768]{1,0:T(8,128)(2,1)}, u32[]{:S(2)}) copy-start(bf16[128,768]{1,0:T(8,128)(2,1)} %param.9) | copy-start | bytes 589828
  7.2 60.3 %all-gather.7.cloned.1.call-start = ((), (), s32[]{:S(2)}) async-start(), calls=%async_computation.3 | async-start | bytes 1880064 | tf_op jit(solution)/shard_map/all_gather | solution.py:109
  11.9 1.9 copy-start.3
  11.9 1.9 copy-start.5
  13.2 126.4 %all-gather.5.cloned.1.call-start = ((), (), s32[]{:S(2)}) async-start(), calls=%async_computation.2 | async-start | bytes 3760128 | tf_op jit(solution)/shard_map/all_gather | solution.py:110
  140.6 1.4 copy-start
  156.7 0.6 copy-start.1
  222.4 9.5 %all-to-all-start.1 = ((bf16[32,4,768]{2,0,1:T(8,128)(2,1)}), bf16[32,4,768]{2,0,1:T(8,128)(2,1)S(1)}, u32[]{:S(2)}, u32[]{:S(2)}) async-start(bf16[32,4,768]{2,0,1:T(8,128)(2,1)} %copy.54), calls=%async_computation.1 | async-start | bytes 393216 | tf_op jit(solution)/shard_map/all_to_all | solution.py:147
Sparse Core Ops, SparseCore 0:
  13.3 54.1 all-gather.6
  70.1 69.3 all-gather.4

commit v7 on v3

--- a/solution.py
+++ b/solution.py
@@ -123,22 +123,24 @@
     denom_hi = denom.astype(jnp.bfloat16)
     denom_lo = (denom - denom_hi.astype(jnp.float32)).astype(jnp.bfloat16)
     packed = jnp.concatenate([numer.astype(jnp.bfloat16), denom_hi, denom_lo], axis=2)
-    packed = lax.all_to_all(packed, "qq", split_axis=0, concat_axis=0, tiled=True)
-    packed = jnp.sum(packed.astype(jnp.float32), axis=0)
-    numer = packed[:, :width].reshape(stride, heads, head_size)
-    denom = packed[:, width:width + heads] + packed[:, width + heads:]
-    result = numer / denom[..., None]
-    merged = result.reshape(stride, width).astype(jnp.bfloat16)
-    image_part = merged[:rows]
-    text_out = merged[rows:]
     sections = lax.axis_size("section")
-    image_out = lax.all_to_all(
-        image_part.reshape(rows // sections, sections, width),
-        "section",
-        split_axis=1,
-        concat_axis=2,
-        tiled=True,
-    )
+    per = rows // sections
+    lanes = packed.shape[2]
+    image_rows = packed[:, :rows].reshape(groups_q, per, sections, lanes).transpose(2, 0, 1, 3)
+    text_part = jnp.broadcast_to(packed[None, :, rows:], (sections, groups_q, text_rows, lanes))
+    packed = jnp.concatenate([image_rows, text_part], axis=2)
+    packed = packed.reshape(sections * groups_q, per + text_rows, lanes)
+    packed = lax.all_to_all(packed, ("section", "qq"), split_axis=0, concat_axis=0, tiled=True)
+    packed = packed.reshape(sections, groups_q, per + text_rows, lanes)
+    packed = jnp.sum(packed.astype(jnp.float32), axis=1)
+    numer = packed[:, :, :width].reshape(sections, per + text_rows, heads, head_size)
+    denom = packed[:, :, width:width + heads] + packed[:, :, width + heads:]
+    result = (numer / denom[..., None]).astype(jnp.bfloat16)
+    image_out = result[:, :per].reshape(sections, per, width).transpose(1, 0, 2)
+    image_out = image_out.reshape(per, 1, sections * width)
+    own_section = lax.axis_index("section")
+    text_out = lax.dynamic_index_in_dim(result[:, per:], own_section, axis=0, keepdims=False)
+    text_out = text_out.reshape(text_rows, width)
     return (image_out, text_out)
 
 

time: 152 us -> 153 us (level)
  blocking collectives: 63.5 us -> 32.1 us
  waiting for transfers between devices: 41.2 us -> 67.7 us
  starting transfers between devices: 5.59 us -> 7.9 us
  local copies, waits for them, and re-layouts: 11 us -> 12.7 us
    all_to_all x1 -> x0, blocking collectives: 31.5 us -> none  [body(): lax.all_to_all(packed, 'qq', split_axis=0, concat_axis=0, tiled=True)]
    all_to_all x1, waiting for transfers between devices: 3.5 us -> 30 us  [body(): lax.all_to_all(packed, ('section', 'qq'), split_axis=0, concat_axis=0, ti...]
    all_to_all x1, starting transfers between devices: 5.55 us -> 7.86 us  [body(): lax.all_to_all(packed, ('section', 'qq'), split_axis=0, concat_axis=0, ti...]
    reshape x2 -> x6, local copies, waits for them, and re-layouts: 0.75 us -> 2.93 us  [the longest x1 1.2 us: body(): packed = packed.reshape(sections * groups_q, per + text_rows, lanes)]
  transfers between devices with their start and end apart: 2 -> 2, of which waited for: 2 -> 2; matrix products, arithmetic and copies ran while one was open for 2% -> 1% of each run, Pallas kernels for 0% -> 0%
where the time goes in v7:
time: 153 us
  waiting for transfers between devices  67.7 us (44%)
  blocking collectives  32.1 us (21%)
  between operations  14.5 us (9%)
  local copies, waits for them, and re-layouts  12.7 us (8%)
  Pallas kernels  12.7 us (8%)
  starting transfers between devices  7.9 us (5%)
  other arithmetic  5 us (3%)
    all_gather x1, waiting for transfers between devices, body(): all_kv = lax.all_gather(pair, 'kk', axis=1, tiled=True)  37.7 us
    all_to_all x1, waiting for transfers between devices, body(): lax.all_to_all(packed, ('section', 'qq'), split_axis=0, concat_axis=0, ti...  30 us
    all_gather x1, blocking collectives, body(): all_q = lax.all_gather(queries, 'qq', axis=0, tiled=True)  16.7 us
    all_gather x1, blocking collectives, body(): flags = lax.all_gather(block_map, 'qq', axis=1, tiled=True)  15.4 us
    pallas_call x1, Pallas kernels, attend(): pl.pallas_call(attend_kernel, grid=(heads,), in_specs=[pl.BlockSpec((grou...  12.7 us
    all_to_all x1, starting transfers between devices, body(): lax.all_to_all(packed, ('section', 'qq'), split_axis=0, concat_axis=0, ti...  7.86 us
  transfers between devices with their start and end apart: 2, of which 2 were waited for; matrix products, arithmetic and copies ran while one was open for 1% of the time, Pallas kernels for 0%

profile of v7, /device:TPU:1, one launch (start us, length us, event | category | flops | bytes accessed | tf_op | source)
XLA Modules:
  0.0 152.6 jit_solution(9801106110355833493)
XLA Ops:
  7.3 0.8 slice_bitcast_fusion.1
  8.1 0.7 convert_multiply_fusion.5
  9.0 1.0 convert_multiply_fusion.1
  10.5 0.8 pad_maximum_fusion.2
  11.4 15.4 %all_gather.11 = s32[6,4,64]{2,0,1:T(8,128)S(1)} all-gather(s32[6,1,64]{2,0,1:T(8,128)S(1)} %copy.73), channel_id=1, replica_groups=mesh['section'=4,'kk'=16,'qq'=4] {'qq'}, dimensions={1}, use_global_device_ids=true | all-gather | bytes 7680 | tf_op jit(solution)/shard_map/all_gather | solution.py:106
  27.0 0.6 dynamic-slice_reduce_fusion
  28.8 16.7 %all_gather.9.qi_ref = bf16[4,132,768]{2,1,0:T(8,128)(2,1)S(1)} all-gather(bf16[1,132,768]{2,1,0:T(8,128)(2,1)S(1)} %copy.70), channel_id=1, replica_groups=mesh['section'=4,'kk'=16,'qq'=4] {'qq'}, dimensions={0}, use_global_device_ids=true | all-gather | bytes 1013760 | tf_op jit(solution)/shard_map/all_gather | solution.py:104
  45.5 37.7 %all-gather.2.cloned.1.call-done.ki_ref.vi_ref = bf16[2,16,132,768]{3,2,1,0:T(8,128)(2,1)} async-done(((bf16[2,1,132,768]{3,2,1,0:T(8,128)(2,1)}), bf16[2,16,132,768]{3,2,1,0:T(8,128)(2,1)}) %all-gather.2.cloned.1.call-update) | async-done | bytes 6488080 | tf_op jit(solution)/shard_map/all_gather | solution.py:105
  83.2 1.1 fusion.12
  84.4 12.7 %shard_map.95 = (f32[512,768]{1,0:T(8,128)S(1)}, f32[16,768]{1,0:T(8,128)S(1)}, f32[512,768]{1,0:T(8,128)S(1)}, f32[16,768]{1,0:T(8,128)S(1)}) custom-call(bf16[4,132,768]{2,1,0:T(8,128)(2,1)S(1)} %all_gather.9.qi_ref, bf16[16,768]{1,0:T(8,128)(2,1)S(1)} %reshape.136.qt_ref, bf16[2,16,132,768]{3,2,1,0:T(8,128)(2,1)} %all-gather.2.cloned.1.call-done.ki_ref.vi_ref, ...), custom_call_target="tpu_custom_call" | custom-call | tf_op jit(solution)/shard_map/pallas_call | solution.py:62
  97.1 1.1 copy-done
  98.4 2.6 %slice.55 = f32[512,6]{1,0:T(8,128)S(1)} slice(f32[512,768]{1,0:T(8,128)} %copy-done), slice={[0:512:1], [0:768:128]} | slice | bytes 24576 | tf_op jit(solution)/shard_map/slice | solution.py:120
  101.2 0.6 copy.75
  101.9 0.2 copy.79
  102.1 0.2 copy.80
  102.4 0.5 pad_maximum_fusion.1
  102.9 0.3 slice.67
  103.3 0.7 pad_maximum_fusion
  104.0 1.2 copy.86
  105.2 7.9 %all-to-all-start = ((bf16[16,36,780]{2,1,0:T(8,128)(2,1)}), bf16[16,36,780]{2,1,0:T(8,128)(2,1)S(1)}, u32[]{:S(2)}, u32[]{:S(2)}) async-start(bf16[16,36,780]{2,1,0:T(8,128)(2,1)} %bitcast.22), calls=%async_computation | async-start | bytes 2293760 | tf_op jit(solution)/shard_map/all_to_all | solution.py:133
  113.1 30.0 %all-to-all-done = bf16[16,36,780]{2,1,0:T(8,128)(2,1)S(1)} async-done(((bf16[16,36,780]{2,1,0:T(8,128)(2,1)}), bf16[16,36,780]{2,1,0:T(8,128)(2,1)S(1)}, u32[]{:S(2)}, u32[]{:S(2)}) %all-to-all-start) | async-done | bytes 898592 | tf_op jit(solution)/shard_map/all_to_all | solution.py:133
  143.7 0.2 divide_convert_fusion
  144.2 0.6 copy.100
  145.0 0.8 reshape.147
  (77 shorter events, 3.7 us)
Async XLA Ops:
  7.2 3.2 %copy-start.4 = (bf16[4,768]{1,0:T(4,128)(2,1)S(1)}, bf16[4,768]{1,0:T(4,128)(2,1)}, u32[]{:S(2)}) copy-start(bf16[4,768]{1,0:T(4,128)(2,1)} %param.12) | copy-start | bytes 18436
  7.2 3.3 %copy-start.1 = (bf16[128,768]{1,0:T(8,128)(2,1)S(1)}, bf16[128,768]{1,0:T(8,128)(2,1)}, u32[]{:S(2)}) copy-start(bf16[128,768]{1,0:T(8,128)(2,1)} %param.9) | copy-start | bytes 589828
  7.2 3.2 %copy-start.6 = (bf16[4,768]{1,0:T(4,128)(2,1)S(1)}, bf16[4,768]{1,0:T(4,128)(2,1)}, u32[]{:S(2)}) copy-start(bf16[4,768]{1,0:T(4,128)(2,1)} %param.13) | copy-start | bytes 18436
  7.2 3.2 %copy-start.2 = (bf16[128,768]{1,0:T(8,128)(2,1)S(1)}, bf16[128,768]{1,0:T(8,128)(2,1)}, u32[]{:S(2)}) copy-start(bf16[128,768]{1,0:T(8,128)(2,1)} %param.10) | copy-start | bytes 589828
  7.2 76.0 %all-gather.2.cloned.1.call-start = ((), (), s32[]{:S(2)}) async-start(), calls=%async_computation.1 | async-start | bytes 7102464 | tf_op jit(solution)/shard_map/all_gather | solution.py:105
  10.1 1.2 copy-start.7
  10.2 16.6 %copy-start.5 = (bf16[4,768]{1,0:T(4,128)(2,1)S(1)}, bf16[4,768]{1,0:T(4,128)(2,1)}, u32[]{:S(2)}) copy-start(bf16[4,768]{1,0:T(4,128)(2,1)} %param.11) | copy-start | bytes 18436
  10.4 17.7 %copy-start.3 = (bf16[128,768]{1,0:T(8,128)(2,1)S(1)}, bf16[128,768]{1,0:T(8,128)(2,1)}, u32[]{:S(2)}) copy-start(bf16[128,768]{1,0:T(8,128)(2,1)} %param.8) | copy-start | bytes 589828
  97.0 1.2 copy-start
  105.2 37.8 %all-to-all-start = ((bf16[16,36,780]{2,1,0:T(8,128)(2,1)}), bf16[16,36,780]{2,1,0:T(8,128)(2,1)S(1)}, u32[]{:S(2)}, u32[]{:S(2)}) async-start(bf16[16,36,780]{2,1,0:T(8,128)(2,1)} %bitcast.22), calls=%async_computation | async-start | bytes 2293760 | tf_op jit(solution)/shard_map/all_to_all | solution.py:133
Sparse Core Ops, SparseCore 0:
  11.5 71.7 all-gather.1

commit v8 on v7

--- a/solution.py
+++ b/solution.py
@@ -16,15 +16,21 @@
     return (floats * lax.rsqrt(power + 1e-06) * gain).astype(jnp.bfloat16)
 
 
-def attend_kernel(qi_ref, qt_ref, ki_ref, kt_ref, vi_ref, vt_ref, fl_ref, ni_ref, nt_ref, di_ref, dt_ref):
-    head_size = qi_ref.shape[-1]
+def attend_kernel(q_ref, qt_ref, ki_ref, kt_ref, vi_ref, vt_ref, fl_ref, num_ref, den_ref):
+    head = pl.program_id(0)
+    head_size = q_ref.shape[-1]
     scale = head_size ** (-0.5)
-    q_blocks = qi_ref.shape[0]
+    q_blocks = q_ref.shape[0]
+    text_rows = qt_ref.shape[0] // q_blocks
     dims = (((1,), (1,)), ((), ()))
     keys_img = ki_ref[0].reshape(-1, head_size)
     keys_txt = kt_ref[...]
     vals_img = vi_ref[0].reshape(-1, head_size)
     vals_txt = vt_ref[...]
+
+    @pl.when(head == 0)
+    def _():
+        den_ref[...] = jnp.zeros(den_ref.shape, den_ref.dtype)
 
     def one(q, flags):
         s_img = lax.dot_general(q, keys_img, dims, preferred_element_type=jnp.float32) * scale
@@ -38,21 +44,23 @@
         num = num + jnp.dot(e_txt.astype(jnp.bfloat16), vals_txt, preferred_element_type=jnp.float32)
         return num, den
 
+    def put(a, lo, hi, num, den):
+        num_ref[a, lo:hi, :] = num
+        lane = lax.broadcasted_iota(jnp.int32, (hi - lo, den_ref.shape[-1]), 1)
+        den_ref[a, lo:hi, :] = jnp.where(lane == head, den, den_ref[a, lo:hi, :])
+
     for a in range(q_blocks):
-        rows = slice(a * BLOCK, (a + 1) * BLOCK)
-        num, den = one(qi_ref[a], fl_ref[0, a:a + 1, :])
-        ni_ref[rows, :] = num
-        di_ref[rows, :] = jnp.broadcast_to(den, num.shape)
+        num, den = one(q_ref[a, 0:BLOCK, :], fl_ref[0, a:a + 1, :])
+        put(a, 0, BLOCK, num, den)
     num, den = one(qt_ref[...], None)
-    nt_ref[...] = num
-    dt_ref[...] = jnp.broadcast_to(den, num.shape)
+    for a in range(q_blocks):
+        part = slice(a * text_rows, (a + 1) * text_rows)
+        put(a, BLOCK, BLOCK + text_rows, num[part], den[part])
 
 
-def attend(qi, qt, kv, kt, vt, fl, heads, head_size):
-    groups_q = qi.shape[0]
+def attend(all_q, qt, kv, kt, vt, fl, heads, head_size):
+    groups_q, stride = all_q.shape[0], all_q.shape[1]
     groups_k = kv.shape[1]
-    n_qi = groups_q * BLOCK
-    n_ki = groups_k * BLOCK
     n_qt, n_kt = qt.shape[0], kt.shape[0]
     width = heads * head_size
 
@@ -63,7 +71,7 @@
         attend_kernel,
         grid=(heads,),
         in_specs=[
-            pl.BlockSpec((groups_q, BLOCK, head_size), lambda h: (0, 0, h)),
+            pl.BlockSpec((groups_q, stride, head_size), lambda h: (0, 0, h)),
             cols(n_qt),
             pl.BlockSpec((1, groups_k, BLOCK, head_size), lambda h: (0, 0, 0, h)),
             cols(n_kt),
@@ -71,15 +79,16 @@
             cols(n_kt),
             pl.BlockSpec((1,) + fl.shape[1:], lambda h: (h, 0, 0)),
         ],
-        out_specs=[cols(n_qi), cols(n_qt), cols(n_qi), cols(n_qt)],
+        out_specs=[
+            pl.BlockSpec((groups_q, stride, head_size), lambda h: (0, 0, h)),
+            pl.BlockSpec((groups_q, stride, BLOCK), lambda h: (0, 0, 0)),
+        ],
         out_shape=[
-            jax.ShapeDtypeStruct((n_qi, width), jnp.float32),
-            jax.ShapeDtypeStruct((n_qt, width), jnp.float32),
-            jax.ShapeDtypeStruct((n_qi, width), jnp.float32),
-            jax.ShapeDtypeStruct((n_qt, width), jnp.float32),
+            jax.ShapeDtypeStruct((groups_q, stride, width), jnp.float32),
+            jax.ShapeDtypeStruct((groups_q, stride, BLOCK), jnp.float32),
         ],
         compiler_params=pltpu.CompilerParams(vmem_limit_bytes=48 * 1024 * 1024),
-    )(qi, qt, kv, kt, kv, vt, fl)
+    )(all_q, qt, kv, kt, kv, vt, fl)
 
 
 def body(q_img, k_img, v_img, q_txt, k_txt, v_txt, norm_gains, block_map):
@@ -112,14 +121,8 @@
     kt = all_kv[0, :, rows:].reshape(groups_k * text_rows, width)
     vt = all_kv[1, :, rows:].reshape(groups_k * text_rows, width)
 
-    ni, nt, di, dt = attend(all_q, qt, all_kv, kt, vt, flags, heads, head_size)
-    numer = jnp.concatenate(
-        [ni.reshape(groups_q, rows, width), nt.reshape(groups_q, text_rows, width)], axis=1
-    )
-    denom = jnp.concatenate(
-        [di[:, ::head_size].reshape(groups_q, rows, heads),
-         dt[:, ::head_size].reshape(groups_q, text_rows, heads)], axis=1
-    )
+    numer, denom = attend(all_q, qt, all_kv, kt, vt, flags, heads, head_size)
+    denom = denom[:, :, :heads]
     denom_hi = denom.astype(jnp.bfloat16)
     denom_lo = (denom - denom_hi.astype(jnp.float32)).astype(jnp.bfloat16)
     packed = jnp.concatenate([numer.astype(jnp.bfloat16), denom_hi, denom_lo], axis=2)

time: 153 us -> 149 us (0.974)
  local copies, waits for them, and re-layouts: 12.7 us -> 8.15 us
    slice x2 -> x1, local copies, waits for them, and re-layouts: 2.63 us -> 0.01 us  [body(): packed[None, :, rows:]]
where the time goes in v8:
time: 149 us; the launch traced here: 148 us
  waiting for transfers between devices  67.7 us (45%)
  blocking collectives  32.1 us (22%)
  between operations  14.5 us (10%)
  Pallas kernels  13.4 us (9%)
  local copies, waits for them, and re-layouts  8.15 us (5%)
  starting transfers between devices  7.91 us (5%)
  other arithmetic  4.59 us (3%)
    all_gather x1, waiting for transfers between devices, body(): all_kv = lax.all_gather(pair, 'kk', axis=1, tiled=True)  37.7 us
    all_to_all x1, waiting for transfers between devices, body(): lax.all_to_all(packed, ('section', 'qq'), split_axis=0, concat_axis=0, ti...  30 us
    all_gather x1, blocking collectives, body(): all_q = lax.all_gather(queries, 'qq', axis=0, tiled=True)  16.7 us
    all_gather x1, blocking collectives, body(): flags = lax.all_gather(block_map, 'qq', axis=1, tiled=True)  15.4 us
    pallas_call x1, Pallas kernels, attend(): pl.pallas_call(attend_kernel, grid=(heads,), in_specs=[pl.BlockSpec((grou...  13.4 us
    all_to_all x1, starting transfers between devices, body(): lax.all_to_all(packed, ('section', 'qq'), split_axis=0, concat_axis=0, ti...  7.87 us
  transfers between devices with their start and end apart: 2, of which 2 were waited for; matrix products, arithmetic and copies ran while one was open for 1% of the time, Pallas kernels for 0%

profile of v8, /device:TPU:1, one launch (start us, length us, event | category | flops | bytes accessed | tf_op | source)
XLA Modules:
  0.0 148.3 jit_solution(1125068410230846130)
XLA Ops:
  7.3 0.8 slice_bitcast_fusion.1
  8.1 0.7 convert_multiply_fusion.5
  9.0 1.0 convert_multiply_fusion.1
  10.2 0.2 copy.60
  10.5 0.8 pad_maximum_fusion.2
  11.4 15.4 %all_gather.11 = s32[6,4,64]{2,0,1:T(8,128)S(1)} all-gather(s32[6,1,64]{2,0,1:T(8,128)S(1)} %copy.61), channel_id=1, replica_groups=mesh['section'=4,'kk'=16,'qq'=4] {'qq'}, dimensions={1}, use_global_device_ids=true | all-gather | bytes 7680 | tf_op jit(solution)/shard_map/all_gather | solution.py:115
  27.0 0.6 dynamic-slice_reduce_fusion
  27.9 0.2 copy.57
  28.4 0.2 fusion.1
  28.8 16.7 %all_gather.9.q_ref = bf16[4,132,768]{2,1,0:T(8,128)(2,1)S(1)} all-gather(bf16[1,132,768]{2,1,0:T(8,128)(2,1)S(1)} %copy.58), channel_id=1, replica_groups=mesh['section'=4,'kk'=16,'qq'=4] {'qq'}, dimensions={0}, use_global_device_ids=true | all-gather | bytes 1013760 | tf_op jit(solution)/shard_map/all_gather | solution.py:113
  45.5 37.7 %all-gather.2.cloned.1.call-done.ki_ref.vi_ref = bf16[2,16,132,768]{3,2,1,0:T(8,128)(2,1)} async-done(((bf16[2,1,132,768]{3,2,1,0:T(8,128)(2,1)}), bf16[2,16,132,768]{3,2,1,0:T(8,128)(2,1)}) %all-gather.2.cloned.1.call-update) | async-done | bytes 6488080 | tf_op jit(solution)/shard_map/all_gather | solution.py:114
  83.2 1.1 fusion.11
  84.4 13.4 %shard_map.95 = (f32[4,132,768]{2,1,0:T(8,128)S(1)}, f32[4,132,128]{2,1,0:T(8,128)S(1)}) custom-call(bf16[4,132,768]{2,1,0:T(8,128)(2,1)S(1)} %all_gather.9.q_ref, bf16[16,768]{1,0:T(8,128)(2,1)S(1)} %reshape.122.qt_ref, bf16[2,16,132,768]{3,2,1,0:T(8,128)(2,1)} %all-gather.2.cloned.1.call-done.ki_ref.vi_ref, bf16[64,768]{1,0:T(8,128)(2,1)S(1)} %reshape_squeeze.6.kt_ref, ...), custom_call_target="tpu_custom_call" | custom-call | tf_op jit(solution)/shard_map/pallas_call | solution.py:70
  98.2 0.7 copy.63
  99.0 0.7 pad_maximum_fusion
  99.7 1.2 copy.70
  100.9 7.9 %all-to-all-start = ((bf16[16,36,780]{2,1,0:T(8,128)(2,1)}), bf16[16,36,780]{2,1,0:T(8,128)(2,1)S(1)}, u32[]{:S(2)}, u32[]{:S(2)}) async-start(bf16[16,36,780]{2,1,0:T(8,128)(2,1)} %bitcast.19), calls=%async_computation | async-start | bytes 2293760 | tf_op jit(solution)/shard_map/all_to_all | solution.py:136
  108.8 30.0 %all-to-all-done = bf16[16,36,780]{2,1,0:T(8,128)(2,1)S(1)} async-done(((bf16[16,36,780]{2,1,0:T(8,128)(2,1)}), bf16[16,36,780]{2,1,0:T(8,128)(2,1)S(1)}, u32[]{:S(2)}, u32[]{:S(2)}) %all-to-all-start) | async-done | bytes 898592 | tf_op jit(solution)/shard_map/all_to_all | solution.py:136
  138.7 0.2 convert_reduce_fusion
  139.0 0.2 copy.66
  139.2 0.2 reshape.127
  139.4 0.2 divide_convert_fusion
  139.9 0.6 copy.84
  140.6 0.8 reshape.129
  (66 shorter events, 2.6 us)
Async XLA Ops:
  7.2 3.2 %copy-start.3 = (bf16[4,768]{1,0:T(4,128)(2,1)S(1)}, bf16[4,768]{1,0:T(4,128)(2,1)}, u32[]{:S(2)}) copy-start(bf16[4,768]{1,0:T(4,128)(2,1)} %param.12) | copy-start | bytes 18436
  7.2 3.3 %copy-start = (bf16[128,768]{1,0:T(8,128)(2,1)S(1)}, bf16[128,768]{1,0:T(8,128)(2,1)}, u32[]{:S(2)}) copy-start(bf16[128,768]{1,0:T(8,128)(2,1)} %param.9) | copy-start | bytes 589828
  7.2 3.2 %copy-start.5 = (bf16[4,768]{1,0:T(4,128)(2,1)S(1)}, bf16[4,768]{1,0:T(4,128)(2,1)}, u32[]{:S(2)}) copy-start(bf16[4,768]{1,0:T(4,128)(2,1)} %param.13) | copy-start | bytes 18436
  7.2 3.2 %copy-start.1 = (bf16[128,768]{1,0:T(8,128)(2,1)S(1)}, bf16[128,768]{1,0:T(8,128)(2,1)}, u32[]{:S(2)}) copy-start(bf16[128,768]{1,0:T(8,128)(2,1)} %param.10) | copy-start | bytes 589828
  7.2 76.0 %all-gather.2.cloned.1.call-start = ((), (), s32[]{:S(2)}) async-start(), calls=%async_computation.1 | async-start | bytes 7102464 | tf_op jit(solution)/shard_map/all_gather | solution.py:114
  10.1 1.2 copy-start.6
  10.2 16.6 %copy-start.4 = (bf16[4,768]{1,0:T(4,128)(2,1)S(1)}, bf16[4,768]{1,0:T(4,128)(2,1)}, u32[]{:S(2)}) copy-start(bf16[4,768]{1,0:T(4,128)(2,1)} %param.11) | copy-start | bytes 18436
  10.4 17.7 %copy-start.2 = (bf16[128,768]{1,0:T(8,128)(2,1)S(1)}, bf16[128,768]{1,0:T(8,128)(2,1)}, u32[]{:S(2)}) copy-start(bf16[128,768]{1,0:T(8,128)(2,1)} %param.8) | copy-start | bytes 589828
  100.9 37.8 %all-to-all-start = ((bf16[16,36,780]{2,1,0:T(8,128)(2,1)}), bf16[16,36,780]{2,1,0:T(8,128)(2,1)S(1)}, u32[]{:S(2)}, u32[]{:S(2)}) async-start(bf16[16,36,780]{2,1,0:T(8,128)(2,1)} %bitcast.19), calls=%async_computation | async-start | bytes 2293760 | tf_op jit(solution)/shard_map/all_to_all | solution.py:136
Sparse Core Ops, SparseCore 0:
  11.5 71.7 all-gather.1

commit v9 on v8

--- a/solution.py
+++ b/solution.py
@@ -125,19 +125,32 @@
     denom = denom[:, :, :heads]
     denom_hi = denom.astype(jnp.bfloat16)
     denom_lo = (denom - denom_hi.astype(jnp.float32)).astype(jnp.bfloat16)
-    packed = jnp.concatenate([numer.astype(jnp.bfloat16), denom_hi, denom_lo], axis=2)
     sections = lax.axis_size("section")
     per = rows // sections
-    lanes = packed.shape[2]
-    image_rows = packed[:, :rows].reshape(groups_q, per, sections, lanes).transpose(2, 0, 1, 3)
-    text_part = jnp.broadcast_to(packed[None, :, rows:], (sections, groups_q, text_rows, lanes))
-    packed = jnp.concatenate([image_rows, text_part], axis=2)
-    packed = packed.reshape(sections * groups_q, per + text_rows, lanes)
+    count = sections * groups_q
+
+    def by_destination(part):
+        lanes = part.shape[2]
+        image_rows = part[:, :rows].reshape(groups_q, per, sections, lanes).transpose(2, 0, 1, 3)
+        text_part = jnp.broadcast_to(part[None, :, rows:], (sections, groups_q, text_rows, lanes))
+        part = jnp.concatenate([image_rows, text_part], axis=2)
+        return part.reshape(count, -1)
+
+    flat_num = by_destination(numer.astype(jnp.bfloat16))
+    flat_den = by_destination(jnp.concatenate([denom_hi, denom_lo], axis=2))
+    num_size, den_size = flat_num.shape[1], flat_den.shape[1]
+    total = num_size + den_size
+    padded = -(-total // (16 * BLOCK)) * (16 * BLOCK)
+    packed = jnp.concatenate(
+        [flat_num, flat_den, jnp.zeros((count, padded - total), jnp.bfloat16)], axis=1
+    ).reshape(count, padded // BLOCK, BLOCK)
     packed = lax.all_to_all(packed, ("section", "qq"), split_axis=0, concat_axis=0, tiled=True)
-    packed = packed.reshape(sections, groups_q, per + text_rows, lanes)
-    packed = jnp.sum(packed.astype(jnp.float32), axis=1)
-    numer = packed[:, :, :width].reshape(sections, per + text_rows, heads, head_size)
-    denom = packed[:, :, width:width + heads] + packed[:, :, width + heads:]
+    packed = packed.reshape(sections, groups_q, padded)
+    numer = jnp.sum(packed[:, :, :num_size].astype(jnp.float32), axis=1)
+    numer = numer.reshape(sections, per + text_rows, heads, head_size)
+    denom = jnp.sum(packed[:, :, num_size:total].astype(jnp.float32), axis=1)
+    denom = denom.reshape(sections, per + text_rows, 2, heads)
+    denom = denom[:, :, 0] + denom[:, :, 1]
     result = (numer / denom[..., None]).astype(jnp.bfloat16)
     image_out = result[:, :per].reshape(sections, per, width).transpose(1, 0, 2)
     image_out = image_out.reshape(per, 1, sections * width)

time: 149 us -> 145 us (0.973)
  waiting for transfers between devices: 67.7 us -> 61.7 us
    all_gather x1, blocking collectives: 16.7 us -> 22.1 us  [body(): all_q = lax.all_gather(queries, 'qq', axis=0, tiled=True)]
    all_to_all x1, waiting for transfers between devices: 30 us -> 25.2 us  [body(): lax.all_to_all(packed, ('section', 'qq'), split_axis=0, concat_axis=0, ti...]
    all_gather x1, blocking collectives: 15.4 us -> 11.1 us  [body(): flags = lax.all_gather(block_map, 'qq', axis=1, tiled=True)]
where the time goes in v9:
time: 145 us
  waiting for transfers between devices  61.7 us (43%)
  blocking collectives  33.3 us (23%)
  between operations  14.5 us (10%)
  Pallas kernels  13.4 us (9%)
  local copies, waits for them, and re-layouts  9.52 us (7%)
  starting transfers between devices  7.92 us (5%)
  other arithmetic  4.34 us (3%)
    all_gather x1, waiting for transfers between devices, body(): all_kv = lax.all_gather(pair, 'kk', axis=1, tiled=True)  36.5 us
    all_to_all x1, waiting for transfers between devices, body(): lax.all_to_all(packed, ('section', 'qq'), split_axis=0, concat_axis=0, ti...  25.2 us
    all_gather x1, blocking collectives, body(): all_q = lax.all_gather(queries, 'qq', axis=0, tiled=True)  22.1 us
    pallas_call x1, Pallas kernels, attend(): pl.pallas_call(attend_kernel, grid=(heads,), in_specs=[pl.BlockSpec((grou...  13.4 us
    all_gather x1, blocking collectives, body(): flags = lax.all_gather(block_map, 'qq', axis=1, tiled=True)  11.1 us
    all_to_all x1, starting transfers between devices, body(): lax.all_to_all(packed, ('section', 'qq'), split_axis=0, concat_axis=0, ti...  7.88 us
  transfers between devices with their start and end apart: 2, of which 2 were waited for; matrix products, arithmetic and copies ran while one was open for 1% of the time, Pallas kernels for 0%

profile of v9, /device:TPU:1, one launch (start us, length us, event | category | flops | bytes accessed | tf_op | source)
XLA Modules:
  0.0 144.7 jit_solution(9657492749600899902)
XLA Ops:
  7.3 0.9 slice_bitcast_fusion.1
  8.1 1.0 convert_multiply_fusion.1
  9.9 0.8 pad_maximum_fusion.1
  11.2 0.2 copy.80
  11.4 0.2 fusion.1
  11.8 22.1 %all_gather.9.q_ref = bf16[4,132,768]{2,1,0:T(8,128)(2,1)S(1)} all-gather(bf16[1,132,768]{2,1,0:T(8,128)(2,1)S(1)} %copy.81), channel_id=1, replica_groups=mesh['section'=4,'kk'=16,'qq'=4] {'qq'}, dimensions={0}, use_global_device_ids=true | all-gather | bytes 1013760 | tf_op jit(solution)/shard_map/all_gather | solution.py:113
  34.0 11.1 %all_gather.11 = s32[6,4,64]{2,0,1:T(8,128)S(1)} all-gather(s32[6,1,64]{2,0,1:T(8,128)S(1)} %copy.84), channel_id=1, replica_groups=mesh['section'=4,'kk'=16,'qq'=4] {'qq'}, dimensions={1}, use_global_device_ids=true | all-gather | bytes 7680 | tf_op jit(solution)/shard_map/all_gather | solution.py:115
  45.2 0.6 dynamic-slice_reduce_fusion
  46.0 36.5 %all-gather.2.cloned.1.call-done.ki_ref.vi_ref = bf16[2,16,132,768]{3,2,1,0:T(8,128)(2,1)} async-done(((bf16[2,1,132,768]{3,2,1,0:T(8,128)(2,1)}), bf16[2,16,132,768]{3,2,1,0:T(8,128)(2,1)}) %all-gather.2.cloned.1.call-update) | async-done | bytes 6488080 | tf_op jit(solution)/shard_map/all_gather | solution.py:114
  82.5 1.1 fusion.12
  83.7 13.4 %shard_map.95 = (f32[4,132,768]{2,1,0:T(8,128)S(1)}, f32[4,132,128]{2,1,0:T(8,128)S(1)}) custom-call(bf16[4,132,768]{2,1,0:T(8,128)(2,1)S(1)} %all_gather.9.q_ref, bf16[16,768]{1,0:T(8,128)(2,1)S(1)} %reshape.144.qt_ref, bf16[2,16,132,768]{3,2,1,0:T(8,128)(2,1)} %all-gather.2.cloned.1.call-done.ki_ref.vi_ref, bf16[64,768]{1,0:T(8,128)(2,1)S(1)} %reshape_squeeze.6.kt_ref, ...), custom_call_target="tpu_custom_call" | custom-call | tf_op jit(solution)/shard_map/pallas_call | solution.py:70
  98.2 0.2 reshape.147
  98.8 0.3 concatenate.29
  99.1 1.0 copy.98
  100.1 7.9 %all-to-all-start = ((bf16[16,224,128]{2,1,0:T(8,128)(2,1)}), bf16[16,224,128]{2,1,0:T(8,128)(2,1)S(1)}, u32[]{:S(2)}, u32[]{:S(2)}) async-start(bf16[16,224,128]{2,1,0:T(8,128)(2,1)} %bitcast.32), calls=%async_computation | async-start | bytes 1835008 | tf_op jit(solution)/shard_map/all_to_all | solution.py:147
  108.0 25.2 %all-to-all-done = bf16[16,224,128]{2,1,0:T(8,128)(2,1)S(1)} async-done(((bf16[16,224,128]{2,1,0:T(8,128)(2,1)}), bf16[16,224,128]{2,1,0:T(8,128)(2,1)S(1)}, u32[]{:S(2)}, u32[]{:S(2)}) %all-to-all-start) | async-done | bytes 917536 | tf_op jit(solution)/shard_map/all_to_all | solution.py:147
  133.2 0.3 reshape.152
  133.5 1.2 convert_reduce_fusion
  134.8 0.3 reshape.153
  135.1 0.2 reshape.154
  135.7 0.2 divide_convert_fusion
  136.0 0.2 reshape.155
  136.4 0.8 reshape.156
  137.2 0.6 copy.109
  (79 shorter events, 3.8 us)
Async XLA Ops:
  7.2 2.6 %copy-start = (bf16[128,768]{1,0:T(8,128)(2,1)S(1)}, bf16[128,768]{1,0:T(8,128)(2,1)}, u32[]{:S(2)}) copy-start(bf16[128,768]{1,0:T(8,128)(2,1)} %param.9) | copy-start | bytes 589828
  7.2 2.3 %copy-start.3 = (bf16[4,768]{1,0:T(4,128)(2,1)S(1)}, bf16[4,768]{1,0:T(4,128)(2,1)}, u32[]{:S(2)}) copy-start(bf16[4,768]{1,0:T(4,128)(2,1)} %param.12) | copy-start | bytes 18436
  7.2 2.6 %copy-start.1 = (bf16[128,768]{1,0:T(8,128)(2,1)S(1)}, bf16[128,768]{1,0:T(8,128)(2,1)}, u32[]{:S(2)}) copy-start(bf16[128,768]{1,0:T(8,128)(2,1)} %param.10) | copy-start | bytes 589828
  7.2 2.6 %copy-start.5 = (bf16[4,768]{1,0:T(4,128)(2,1)S(1)}, bf16[4,768]{1,0:T(4,128)(2,1)}, u32[]{:S(2)}) copy-start(bf16[4,768]{1,0:T(4,128)(2,1)} %param.13) | copy-start | bytes 18436
  7.2 75.3 %all-gather.2.cloned.1.call-start = ((), (), s32[]{:S(2)}) async-start(), calls=%async_computation.1 | async-start | bytes 7102464 | tf_op jit(solution)/shard_map/all_gather | solution.py:114
  9.3 1.4 copy-start.2
  9.5 1.4 copy-start.4
  10.9 23.0 %copy-start.6 = (s32[6,1,64]{2,1,0:T(1,128)S(1)}, s32[6,1,64]{2,1,0:T(1,128)}, u32[]{:S(2)}) copy-start(s32[6,1,64]{2,1,0:T(1,128)} %param.15) | copy-start | bytes 4612
  100.1 33.1 %all-to-all-start = ((bf16[16,224,128]{2,1,0:T(8,128)(2,1)}), bf16[16,224,128]{2,1,0:T(8,128)(2,1)S(1)}, u32[]{:S(2)}, u32[]{:S(2)}) async-start(bf16[16,224,128]{2,1,0:T(8,128)(2,1)} %bitcast.32), calls=%async_computation | async-start | bytes 1835008 | tf_op jit(solution)/shard_map/all_to_all | solution.py:147
Sparse Core Ops, SparseCore 0:
  10.8 71.6 all-gather.1

commit v10 on v9

--- a/solution.py
+++ b/solution.py
@@ -1,3 +1,5 @@
+import math
+
 import jax
 import jax.numpy as jnp
 from jax import lax
@@ -19,7 +21,7 @@
 def attend_kernel(q_ref, qt_ref, ki_ref, kt_ref, vi_ref, vt_ref, fl_ref, num_ref, den_ref):
     head = pl.program_id(0)
     head_size = q_ref.shape[-1]
-    scale = head_size ** (-0.5)
+    scale = head_size ** (-0.5) * math.log2(math.e)
     q_blocks = q_ref.shape[0]
     text_rows = qt_ref.shape[0] // q_blocks
     dims = (((1,), (1,)), ((), ()))
@@ -35,10 +37,10 @@
     def one(q, flags):
         s_img = lax.dot_general(q, keys_img, dims, preferred_element_type=jnp.float32) * scale
         s_txt = lax.dot_general(q, keys_txt, dims, preferred_element_type=jnp.float32) * scale
-        e_img = jnp.exp(s_img)
+        e_img = jnp.exp2(s_img)
         if flags is not None:
             e_img = jnp.where(flags > 0, e_img, jnp.float32(0.0))
-        e_txt = jnp.exp(s_txt)
+        e_txt = jnp.exp2(s_txt)
         den = jnp.sum(e_img, axis=1, keepdims=True) + jnp.sum(e_txt, axis=1, keepdims=True)
         num = jnp.dot(e_img.astype(jnp.bfloat16), vals_img, preferred_element_type=jnp.float32)
         num = num + jnp.dot(e_txt.astype(jnp.bfloat16), vals_txt, preferred_element_type=jnp.float32)

time: 145 us -> 144 us (level)
  no operation moved by 1% of the time
where the time goes in v10:
time: 144 us
  waiting for transfers between devices  61.7 us (43%)
  blocking collectives  33.3 us (23%)
  between operations  14.5 us (10%)
  Pallas kernels  12.9 us (9%)
  local copies, waits for them, and re-layouts  9.52 us (7%)
  starting transfers between devices  7.97 us (6%)
  other arithmetic  4.34 us (3%)
    all_gather x1, waiting for transfers between devices, body(): all_kv = lax.all_gather(pair, 'kk', axis=1, tiled=True)  36.5 us
    all_to_all x1, waiting for transfers between devices, body(): lax.all_to_all(packed, ('section', 'qq'), split_axis=0, concat_axis=0, ti...  25.2 us
    all_gather x1, blocking collectives, body(): all_q = lax.all_gather(queries, 'qq', axis=0, tiled=True)  22.1 us
    pallas_call x1, Pallas kernels, attend(): pl.pallas_call(attend_kernel, grid=(heads,), in_specs=[pl.BlockSpec((grou...  12.9 us
    all_gather x1, blocking collectives, body(): flags = lax.all_gather(block_map, 'qq', axis=1, tiled=True)  11.1 us
    all_to_all x1, starting transfers between devices, body(): lax.all_to_all(packed, ('section', 'qq'), split_axis=0, concat_axis=0, ti...  7.93 us
  transfers between devices with their start and end apart: 2, of which 2 were waited for; matrix products, arithmetic and copies ran while one was open for 1% of the time, Pallas kernels for 0%

profile of v10, /device:TPU:1, one launch (start us, length us, event | category | flops | bytes accessed | tf_op | source)
XLA Modules:
  0.0 144.2 jit_solution(13591008900239210747)
XLA Ops:
  7.3 0.9 slice_bitcast_fusion.1
  8.1 1.0 convert_multiply_fusion.1
  9.9 0.8 pad_maximum_fusion.1
  11.2 0.2 copy.80
  11.4 0.2 fusion.1
  11.8 22.1 %all_gather.9.q_ref = bf16[4,132,768]{2,1,0:T(8,128)(2,1)S(1)} all-gather(bf16[1,132,768]{2,1,0:T(8,128)(2,1)S(1)} %copy.81), channel_id=1, replica_groups=mesh['section'=4,'kk'=16,'qq'=4] {'qq'}, dimensions={0}, use_global_device_ids=true | all-gather | bytes 1013760 | tf_op jit(solution)/shard_map/all_gather | solution.py:115
  34.0 11.1 %all_gather.11 = s32[6,4,64]{2,0,1:T(8,128)S(1)} all-gather(s32[6,1,64]{2,0,1:T(8,128)S(1)} %copy.84), channel_id=1, replica_groups=mesh['section'=4,'kk'=16,'qq'=4] {'qq'}, dimensions={1}, use_global_device_ids=true | all-gather | bytes 7680 | tf_op jit(solution)/shard_map/all_gather | solution.py:117
  45.2 0.6 dynamic-slice_reduce_fusion
  46.0 36.5 %all-gather.2.cloned.1.call-done.ki_ref.vi_ref = bf16[2,16,132,768]{3,2,1,0:T(8,128)(2,1)} async-done(((bf16[2,1,132,768]{3,2,1,0:T(8,128)(2,1)}), bf16[2,16,132,768]{3,2,1,0:T(8,128)(2,1)}) %all-gather.2.cloned.1.call-update) | async-done | bytes 6488080 | tf_op jit(solution)/shard_map/all_gather | solution.py:116
  82.5 1.1 fusion.12
  83.7 12.9 %shard_map.95 = (f32[4,132,768]{2,1,0:T(8,128)S(1)}, f32[4,132,128]{2,1,0:T(8,128)S(1)}) custom-call(bf16[4,132,768]{2,1,0:T(8,128)(2,1)S(1)} %all_gather.9.q_ref, bf16[16,768]{1,0:T(8,128)(2,1)S(1)} %reshape.144.qt_ref, bf16[2,16,132,768]{3,2,1,0:T(8,128)(2,1)} %all-gather.2.cloned.1.call-done.ki_ref.vi_ref, bf16[64,768]{1,0:T(8,128)(2,1)S(1)} %reshape_squeeze.6.kt_ref, ...), custom_call_target="tpu_custom_call" | custom-call | tf_op jit(solution)/shard_map/pallas_call | solution.py:72
  97.7 0.2 reshape.147
  98.3 0.3 concatenate.29
  98.6 1.0 copy.98
  99.6 7.9 %all-to-all-start = ((bf16[16,224,128]{2,1,0:T(8,128)(2,1)}), bf16[16,224,128]{2,1,0:T(8,128)(2,1)S(1)}, u32[]{:S(2)}, u32[]{:S(2)}) async-start(bf16[16,224,128]{2,1,0:T(8,128)(2,1)} %bitcast.32), calls=%async_computation | async-start | bytes 1835008 | tf_op jit(solution)/shard_map/all_to_all | solution.py:149
  107.6 25.2 %all-to-all-done = bf16[16,224,128]{2,1,0:T(8,128)(2,1)S(1)} async-done(((bf16[16,224,128]{2,1,0:T(8,128)(2,1)}), bf16[16,224,128]{2,1,0:T(8,128)(2,1)S(1)}, u32[]{:S(2)}, u32[]{:S(2)}) %all-to-all-start) | async-done | bytes 917536 | tf_op jit(solution)/shard_map/all_to_all | solution.py:149
  132.8 0.3 reshape.152
  133.1 1.2 convert_reduce_fusion
  134.4 0.3 reshape.153
  134.7 0.2 reshape.154
  135.2 0.2 divide_convert_fusion
  135.5 0.2 reshape.155
  136.0 0.8 reshape.156
  136.8 0.6 copy.109
  (79 shorter events, 3.8 us)
Async XLA Ops:
  7.2 2.6 %copy-start = (bf16[128,768]{1,0:T(8,128)(2,1)S(1)}, bf16[128,768]{1,0:T(8,128)(2,1)}, u32[]{:S(2)}) copy-start(bf16[128,768]{1,0:T(8,128)(2,1)} %param.9) | copy-start | bytes 589828
  7.2 2.3 %copy-start.3 = (bf16[4,768]{1,0:T(4,128)(2,1)S(1)}, bf16[4,768]{1,0:T(4,128)(2,1)}, u32[]{:S(2)}) copy-start(bf16[4,768]{1,0:T(4,128)(2,1)} %param.12) | copy-start | bytes 18436
  7.2 2.6 %copy-start.1 = (bf16[128,768]{1,0:T(8,128)(2,1)S(1)}, bf16[128,768]{1,0:T(8,128)(2,1)}, u32[]{:S(2)}) copy-start(bf16[128,768]{1,0:T(8,128)(2,1)} %param.10) | copy-start | bytes 589828
  7.2 2.6 %copy-start.5 = (bf16[4,768]{1,0:T(4,128)(2,1)S(1)}, bf16[4,768]{1,0:T(4,128)(2,1)}, u32[]{:S(2)}) copy-start(bf16[4,768]{1,0:T(4,128)(2,1)} %param.13) | copy-start | bytes 18436
  7.2 75.3 %all-gather.2.cloned.1.call-start = ((), (), s32[]{:S(2)}) async-start(), calls=%async_computation.1 | async-start | bytes 7102464 | tf_op jit(solution)/shard_map/all_gather | solution.py:116
  9.3 1.4 copy-start.2
  9.5 1.4 copy-start.4
  10.9 23.0 %copy-start.6 = (s32[6,1,64]{2,1,0:T(1,128)S(1)}, s32[6,1,64]{2,1,0:T(1,128)}, u32[]{:S(2)}) copy-start(s32[6,1,64]{2,1,0:T(1,128)} %param.15) | copy-start | bytes 4612
  99.6 33.1 %all-to-all-start = ((bf16[16,224,128]{2,1,0:T(8,128)(2,1)}), bf16[16,224,128]{2,1,0:T(8,128)(2,1)S(1)}, u32[]{:S(2)}, u32[]{:S(2)}) async-start(bf16[16,224,128]{2,1,0:T(8,128)(2,1)} %bitcast.32), calls=%async_computation | async-start | bytes 1835008 | tf_op jit(solution)/shard_map/all_to_all | solution.py:149
Sparse Core Ops, SparseCore 0:
  10.8 71.6 all-gather.1

commit v11 on v9

--- a/solution.py
+++ b/solution.py
@@ -23,9 +23,9 @@
     q_blocks = q_ref.shape[0]
     text_rows = qt_ref.shape[0] // q_blocks
     dims = (((1,), (1,)), ((), ()))
-    keys_img = ki_ref[0].reshape(-1, head_size)
+    keys_img = ki_ref[...].reshape(-1, head_size)
     keys_txt = kt_ref[...]
-    vals_img = vi_ref[0].reshape(-1, head_size)
+    vals_img = vi_ref[...].reshape(-1, head_size)
     vals_txt = vt_ref[...]
 
     @pl.when(head == 0)
@@ -60,7 +60,7 @@
 
 def attend(all_q, qt, kv, kt, vt, fl, heads, head_size):
     groups_q, stride = all_q.shape[0], all_q.shape[1]
-    groups_k = kv.shape[1]
+    groups_k = kv.shape[0]
     n_qt, n_kt = qt.shape[0], kt.shape[0]
     width = heads * head_size
 
@@ -73,9 +73,9 @@
         in_specs=[
             pl.BlockSpec((groups_q, stride, head_size), lambda h: (0, 0, h)),
             cols(n_qt),
-            pl.BlockSpec((1, groups_k, BLOCK, head_size), lambda h: (0, 0, 0, h)),
+            pl.BlockSpec((groups_k, BLOCK, head_size), lambda h: (0, 0, h)),
             cols(n_kt),
-            pl.BlockSpec((1, groups_k, BLOCK, head_size), lambda h: (1, 0, 0, h)),
+            pl.BlockSpec((groups_k, BLOCK, head_size), lambda h: (0, 1, h)),
             cols(n_kt),
             pl.BlockSpec((1,) + fl.shape[1:], lambda h: (h, 0, 0)),
         ],
@@ -104,22 +104,20 @@
     queries = jnp.concatenate(
         [normed(q_img, norm_gains[0], heads), normed(q_txt, norm_gains[2], heads)], axis=0
     ).reshape(1, stride, width)
-    keys = jnp.concatenate(
-        [normed(k_img, norm_gains[1], heads), normed(k_txt, norm_gains[3], heads)], axis=0
-    ).reshape(1, stride, width)
-    values = jnp.concatenate([v_img, v_txt], axis=0).reshape(1, stride, width)
-    pair = jnp.stack([keys, values], axis=0)
+    keys_image = normed(k_img, norm_gains[1], heads).reshape(rows, width)
+    keys_text = normed(k_txt, norm_gains[3], heads).reshape(text_rows, width)
+    pair = jnp.concatenate([keys_image, v_img, keys_text, v_txt], axis=0)[None]
 
     all_q = lax.all_gather(queries, "qq", axis=0, tiled=True)
-    all_kv = lax.all_gather(pair, "kk", axis=1, tiled=True)
+    all_kv = lax.all_gather(pair, "kk", axis=0, tiled=True)
     flags = lax.all_gather(block_map, "qq", axis=1, tiled=True)
     flags = flags.reshape(heads, groups_q, groups_k, groups_q)
     flags = lax.dynamic_index_in_dim(flags, own_q, axis=3, keepdims=False)
     flags = jnp.repeat(flags, BLOCK, axis=2)
 
     qt = all_q[:, rows:].reshape(groups_q * text_rows, width)
-    kt = all_kv[0, :, rows:].reshape(groups_k * text_rows, width)
-    vt = all_kv[1, :, rows:].reshape(groups_k * text_rows, width)
+    kt = all_kv[:, 2 * rows:2 * rows + text_rows].reshape(groups_k * text_rows, width)
+    vt = all_kv[:, 2 * rows + text_rows:].reshape(groups_k * text_rows, width)
 
     numer, denom = attend(all_q, qt, all_kv, kt, vt, flags, heads, head_size)
     denom = denom[:, :, :heads]

time: 145 us -> 146 us (level)
  local copies, waits for them, and re-layouts: 9.52 us -> 11.8 us
    unnamed x22 -> x21, local copies, waits for them, and re-layouts: 2.15 us -> 3.56 us
where the time goes in v11:
time: 146 us
  waiting for transfers between devices  60.8 us (42%)
  blocking collectives  33.3 us (23%)
  between operations  14.5 us (10%)
  Pallas kernels  13.4 us (9%)
  local copies, waits for them, and re-layouts  11.8 us (8%)
  starting transfers between devices  7.92 us (5%)
  other arithmetic  4.25 us (3%)
    all_gather x1, waiting for transfers between devices, body(): all_kv = lax.all_gather(pair, 'kk', axis=0, tiled=True)  35.6 us
    all_to_all x1, waiting for transfers between devices, body(): lax.all_to_all(packed, ('section', 'qq'), split_axis=0, concat_axis=0, ti...  25.2 us
    all_gather x1, blocking collectives, body(): all_q = lax.all_gather(queries, 'qq', axis=0, tiled=True)  22.1 us
    pallas_call x1, Pallas kernels, attend(): pl.pallas_call(attend_kernel, grid=(heads,), in_specs=[pl.BlockSpec((grou...  13.4 us
    all_gather x1, blocking collectives, body(): flags = lax.all_gather(block_map, 'qq', axis=1, tiled=True)  11.1 us
    all_to_all x1, starting transfers between devices, body(): lax.all_to_all(packed, ('section', 'qq'), split_axis=0, concat_axis=0, ti...  7.89 us
    unnamed x21, local copies, waits for them, and re-layouts  3.56 us
  transfers between devices with their start and end apart: 2, of which 2 were waited for; matrix products, arithmetic and copies ran while one was open for 1% of the time, Pallas kernels for 0%

profile of v11, /device:TPU:1, one launch (start us, length us, event | category | flops | bytes accessed | tf_op | source)
XLA Modules:
  0.0 145.9 jit_solution(9448445780072887819)
XLA Ops:
  7.2 0.8 slice_bitcast_fusion.1
  8.1 1.1 copy.107
  9.2 0.7 convert_multiply_fusion.5
  10.1 0.7 fusion.7
  11.7 1.0 copy.111
  13.3 0.2 copy.105
  13.9 22.1 %all_gather.9.q_ref = bf16[4,132,768]{2,1,0:T(8,128)(2,1)S(1)} all-gather(bf16[1,132,768]{2,1,0:T(8,128)(2,1)S(1)} %copy.106), channel_id=1, replica_groups=mesh['section'=4,'kk'=16,'qq'=4] {'qq'}, dimensions={0}, use_global_device_ids=true | all-gather | bytes 1013760 | tf_op jit(solution)/shard_map/all_gather | solution.py:111
  36.0 11.1 %all_gather.11 = s32[6,4,64]{2,0,1:T(8,128)S(1)} all-gather(s32[6,1,64]{2,0,1:T(8,128)S(1)} %copy.112), channel_id=1, replica_groups=mesh['section'=4,'kk'=16,'qq'=4] {'qq'}, dimensions={1}, use_global_device_ids=true | all-gather | bytes 7680 | tf_op jit(solution)/shard_map/all_gather | solution.py:113
  47.3 0.6 dynamic-slice_reduce_fusion
  48.1 35.6 %all-gather.3.cloned.1.call-done = bf16[4224,768]{1,0:T(8,128)(2,1)} async-done(((bf16[264,768]{1,0:T(8,128)(2,1)}), bf16[4224,768]{1,0:T(8,128)(2,1)}) %all-gather.3.cloned.1.call-update) | async-done | bytes 6488080 | tf_op jit(solution)/shard_map/all_gather | solution.py:112
  83.7 1.1 fusion.10
  84.9 13.4 %shard_map.95 = (f32[4,132,768]{2,1,0:T(8,128)S(1)}, f32[4,132,128]{2,1,0:T(8,128)S(1)}) custom-call(bf16[4,132,768]{2,1,0:T(8,128)(2,1)S(1)} %all_gather.9.q_ref, bf16[16,768]{1,0:T(8,128)(2,1)S(1)} %reshape.136.qt_ref, bf16[16,264,768]{2,1,0:T(8,128)(2,1)} %bitcast.58, bf16[64,768]{1,0:T(8,128)(2,1)S(1)} %reshape.137.kt_ref, ...), custom_call_target="tpu_custom_call" | custom-call | tf_op jit(solution)/shard_map/pallas_call | solution.py:70
  100.1 0.3 concatenate.24
  100.3 1.0 copy.126
  101.4 7.9 %all-to-all-start = ((bf16[16,224,128]{2,1,0:T(8,128)(2,1)}), bf16[16,224,128]{2,1,0:T(8,128)(2,1)S(1)}, u32[]{:S(2)}, u32[]{:S(2)}) async-start(bf16[16,224,128]{2,1,0:T(8,128)(2,1)} %bitcast.30), calls=%async_computation | async-start | bytes 1835008 | tf_op jit(solution)/shard_map/all_to_all | solution.py:145
  109.2 25.2 %all-to-all-done = bf16[16,224,128]{2,1,0:T(8,128)(2,1)S(1)} async-done(((bf16[16,224,128]{2,1,0:T(8,128)(2,1)}), bf16[16,224,128]{2,1,0:T(8,128)(2,1)S(1)}, u32[]{:S(2)}, u32[]{:S(2)}) %all-to-all-start) | async-done | bytes 917536 | tf_op jit(solution)/shard_map/all_to_all | solution.py:145
  134.5 0.3 reshape.146
  134.8 1.2 convert_reduce_fusion
  136.0 0.3 reshape.147
  136.4 0.2 reshape.148
  136.9 0.2 divide_convert_fusion
  137.2 0.2 reshape.149
  137.6 0.8 reshape.150
  138.4 0.6 copy.135
  (76 shorter events, 4.6 us)
Async XLA Ops:
  7.2 3.9 %copy-start = (bf16[128,768]{1,0:T(8,128)(2,1)S(1)}, bf16[128,768]{1,0:T(8,128)(2,1)}, u32[]{:S(2)}) copy-start(bf16[128,768]{1,0:T(8,128)(2,1)} %param.10) | copy-start | bytes 589828
  7.2 4.0 %copy-start.3 = (bf16[4,768]{1,0:T(4,128)(2,1)S(1)}, bf16[4,768]{1,0:T(4,128)(2,1)}, u32[]{:S(2)}) copy-start(bf16[4,768]{1,0:T(4,128)(2,1)} %param.13) | copy-start | bytes 18436
  7.2 76.5 %all-gather.3.cloned.1.call-start = ((), (), s32[]{:S(2)}) async-start(), calls=%async_computation.1 | async-start | bytes 6893568 | tf_op jit(solution)/shard_map/all_gather | solution.py:112
  11.2 1.6 %copy-start.1 = (bf16[128,768]{1,0:T(8,128)(2,1)S(1)}, bf16[128,768]{1,0:T(8,128)(2,1)}, u32[]{:S(2)}) copy-start(bf16[128,768]{1,0:T(8,128)(2,1)} %param.8) | copy-start | bytes 589828
  11.7 1.3 copy-start.2
  13.0 23.0 %copy-start.4 = (s32[6,1,64]{2,1,0:T(1,128)S(1)}, s32[6,1,64]{2,1,0:T(1,128)}, u32[]{:S(2)}) copy-start(s32[6,1,64]{2,1,0:T(1,128)} %param.15) | copy-start | bytes 4612
  101.4 33.1 %all-to-all-start = ((bf16[16,224,128]{2,1,0:T(8,128)(2,1)}), bf16[16,224,128]{2,1,0:T(8,128)(2,1)S(1)}, u32[]{:S(2)}, u32[]{:S(2)}) async-start(bf16[16,224,128]{2,1,0:T(8,128)(2,1)} %bitcast.30), calls=%async_computation | async-start | bytes 1835008 | tf_op jit(solution)/shard_map/all_to_all | solution.py:145
Sparse Core Ops, SparseCore 0:
  12.9 70.7 all-gather.2

commit v12 on v9

--- a/solution.py
+++ b/solution.py
@@ -111,7 +111,8 @@
     pair = jnp.stack([keys, values], axis=0)
 
     all_q = lax.all_gather(queries, "qq", axis=0, tiled=True)
-    all_kv = lax.all_gather(pair, "kk", axis=1, tiled=True)
+    spread = jnp.broadcast_to(pair, (2, groups_k) + pair.shape[2:])
+    all_kv = lax.all_to_all(spread, "kk", split_axis=1, concat_axis=1, tiled=True)
     flags = lax.all_gather(block_map, "qq", axis=1, tiled=True)
     flags = flags.reshape(heads, groups_q, groups_k, groups_q)
     flags = lax.dynamic_index_in_dim(flags, own_q, axis=3, keepdims=False)

time: 145 us -> 180 us (1.24)
  waiting for transfers between devices: 61.7 us -> 85.5 us
  local copies, waits for them, and re-layouts: 9.52 us -> 24 us
  between operations: 14.5 us -> 1.08 us
  starting transfers between devices: 7.92 us -> 18 us
    all_to_all x0 -> x1, waiting for transfers between devices: none -> 60.3 us  [body(): lax.all_to_all(spread, 'kk', split_axis=1, concat_axis=1, tiled=True)]
    all_gather x1 -> x0, waiting for transfers between devices: 36.5 us -> none  [body(): all_kv = lax.all_gather(pair, 'kk', axis=1, tiled=True)]
    all_to_all x0 -> x1, starting transfers between devices: none -> 7.75 us  [body(): lax.all_to_all(spread, 'kk', split_axis=1, concat_axis=1, tiled=True)]
    all_to_all x0 -> x1, local copies, waits for them, and re-layouts: none -> 6.48 us  [body(): lax.all_to_all(spread, 'kk', split_axis=1, concat_axis=1, tiled=True)]
    broadcast_in_dim x0 -> x2, local copies, waits for them, and re-layouts: none -> 4.93 us  [body(): spread = jnp.broadcast_to(pair, (2, groups_k) + pair.shape[2:])]
    all_to_all x1, starting transfers between devices: 7.88 us -> 10.3 us  [body(): lax.all_to_all(packed, ('section', 'qq'), split_axis=0, concat_axis=0, ti...]
    unnamed x22 -> x19, local copies, waits for them, and re-layouts: 2.15 us -> 4.48 us
where the time goes in v12:
time: 180 us; the launch traced here: 179 us
  waiting for transfers between devices  85.5 us (48%)
  blocking collectives  33 us (18%)
  local copies, waits for them, and re-layouts  24 us (13%)
  starting transfers between devices  18 us (10%)
  Pallas kernels  13.4 us (7%)
  other arithmetic  4.33 us (2%)
    all_to_all x1, waiting for transfers between devices, body(): lax.all_to_all(spread, 'kk', split_axis=1, concat_axis=1, tiled=True)  60.3 us
    all_to_all x1, waiting for transfers between devices, body(): lax.all_to_all(packed, ('section', 'qq'), split_axis=0, concat_axis=0, ti...  25.2 us
    all_gather x1, blocking collectives, body(): all_q = lax.all_gather(queries, 'qq', axis=0, tiled=True)  20.4 us
    pallas_call x1, Pallas kernels, attend(): pl.pallas_call(attend_kernel, grid=(heads,), in_specs=[pl.BlockSpec((grou...  13.4 us
    all_gather x1, blocking collectives, body(): flags = lax.all_gather(block_map, 'qq', axis=1, tiled=True)  12.6 us
    all_to_all x1, starting transfers between devices, body(): lax.all_to_all(packed, ('section', 'qq'), split_axis=0, concat_axis=0, ti...  10.3 us
    all_to_all x1, starting transfers between devices, body(): lax.all_to_all(spread, 'kk', split_axis=1, concat_axis=1, tiled=True)  7.75 us
    all_to_all x1, local copies, waits for them, and re-layouts, body(): lax.all_to_all(spread, 'kk', split_axis=1, concat_axis=1, tiled=True)  6.48 us
  transfers between devices with their start and end apart: 2, of which 2 were waited for; matrix products, arithmetic and copies ran while one was open for 1% of the time, Pallas kernels for 0%

profile of v12, /device:TPU:1, one launch (start us, length us, event | category | flops | bytes accessed | tf_op | source)
XLA Modules:
  0.0 179.2 jit_solution(5725570001404916609)
XLA Ops:
  0.6 0.8 slice_bitcast_fusion.1
  1.5 1.1 copy.113
  2.7 0.7 convert_multiply_fusion.5
  3.5 0.7 fusion.9
  4.4 1.1 copy.115
  6.1 0.6 copy.117
  6.7 4.4 %broadcast_in_dim.13 = bf16[2,16,132,768]{3,0,2,1:T(2,128)(2,1)} broadcast(bf16[2,132,768]{2,0,1:T(2,128)(2,1)S(1)} %copy.117), dimensions={0,2,3} | broadcast | bytes 6893568 | tf_op jit(solution)/shard_map/broadcast_in_dim | solution.py:114
  11.1 7.7 %all-to-all-start = ((bf16[2,16,132,768]{3,0,2,1:T(2,128)(2,1)}), bf16[2,16,132,768]{3,0,2,1:T(2,128)(2,1)}, u32[]{:S(2)}, u32[]{:S(2)}) async-start(bf16[2,16,132,768]{3,0,2,1:T(2,128)(2,1)} %broadcast_in_dim.13), calls=%async_computation | async-start | bytes 12976128 | tf_op jit(solution)/shard_map/all_to_all | solution.py:115
  19.9 20.4 %all_gather.6.q_ref = bf16[4,132,768]{2,1,0:T(8,128)(2,1)S(1)} all-gather(bf16[1,132,768]{2,1,0:T(8,128)(2,1)S(1)} %copy.112), channel_id=1, replica_groups=mesh['section'=4,'kk'=16,'qq'=4] {'qq'}, dimensions={0}, use_global_device_ids=true | all-gather | bytes 1013760 | tf_op jit(solution)/shard_map/all_gather | solution.py:113
  40.4 12.6 %all_gather.7 = s32[6,4,64]{2,0,1:T(8,128)S(1)} all-gather(s32[6,1,64]{2,0,1:T(8,128)S(1)} %copy.118), channel_id=1, replica_groups=mesh['section'=4,'kk'=16,'qq'=4] {'qq'}, dimensions={1}, use_global_device_ids=true | all-gather | bytes 7680 | tf_op jit(solution)/shard_map/all_gather | solution.py:116
  53.1 0.6 dynamic-slice_reduce_fusion
  53.9 60.3 %all-to-all-done = bf16[2,16,132,768]{3,0,2,1:T(2,128)(2,1)} async-done(((bf16[2,16,132,768]{3,0,2,1:T(2,128)(2,1)}), bf16[2,16,132,768]{3,0,2,1:T(2,128)(2,1)}, u32[]{:S(2)}, u32[]{:S(2)}) %all-to-all-start) | async-done | bytes 6488096 | tf_op jit(solution)/shard_map/all_to_all | solution.py:115
  114.2 2.0 %slice_reduce_fusion = (bf16[16,4,768]{2,1,0:T(4,128)(2,1)S(1)}, bf16[16,4,768]{2,1,0:T(4,128)(2,1)S(1)}) fusion(bf16[2,16,132,768]{3,0,2,1:T(2,128)(2,1)} %all-to-all-done), kind=kLoop, calls=%fused_computation.17 | loop fusion | bytes 393216 | tf_op jit(solution)/shard_map/slice | solution.py:123
  116.2 6.5 %copy.120.ki_ref.vi_ref = bf16[2,16,132,768]{3,2,1,0:T(8,128)(2,1)} copy(bf16[2,16,132,768]{3,0,2,1:T(2,128)(2,1)} %all-to-all-done) | data formatting | bytes 12976128 | tf_op jit(solution)/shard_map/all_to_all | solution.py:115
  122.7 13.4 %shard_map.95 = (f32[4,132,768]{2,1,0:T(8,128)S(1)}, f32[4,132,128]{2,1,0:T(8,128)S(1)}) custom-call(bf16[4,132,768]{2,1,0:T(8,128)(2,1)S(1)} %all_gather.6.q_ref, bf16[16,768]{1,0:T(8,128)(2,1)S(1)} %reshape.144.qt_ref, bf16[2,16,132,768]{3,2,1,0:T(8,128)(2,1)} %copy.120.ki_ref.vi_ref, bf16[64,768]{1,0:T(8,128)(2,1)S(1)} %reshape_squeeze.6.kt_ref, ...), custom_call_target="tpu_custom_call" | custom-call | tf_op jit(solution)/shard_map/pallas_call | solution.py:70
  137.9 0.3 concatenate.29
  138.1 1.0 copy.136
  139.2 10.3 %all-to-all-start.1 = ((bf16[16,224,128]{2,1,0:T(8,128)(2,1)}), bf16[16,224,128]{2,1,0:T(8,128)(2,1)S(1)}, u32[]{:S(2)}, u32[]{:S(2)}) async-start(bf16[16,224,128]{2,1,0:T(8,128)(2,1)} %bitcast.33), calls=%async_computation.1 | async-start | bytes 1835008 | tf_op jit(solution)/shard_map/all_to_all | solution.py:148
  149.4 25.2 %all-to-all-done.1 = bf16[16,224,128]{2,1,0:T(8,128)(2,1)S(1)} async-done(((bf16[16,224,128]{2,1,0:T(8,128)(2,1)}), bf16[16,224,128]{2,1,0:T(8,128)(2,1)S(1)}, u32[]{:S(2)}, u32[]{:S(2)}) %all-to-all-start.1) | async-done | bytes 917536 | tf_op jit(solution)/shard_map/all_to_all | solution.py:148
  174.6 0.3 reshape.152
  174.9 1.2 convert_reduce_fusion
  176.2 0.3 reshape.153
  177.8 0.8 reshape.156
  178.6 0.6 copy.147
  (76 shorter events, 5.3 us)
Async XLA Ops:
  0.6 4.9 %copy-start.2 = (bf16[4,768]{1,0:T(4,128)(2,1)S(1)}, bf16[4,768]{1,0:T(4,128)(2,1)}, u32[]{:S(2)}) copy-start(bf16[4,768]{1,0:T(4,128)(2,1)} %param.13) | copy-start | bytes 18436
  11.1 7.8 %copy-start = (bf16[128,768]{1,0:T(8,128)(2,1)S(1)}, bf16[128,768]{1,0:T(8,128)(2,1)}, u32[]{:S(2)}) copy-start(bf16[128,768]{1,0:T(8,128)(2,1)} %param.8) | copy-start | bytes 589828
  11.1 8.0 %copy-start.1 = (bf16[4,768]{1,0:T(4,128)(2,1)S(1)}, bf16[4,768]{1,0:T(4,128)(2,1)}, u32[]{:S(2)}) copy-start(bf16[4,768]{1,0:T(4,128)(2,1)} %param.11) | copy-start | bytes 18436
  11.1 103.2 %all-to-all-start = ((bf16[2,16,132,768]{3,0,2,1:T(2,128)(2,1)}), bf16[2,16,132,768]{3,0,2,1:T(2,128)(2,1)}, u32[]{:S(2)}, u32[]{:S(2)}) async-start(bf16[2,16,132,768]{3,0,2,1:T(2,128)(2,1)} %broadcast_in_dim.13), calls=%async_computation | async-start | bytes 12976128 | tf_op jit(solution)/shard_map/all_to_all | solution.py:115
  19.0 21.3 %copy-start.3 = (s32[6,1,64]{2,1,0:T(1,128)S(1)}, s32[6,1,64]{2,1,0:T(1,128)}, u32[]{:S(2)}) copy-start(s32[6,1,64]{2,1,0:T(1,128)} %param.15) | copy-start | bytes 4612
  139.2 35.5 %all-to-all-start.1 = ((bf16[16,224,128]{2,1,0:T(8,128)(2,1)}), bf16[16,224,128]{2,1,0:T(8,128)(2,1)S(1)}, u32[]{:S(2)}, u32[]{:S(2)}) async-start(bf16[16,224,128]{2,1,0:T(8,128)(2,1)} %bitcast.33), calls=%async_computation.1 | async-start | bytes 1835008 | tf_op jit(solution)/shard_map/all_to_all | solution.py:148

commit v13 on v9

--- a/solution.py
+++ b/solution.py
@@ -16,33 +16,24 @@
     return (floats * lax.rsqrt(power + 1e-06) * gain).astype(jnp.bfloat16)
 
 
-def attend_kernel(q_ref, qt_ref, ki_ref, kt_ref, vi_ref, vt_ref, fl_ref, num_ref, den_ref):
+def attend_kernel(fl_ref, q_ref, qt_ref, ki_ref, kt_ref, vi_ref, vt_ref, num_ref, den_ref):
     head = pl.program_id(0)
     head_size = q_ref.shape[-1]
     scale = head_size ** (-0.5)
     q_blocks = q_ref.shape[0]
+    k_blocks = ki_ref.shape[1]
     text_rows = qt_ref.shape[0] // q_blocks
     dims = (((1,), (1,)), ((), ()))
-    keys_img = ki_ref[0].reshape(-1, head_size)
     keys_txt = kt_ref[...]
-    vals_img = vi_ref[0].reshape(-1, head_size)
     vals_txt = vt_ref[...]
 
     @pl.when(head == 0)
     def _():
         den_ref[...] = jnp.zeros(den_ref.shape, den_ref.dtype)
 
-    def one(q, flags):
-        s_img = lax.dot_general(q, keys_img, dims, preferred_element_type=jnp.float32) * scale
-        s_txt = lax.dot_general(q, keys_txt, dims, preferred_element_type=jnp.float32) * scale
-        e_img = jnp.exp(s_img)
-        if flags is not None:
-            e_img = jnp.where(flags > 0, e_img, jnp.float32(0.0))
-        e_txt = jnp.exp(s_txt)
-        den = jnp.sum(e_img, axis=1, keepdims=True) + jnp.sum(e_txt, axis=1, keepdims=True)
-        num = jnp.dot(e_img.astype(jnp.bfloat16), vals_img, preferred_element_type=jnp.float32)
-        num = num + jnp.dot(e_txt.astype(jnp.bfloat16), vals_txt, preferred_element_type=jnp.float32)
-        return num, den
+    def weigh(q, keys):
+        s = lax.dot_general(q, keys, dims, preferred_element_type=jnp.float32) * scale
+        return jnp.exp(s)
 
     def put(a, lo, hi, num, den):
         num_ref[a, lo:hi, :] = num
@@ -50,9 +41,34 @@
         den_ref[a, lo:hi, :] = jnp.where(lane == head, den, den_ref[a, lo:hi, :])
 
     for a in range(q_blocks):
-        num, den = one(q_ref[a, 0:BLOCK, :], fl_ref[0, a:a + 1, :])
+        q = q_ref[a, 0:BLOCK, :]
+        e_txt = weigh(q, keys_txt)
+        start = (
+            jnp.dot(e_txt.astype(jnp.bfloat16), vals_txt, preferred_element_type=jnp.float32),
+            jnp.sum(e_txt, axis=1, keepdims=True),
+        )
+
+        def step(b, carry):
+            def take(carry):
+                num, den = carry
+                e = weigh(q, ki_ref[0, b])
+                num = num + jnp.dot(e.astype(jnp.bfloat16), vi_ref[0, b], preferred_element_type=jnp.float32)
+                return num, den + jnp.sum(e, axis=1, keepdims=True)
+
+            flag = fl_ref[(head * q_blocks + a) * k_blocks + b]
+            return lax.cond(flag > 0, take, lambda c: c, carry)
+
+        num, den = lax.fori_loop(0, k_blocks, step, start)
         put(a, 0, BLOCK, num, den)
-    num, den = one(qt_ref[...], None)
+
+    keys_img = ki_ref[0].reshape(-1, head_size)
+    vals_img = vi_ref[0].reshape(-1, head_size)
+    qt = qt_ref[...]
+    e_img = weigh(qt, keys_img)
+    e_txt = weigh(qt, keys_txt)
+    den = jnp.sum(e_img, axis=1, keepdims=True) + jnp.sum(e_txt, axis=1, keepdims=True)
+    num = jnp.dot(e_img.astype(jnp.bfloat16), vals_img, preferred_element_type=jnp.float32)
+    num = num + jnp.dot(e_txt.astype(jnp.bfloat16), vals_txt, preferred_element_type=jnp.float32)
     for a in range(q_blocks):
         part = slice(a * text_rows, (a + 1) * text_rows)
         put(a, BLOCK, BLOCK + text_rows, num[part], den[part])
@@ -65,30 +81,33 @@
     width = heads * head_size
 
     def cols(rows):
-        return pl.BlockSpec((rows, head_size), lambda h: (0, h))
-
+        return pl.BlockSpec((rows, head_size), lambda h, f: (0, h))
+
+    grid_spec = pltpu.PrefetchScalarGridSpec(
+        num_scalar_prefetch=1,
+        grid=(heads,),
+        in_specs=[
+            pl.BlockSpec((groups_q, stride, head_size), lambda h, f: (0, 0, h)),
+            cols(n_qt),
+            pl.BlockSpec((1, groups_k, BLOCK, head_size), lambda h, f: (0, 0, 0, h)),
+            cols(n_kt),
+            pl.BlockSpec((1, groups_k, BLOCK, head_size), lambda h, f: (1, 0, 0, h)),
+            cols(n_kt),
+        ],
+        out_specs=[
+            pl.BlockSpec((groups_q, stride, head_size), lambda h, f: (0, 0, h)),
+            pl.BlockSpec((groups_q, stride, BLOCK), lambda h, f: (0, 0, 0)),
+        ],
+    )
     return pl.pallas_call(
         attend_kernel,
-        grid=(heads,),
-        in_specs=[
-            pl.BlockSpec((groups_q, stride, head_size), lambda h: (0, 0, h)),
-            cols(n_qt),
-            pl.BlockSpec((1, groups_k, BLOCK, head_size), lambda h: (0, 0, 0, h)),
-            cols(n_kt),
-            pl.BlockSpec((1, groups_k, BLOCK, head_size), lambda h: (1, 0, 0, h)),
-            cols(n_kt),
-            pl.BlockSpec((1,) + fl.shape[1:], lambda h: (h, 0, 0)),
-        ],
-        out_specs=[
-            pl.BlockSpec((groups_q, stride, head_size), lambda h: (0, 0, h)),
-            pl.BlockSpec((groups_q, stride, BLOCK), lambda h: (0, 0, 0)),
-        ],
+        grid_spec=grid_spec,
         out_shape=[
             jax.ShapeDtypeStruct((groups_q, stride, width), jnp.float32),
             jax.ShapeDtypeStruct((groups_q, stride, BLOCK), jnp.float32),
         ],
         compiler_params=pltpu.CompilerParams(vmem_limit_bytes=48 * 1024 * 1024),
-    )(all_q, qt, kv, kt, kv, vt, fl)
+    )(fl.reshape(-1), all_q, qt, kv, kt, kv, vt)
 
 
 def body(q_img, k_img, v_img, q_txt, k_txt, v_txt, norm_gains, block_map):
@@ -115,7 +134,7 @@
     flags = lax.all_gather(block_map, "qq", axis=1, tiled=True)
     flags = flags.reshape(heads, groups_q, groups_k, groups_q)
     flags = lax.dynamic_index_in_dim(flags, own_q, axis=3, keepdims=False)
-    flags = jnp.repeat(flags, BLOCK, axis=2)
+    flags = (flags > 0).astype(jnp.int32)
 
     qt = all_q[:, rows:].reshape(groups_q * text_rows, width)
     kt = all_kv[0, :, rows:].reshape(groups_k * text_rows, width)

time: 145 us -> 211 us (1.46); the launches traced: 145 us -> 208 us
  Pallas kernels: 13.4 us -> 69.2 us
  starting transfers between devices: 7.92 us -> 15.4 us
    pallas_call x1, Pallas kernels: 13.4 us -> 69.2 us  [attend(): pl.pallas_call(attend_kernel, grid_spec=grid_spec, out_shape=[jax.ShapeDt...]
    all_to_all x1, starting transfers between devices: 7.88 us -> 15.3 us  [body(): lax.all_to_all(packed, ('section', 'qq'), split_axis=0, concat_axis=0, ti...]
where the time goes in v13:
time: 211 us; the launch traced here: 208 us
  Pallas kernels  69.2 us (33%)
  waiting for transfers between devices  61.8 us (29%)
  blocking collectives  33.3 us (16%)
  starting transfers between devices  15.4 us (7%)
  between operations  14.5 us (7%)
  local copies, waits for them, and re-layouts  8.83 us (4%)
  other arithmetic  4.94 us (2%)
    pallas_call x1, Pallas kernels, attend(): pl.pallas_call(attend_kernel, grid_spec=grid_spec, out_shape=[jax.ShapeDt...  69.2 us
    all_gather x1, waiting for transfers between devices, body(): all_kv = lax.all_gather(pair, 'kk', axis=1, tiled=True)  36.6 us
    all_to_all x1, waiting for transfers between devices, body(): lax.all_to_all(packed, ('section', 'qq'), split_axis=0, concat_axis=0, ti...  25.2 us
    all_gather x1, blocking collectives, body(): all_q = lax.all_gather(queries, 'qq', axis=0, tiled=True)  22.1 us
    all_to_all x1, starting transfers between devices, body(): lax.all_to_all(packed, ('section', 'qq'), split_axis=0, concat_axis=0, ti...  15.3 us
    all_gather x1, blocking collectives, body(): flags = lax.all_gather(block_map, 'qq', axis=1, tiled=True)  11.1 us
  transfers between devices with their start and end apart: 2, of which 2 were waited for; matrix products, arithmetic and copies ran while one was open for 1% of the time, Pallas kernels for 0%

profile of v13, /device:TPU:1, one launch (start us, length us, event | category | flops | bytes accessed | tf_op | source)
XLA Modules:
  0.0 208.0 jit_solution(5794423121099961340)
XLA Ops:
  7.3 0.9 slice_bitcast_fusion.1
  8.1 1.0 convert_multiply_fusion.1
  9.9 0.8 pad_maximum_fusion.1
  11.2 0.2 copy.82
  11.4 0.2 fusion.1
  11.8 22.1 %all_gather.10.q_ref = bf16[4,132,768]{2,1,0:T(8,128)(2,1)S(1)} all-gather(bf16[1,132,768]{2,1,0:T(8,128)(2,1)S(1)} %copy.83), channel_id=1, replica_groups=mesh['section'=4,'kk'=16,'qq'=4] {'qq'}, dimensions={0}, use_global_device_ids=true | all-gather | bytes 1013760 | tf_op jit(solution)/shard_map/all_gather | solution.py:132
  34.0 11.1 %all_gather.9 = s32[6,4,64]{2,0,1:T(8,128)S(1)} all-gather(s32[6,1,64]{2,0,1:T(8,128)S(1)} %copy.79), channel_id=1, replica_groups=mesh['section'=4,'kk'=16,'qq'=4] {'qq'}, dimensions={1}, use_global_device_ids=true | all-gather | bytes 7680 | tf_op jit(solution)/shard_map/all_gather | solution.py:134
  45.2 0.6 convert_reduce_fusion.1
  45.9 36.6 %all-gather.2.cloned.1.call-done.ki_ref.vi_ref = bf16[2,16,132,768]{3,2,1,0:T(8,128)(2,1)} async-done(((bf16[2,1,132,768]{3,2,1,0:T(8,128)(2,1)}), bf16[2,16,132,768]{3,2,1,0:T(8,128)(2,1)}) %all-gather.2.cloned.1.call-update) | async-done | bytes 6488080 | tf_op jit(solution)/shard_map/all_gather | solution.py:133
  82.5 1.1 fusion.12
  83.7 69.2 %shard_map.95 = (f32[4,132,768]{2,1,0:T(8,128)S(1)}, f32[4,132,128]{2,1,0:T(8,128)S(1)}) custom-call(s32[384]{0:T(512)S(1)} %reshape.160.fl_ref, bf16[4,132,768]{2,1,0:T(8,128)(2,1)S(1)} %all_gather.10.q_ref, bf16[16,768]{1,0:T(8,128)(2,1)S(1)} %reshape.148.qt_ref, bf16[2,16,132,768]{3,2,1,0:T(8,128)(2,1)} %all-gather.2.cloned.1.call-done.ki_ref.vi_ref, ...), custom_call_target="tpu_custom_call" | custom-call | tf_op jit(solution)/shard_map/pallas_call | solution.py:102
  154.1 0.2 reshape.149
  154.7 0.3 concatenate.29
  154.9 1.0 copy.98
  156.0 15.3 %all-to-all-start = ((bf16[16,224,128]{2,1,0:T(8,128)(2,1)}), bf16[16,224,128]{2,1,0:T(8,128)(2,1)S(1)}, u32[]{:S(2)}, u32[]{:S(2)}) async-start(bf16[16,224,128]{2,1,0:T(8,128)(2,1)} %bitcast.31), calls=%async_computation | async-start | bytes 1835008 | tf_op jit(solution)/shard_map/all_to_all | solution.py:166
  171.3 25.2 %all-to-all-done = bf16[16,224,128]{2,1,0:T(8,128)(2,1)S(1)} async-done(((bf16[16,224,128]{2,1,0:T(8,128)(2,1)}), bf16[16,224,128]{2,1,0:T(8,128)(2,1)S(1)}, u32[]{:S(2)}, u32[]{:S(2)}) %all-to-all-start) | async-done | bytes 917536 | tf_op jit(solution)/shard_map/all_to_all | solution.py:166
  196.5 0.3 reshape.154
  196.8 1.2 convert_reduce_fusion
  198.1 0.3 reshape.155
  198.4 0.2 reshape.156
  199.0 0.2 divide_convert_fusion
  199.3 0.2 reshape.157
  199.7 0.8 reshape.158
  200.5 0.6 copy.109
  (78 shorter events, 3.7 us)
Async XLA Ops:
  7.2 2.6 %copy-start = (bf16[128,768]{1,0:T(8,128)(2,1)S(1)}, bf16[128,768]{1,0:T(8,128)(2,1)}, u32[]{:S(2)}) copy-start(bf16[128,768]{1,0:T(8,128)(2,1)} %param.9) | copy-start | bytes 589828
  7.2 2.3 %copy-start.3 = (bf16[4,768]{1,0:T(4,128)(2,1)S(1)}, bf16[4,768]{1,0:T(4,128)(2,1)}, u32[]{:S(2)}) copy-start(bf16[4,768]{1,0:T(4,128)(2,1)} %param.12) | copy-start | bytes 18436
  7.2 2.6 %copy-start.1 = (bf16[128,768]{1,0:T(8,128)(2,1)S(1)}, bf16[128,768]{1,0:T(8,128)(2,1)}, u32[]{:S(2)}) copy-start(bf16[128,768]{1,0:T(8,128)(2,1)} %param.10) | copy-start | bytes 589828
  7.2 2.6 %copy-start.5 = (bf16[4,768]{1,0:T(4,128)(2,1)S(1)}, bf16[4,768]{1,0:T(4,128)(2,1)}, u32[]{:S(2)}) copy-start(bf16[4,768]{1,0:T(4,128)(2,1)} %param.13) | copy-start | bytes 18436
  7.2 75.3 %all-gather.2.cloned.1.call-start = ((), (), s32[]{:S(2)}) async-start(), calls=%async_computation.1 | async-start | bytes 7102464 | tf_op jit(solution)/shard_map/all_gather | solution.py:133
  9.3 1.4 copy-start.2
  9.5 1.4 copy-start.4
  10.9 23.0 %copy-start.6 = (s32[6,1,64]{2,1,0:T(1,128)S(1)}, s32[6,1,64]{2,1,0:T(1,128)}, u32[]{:S(2)}) copy-start(s32[6,1,64]{2,1,0:T(1,128)} %param.15) | copy-start | bytes 4612
  156.0 40.5 %all-to-all-start = ((bf16[16,224,128]{2,1,0:T(8,128)(2,1)}), bf16[16,224,128]{2,1,0:T(8,128)(2,1)S(1)}, u32[]{:S(2)}, u32[]{:S(2)}) async-start(bf16[16,224,128]{2,1,0:T(8,128)(2,1)} %bitcast.31), calls=%async_computation | async-start | bytes 1835008 | tf_op jit(solution)/shard_map/all_to_all | solution.py:166
Sparse Core Ops, SparseCore 0:
  10.8 71.6 all-gather.1

commit v14 on v9

--- a/solution.py
+++ b/solution.py
@@ -104,22 +104,23 @@
     queries = jnp.concatenate(
         [normed(q_img, norm_gains[0], heads), normed(q_txt, norm_gains[2], heads)], axis=0
     ).reshape(1, stride, width)
-    keys = jnp.concatenate(
-        [normed(k_img, norm_gains[1], heads), normed(k_txt, norm_gains[3], heads)], axis=0
-    ).reshape(1, stride, width)
-    values = jnp.concatenate([v_img, v_txt], axis=0).reshape(1, stride, width)
-    pair = jnp.stack([keys, values], axis=0)
+    keys_image = normed(k_img, norm_gains[1], heads).reshape(1, rows, width)
+    keys_text = normed(k_txt, norm_gains[3], heads).reshape(1, text_rows, width)
+    pair = jnp.stack([keys_image, v_img.reshape(1, rows, width)], axis=0)
+    text_pair = jnp.concatenate([keys_text, v_txt.reshape(1, text_rows, width)], axis=0)
 
     all_q = lax.all_gather(queries, "qq", axis=0, tiled=True)
     all_kv = lax.all_gather(pair, "kk", axis=1, tiled=True)
+    text_spread = jnp.broadcast_to(text_pair[None], (groups_k,) + text_pair.shape)
+    all_text = lax.all_to_all(text_spread, "kk", split_axis=0, concat_axis=0, tiled=True)
     flags = lax.all_gather(block_map, "qq", axis=1, tiled=True)
     flags = flags.reshape(heads, groups_q, groups_k, groups_q)
     flags = lax.dynamic_index_in_dim(flags, own_q, axis=3, keepdims=False)
     flags = jnp.repeat(flags, BLOCK, axis=2)
 
     qt = all_q[:, rows:].reshape(groups_q * text_rows, width)
-    kt = all_kv[0, :, rows:].reshape(groups_k * text_rows, width)
-    vt = all_kv[1, :, rows:].reshape(groups_k * text_rows, width)
+    kt = all_text[:, 0].reshape(groups_k * text_rows, width)
+    vt = all_text[:, 1].reshape(groups_k * text_rows, width)
 
     numer, denom = attend(all_q, qt, all_kv, kt, vt, flags, heads, head_size)
     denom = denom[:, :, :heads]

time: 145 us -> 141 us (0.972)
  waiting for transfers between devices: 61.7 us -> 52.2 us
  starting transfers between devices: 7.92 us -> 15.5 us
    all_gather x1, waiting for transfers between devices: 36.5 us -> 27 us  [body(): all_kv = lax.all_gather(pair, 'kk', axis=1, tiled=True)]
    all_to_all x0 -> x1, starting transfers between devices: none -> 7.57 us  [body(): lax.all_to_all(text_spread, 'kk', split_axis=0, concat_axis=0, tiled=True)]
  transfers between devices with their start and end apart: 2 -> 3, of which waited for: 2 -> 2; matrix products, arithmetic and copies ran while one was open for 1% -> 2% of each run, Pallas kernels for 0% -> 0%
where the time goes in v14:
time: 141 us
  waiting for transfers between devices  52.2 us (37%)
  blocking collectives  32 us (23%)
  starting transfers between devices  15.5 us (11%)
  between operations  14.6 us (10%)
  Pallas kernels  13.3 us (9%)
  local copies, waits for them, and re-layouts  9.22 us (7%)
  other arithmetic  4.34 us (3%)
    all_gather x1, waiting for transfers between devices, body(): all_kv = lax.all_gather(pair, 'kk', axis=1, tiled=True)  27 us
    all_to_all x1, waiting for transfers between devices, body(): lax.all_to_all(packed, ('section', 'qq'), split_axis=0, concat_axis=0, ti...  25.2 us
    all_gather x1, blocking collectives, body(): all_q = lax.all_gather(queries, 'qq', axis=0, tiled=True)  20.8 us
    pallas_call x1, Pallas kernels, attend(): pl.pallas_call(attend_kernel, grid=(heads,), in_specs=[pl.BlockSpec((grou...  13.3 us
    all_gather x1, blocking collectives, body(): flags = lax.all_gather(block_map, 'qq', axis=1, tiled=True)  11.2 us
    all_to_all x1, starting transfers between devices, body(): lax.all_to_all(packed, ('section', 'qq'), split_axis=0, concat_axis=0, ti...  7.86 us
    all_to_all x1, starting transfers between devices, body(): lax.all_to_all(text_spread, 'kk', split_axis=0, concat_axis=0, tiled=True)  7.57 us
  transfers between devices with their start and end apart: 3, of which 2 were waited for; matrix products, arithmetic and copies ran while one was open for 2% of the time, Pallas kernels for 0%

profile of v14, /device:TPU:1, one launch (start us, length us, event | category | flops | bytes accessed | tf_op | source)
XLA Modules:
  0.0 141.1 jit_solution(15197409853453438125)
XLA Ops:
  7.2 0.8 slice_bitcast_fusion
  8.1 1.0 convert_multiply_fusion.1
  9.6 0.8 pad_maximum_fusion.2
  10.7 0.7 broadcast_in_dim.10
  11.4 7.6 %all-to-all-start = ((bf16[16,2,4,768]{3,2,1,0:T(4,128)(2,1)}), bf16[16,2,4,768]{3,2,1,0:T(4,128)(2,1)S(1)}, u32[]{:S(2)}, u32[]{:S(2)}) async-start(bf16[16,2,4,768]{3,2,1,0:T(4,128)(2,1)} %broadcast_in_dim.10), calls=%async_computation | async-start | bytes 393216 | tf_op jit(solution)/shard_map/all_to_all | solution.py:115
  19.5 0.2 copy.80
  20.1 20.8 %all_gather.9.q_ref = bf16[4,132,768]{2,1,0:T(8,128)(2,1)S(1)} all-gather(bf16[1,132,768]{2,1,0:T(8,128)(2,1)S(1)} %copy.81), channel_id=1, replica_groups=mesh['section'=4,'kk'=16,'qq'=4] {'qq'}, dimensions={0}, use_global_device_ids=true | all-gather | bytes 1013760 | tf_op jit(solution)/shard_map/all_gather | solution.py:112
  40.9 11.2 %all_gather.11 = s32[6,4,64]{2,0,1:T(8,128)S(1)} all-gather(s32[6,1,64]{2,0,1:T(8,128)S(1)} %copy.84), channel_id=1, replica_groups=mesh['section'=4,'kk'=16,'qq'=4] {'qq'}, dimensions={1}, use_global_device_ids=true | all-gather | bytes 7680 | tf_op jit(solution)/shard_map/all_gather | solution.py:116
  52.3 0.6 dynamic-slice_reduce_fusion
  53.2 27.0 %all-gather.2.cloned.1.call-done.ki_ref.vi_ref = bf16[2,16,128,768]{3,2,1,0:T(8,128)(2,1)} async-done(((bf16[2,1,128,768]{3,2,1,0:T(8,128)(2,1)}), bf16[2,16,128,768]{3,2,1,0:T(8,128)(2,1)}) %all-gather.2.cloned.1.call-update) | async-done | bytes 6291472 | tf_op jit(solution)/shard_map/all_gather | solution.py:113
  80.3 13.3 %shard_map.95 = (f32[4,132,768]{2,1,0:T(8,128)S(1)}, f32[4,132,128]{2,1,0:T(8,128)S(1)}) custom-call(bf16[4,132,768]{2,1,0:T(8,128)(2,1)S(1)} %all_gather.9.q_ref, bf16[16,768]{1,0:T(8,128)(2,1)S(1)} %reshape.147.qt_ref, bf16[2,16,128,768]{3,2,1,0:T(8,128)(2,1)} %all-gather.2.cloned.1.call-done.ki_ref.vi_ref, bf16[64,768]{1,0:T(8,128)(2,1)S(1)} %reshape_squeeze.6.kt_ref, ...), custom_call_target="tpu_custom_call" | custom-call | tf_op jit(solution)/shard_map/pallas_call | solution.py:70
  94.7 0.2 reshape.151
  95.3 0.3 concatenate.24
  95.6 1.0 copy.98
  96.6 7.9 %all-to-all-start.1 = ((bf16[16,224,128]{2,1,0:T(8,128)(2,1)}), bf16[16,224,128]{2,1,0:T(8,128)(2,1)S(1)}, u32[]{:S(2)}, u32[]{:S(2)}) async-start(bf16[16,224,128]{2,1,0:T(8,128)(2,1)} %bitcast.33), calls=%async_computation.1 | async-start | bytes 1835008 | tf_op jit(solution)/shard_map/all_to_all | solution.py:148
  104.5 25.2 %all-to-all-done.1 = bf16[16,224,128]{2,1,0:T(8,128)(2,1)S(1)} async-done(((bf16[16,224,128]{2,1,0:T(8,128)(2,1)}), bf16[16,224,128]{2,1,0:T(8,128)(2,1)S(1)}, u32[]{:S(2)}, u32[]{:S(2)}) %all-to-all-start.1) | async-done | bytes 917536 | tf_op jit(solution)/shard_map/all_to_all | solution.py:148
  129.7 0.3 reshape.156
  130.0 1.2 convert_reduce_fusion
  131.3 0.3 reshape.157
  131.6 0.2 reshape.158
  132.2 0.2 divide_convert_fusion
  132.5 0.2 reshape.159
  132.9 0.8 reshape.160
  133.7 0.6 copy.109
  (82 shorter events, 4.1 us)
Async XLA Ops:
  7.2 2.3 %copy-start = (bf16[128,768]{1,0:T(8,128)(2,1)S(1)}, bf16[128,768]{1,0:T(8,128)(2,1)}, u32[]{:S(2)}) copy-start(bf16[128,768]{1,0:T(8,128)(2,1)} %param.9) | copy-start | bytes 589828
  7.2 2.4 %copy-start.2 = (bf16[128,768]{1,0:T(8,128)(2,1)S(1)}, bf16[128,768]{1,0:T(8,128)(2,1)}, u32[]{:S(2)}) copy-start(bf16[128,768]{1,0:T(8,128)(2,1)} %param.10) | copy-start | bytes 589828
  7.2 73.1 %all-gather.2.cloned.1.call-start = ((), (), s32[]{:S(2)}) async-start(), calls=%async_computation.2 | async-start | bytes 6684672 | tf_op jit(solution)/shard_map/all_gather | solution.py:113
  9.2 1.2 copy-start.3
  9.2 1.4 %copy-start.5 = (bf16[4,768]{1,0:T(4,128)(2,1)S(1)}, bf16[4,768]{1,0:T(4,128)(2,1)}, u32[]{:S(2)}) copy-start(bf16[4,768]{1,0:T(4,128)(2,1)} %param.13) | copy-start | bytes 18436
  9.3 9.7 %copy-start.1 = (bf16[128,768]{1,0:T(8,128)(2,1)S(1)}, bf16[128,768]{1,0:T(8,128)(2,1)}, u32[]{:S(2)}) copy-start(bf16[128,768]{1,0:T(8,128)(2,1)} %param.8) | copy-start | bytes 589828
  9.5 9.8 %copy-start.4 = (bf16[4,768]{1,0:T(4,128)(2,1)S(1)}, bf16[4,768]{1,0:T(4,128)(2,1)}, u32[]{:S(2)}) copy-start(bf16[4,768]{1,0:T(4,128)(2,1)} %param.11) | copy-start | bytes 18436
  11.4 41.7 %all-to-all-start = ((bf16[16,2,4,768]{3,2,1,0:T(4,128)(2,1)}), bf16[16,2,4,768]{3,2,1,0:T(4,128)(2,1)S(1)}, u32[]{:S(2)}, u32[]{:S(2)}) async-start(bf16[16,2,4,768]{3,2,1,0:T(4,128)(2,1)} %broadcast_in_dim.10), calls=%async_computation | async-start | bytes 393216 | tf_op jit(solution)/shard_map/all_to_all | solution.py:115
  19.2 21.7 %copy-start.6 = (s32[6,1,64]{2,1,0:T(1,128)S(1)}, s32[6,1,64]{2,1,0:T(1,128)}, u32[]{:S(2)}) copy-start(s32[6,1,64]{2,1,0:T(1,128)} %param.15) | copy-start | bytes 4612
  96.6 33.1 %all-to-all-start.1 = ((bf16[16,224,128]{2,1,0:T(8,128)(2,1)}), bf16[16,224,128]{2,1,0:T(8,128)(2,1)S(1)}, u32[]{:S(2)}, u32[]{:S(2)}) async-start(bf16[16,224,128]{2,1,0:T(8,128)(2,1)} %bitcast.33), calls=%async_computation.1 | async-start | bytes 1835008 | tf_op jit(solution)/shard_map/all_to_all | solution.py:148
Sparse Core Ops, SparseCore 0:
  10.5 69.6 all-gather.1

commit v15 on v14

--- a/solution.py
+++ b/solution.py
@@ -1,3 +1,5 @@
+import math
+
 import jax
 import jax.numpy as jnp
 from jax import lax
@@ -19,7 +21,7 @@
 def attend_kernel(q_ref, qt_ref, ki_ref, kt_ref, vi_ref, vt_ref, fl_ref, num_ref, den_ref):
     head = pl.program_id(0)
     head_size = q_ref.shape[-1]
-    scale = head_size ** (-0.5)
+    scale = head_size ** (-0.5) * math.log2(math.e)
     q_blocks = q_ref.shape[0]
     text_rows = qt_ref.shape[0] // q_blocks
     dims = (((1,), (1,)), ((), ()))
@@ -35,10 +37,10 @@
     def one(q, flags):
         s_img = lax.dot_general(q, keys_img, dims, preferred_element_type=jnp.float32) * scale
         s_txt = lax.dot_general(q, keys_txt, dims, preferred_element_type=jnp.float32) * scale
-        e_img = jnp.exp(s_img)
+        e_img = jnp.exp2(s_img)
         if flags is not None:
             e_img = jnp.where(flags > 0, e_img, jnp.float32(0.0))
-        e_txt = jnp.exp(s_txt)
+        e_txt = jnp.exp2(s_txt)
         den = jnp.sum(e_img, axis=1, keepdims=True) + jnp.sum(e_txt, axis=1, keepdims=True)
         num = jnp.dot(e_img.astype(jnp.bfloat16), vals_img, preferred_element_type=jnp.float32)
         num = num + jnp.dot(e_txt.astype(jnp.bfloat16), vals_txt, preferred_element_type=jnp.float32)

time: 141 us -> 141 us (level)
  no operation moved by 1% of the time
where the time goes in v15:
time: 141 us
  waiting for transfers between devices  52.2 us (37%)
  blocking collectives  32 us (23%)
  starting transfers between devices  15.5 us (11%)
  between operations  14.6 us (10%)
  Pallas kernels  12.8 us (9%)
  local copies, waits for them, and re-layouts  9.22 us (7%)
  other arithmetic  4.34 us (3%)
    all_gather x1, waiting for transfers between devices, body(): all_kv = lax.all_gather(pair, 'kk', axis=1, tiled=True)  27 us
    all_to_all x1, waiting for transfers between devices, body(): lax.all_to_all(packed, ('section', 'qq'), split_axis=0, concat_axis=0, ti...  25.2 us
    all_gather x1, blocking collectives, body(): all_q = lax.all_gather(queries, 'qq', axis=0, tiled=True)  20.8 us
    pallas_call x1, Pallas kernels, attend(): pl.pallas_call(attend_kernel, grid=(heads,), in_specs=[pl.BlockSpec((grou...  12.8 us
    all_gather x1, blocking collectives, body(): flags = lax.all_gather(block_map, 'qq', axis=1, tiled=True)  11.2 us
    all_to_all x1, starting transfers between devices, body(): lax.all_to_all(packed, ('section', 'qq'), split_axis=0, concat_axis=0, ti...  7.85 us
    all_to_all x1, starting transfers between devices, body(): lax.all_to_all(text_spread, 'kk', split_axis=0, concat_axis=0, tiled=True)  7.57 us
  transfers between devices with their start and end apart: 3, of which 2 were waited for; matrix products, arithmetic and copies ran while one was open for 2% of the time, Pallas kernels for 0%

profile of v15, /device:TPU:1, one launch (start us, length us, event | category | flops | bytes accessed | tf_op | source)
XLA Modules:
  0.0 140.6 jit_solution(4730771582637721362)
XLA Ops:
  7.2 0.8 slice_bitcast_fusion
  8.1 1.0 convert_multiply_fusion.1
  9.6 0.8 pad_maximum_fusion.2
  10.7 0.7 broadcast_in_dim.10
  11.4 7.6 %all-to-all-start = ((bf16[16,2,4,768]{3,2,1,0:T(4,128)(2,1)}), bf16[16,2,4,768]{3,2,1,0:T(4,128)(2,1)S(1)}, u32[]{:S(2)}, u32[]{:S(2)}) async-start(bf16[16,2,4,768]{3,2,1,0:T(4,128)(2,1)} %broadcast_in_dim.10), calls=%async_computation | async-start | bytes 393216 | tf_op jit(solution)/shard_map/all_to_all | solution.py:117
  19.5 0.2 copy.80
  20.1 20.8 %all_gather.9.q_ref = bf16[4,132,768]{2,1,0:T(8,128)(2,1)S(1)} all-gather(bf16[1,132,768]{2,1,0:T(8,128)(2,1)S(1)} %copy.81), channel_id=1, replica_groups=mesh['section'=4,'kk'=16,'qq'=4] {'qq'}, dimensions={0}, use_global_device_ids=true | all-gather | bytes 1013760 | tf_op jit(solution)/shard_map/all_gather | solution.py:114
  40.9 11.2 %all_gather.11 = s32[6,4,64]{2,0,1:T(8,128)S(1)} all-gather(s32[6,1,64]{2,0,1:T(8,128)S(1)} %copy.84), channel_id=1, replica_groups=mesh['section'=4,'kk'=16,'qq'=4] {'qq'}, dimensions={1}, use_global_device_ids=true | all-gather | bytes 7680 | tf_op jit(solution)/shard_map/all_gather | solution.py:118
  52.3 0.6 dynamic-slice_reduce_fusion
  53.2 27.0 %all-gather.2.cloned.1.call-done.ki_ref.vi_ref = bf16[2,16,128,768]{3,2,1,0:T(8,128)(2,1)} async-done(((bf16[2,1,128,768]{3,2,1,0:T(8,128)(2,1)}), bf16[2,16,128,768]{3,2,1,0:T(8,128)(2,1)}) %all-gather.2.cloned.1.call-update) | async-done | bytes 6291472 | tf_op jit(solution)/shard_map/all_gather | solution.py:115
  80.3 12.8 %shard_map.95 = (f32[4,132,768]{2,1,0:T(8,128)S(1)}, f32[4,132,128]{2,1,0:T(8,128)S(1)}) custom-call(bf16[4,132,768]{2,1,0:T(8,128)(2,1)S(1)} %all_gather.9.q_ref, bf16[16,768]{1,0:T(8,128)(2,1)S(1)} %reshape.147.qt_ref, bf16[2,16,128,768]{3,2,1,0:T(8,128)(2,1)} %all-gather.2.cloned.1.call-done.ki_ref.vi_ref, bf16[64,768]{1,0:T(8,128)(2,1)S(1)} %reshape_squeeze.6.kt_ref, ...), custom_call_target="tpu_custom_call" | custom-call | tf_op jit(solution)/shard_map/pallas_call | solution.py:72
  94.2 0.2 reshape.151
  94.8 0.3 concatenate.24
  95.1 1.0 copy.98
  96.2 7.9 %all-to-all-start.1 = ((bf16[16,224,128]{2,1,0:T(8,128)(2,1)}), bf16[16,224,128]{2,1,0:T(8,128)(2,1)S(1)}, u32[]{:S(2)}, u32[]{:S(2)}) async-start(bf16[16,224,128]{2,1,0:T(8,128)(2,1)} %bitcast.33), calls=%async_computation.1 | async-start | bytes 1835008 | tf_op jit(solution)/shard_map/all_to_all | solution.py:150
  104.0 25.2 %all-to-all-done.1 = bf16[16,224,128]{2,1,0:T(8,128)(2,1)S(1)} async-done(((bf16[16,224,128]{2,1,0:T(8,128)(2,1)}), bf16[16,224,128]{2,1,0:T(8,128)(2,1)S(1)}, u32[]{:S(2)}, u32[]{:S(2)}) %all-to-all-start.1) | async-done | bytes 917536 | tf_op jit(solution)/shard_map/all_to_all | solution.py:150
  129.2 0.3 reshape.156
  129.5 1.2 convert_reduce_fusion
  130.8 0.3 reshape.157
  131.1 0.2 reshape.158
  131.7 0.2 divide_convert_fusion
  132.0 0.2 reshape.159
  132.4 0.8 reshape.160
  133.2 0.6 copy.109
  (82 shorter events, 4.1 us)
Async XLA Ops:
  7.2 2.3 %copy-start = (bf16[128,768]{1,0:T(8,128)(2,1)S(1)}, bf16[128,768]{1,0:T(8,128)(2,1)}, u32[]{:S(2)}) copy-start(bf16[128,768]{1,0:T(8,128)(2,1)} %param.9) | copy-start | bytes 589828
  7.2 2.4 %copy-start.2 = (bf16[128,768]{1,0:T(8,128)(2,1)S(1)}, bf16[128,768]{1,0:T(8,128)(2,1)}, u32[]{:S(2)}) copy-start(bf16[128,768]{1,0:T(8,128)(2,1)} %param.10) | copy-start | bytes 589828
  7.2 73.1 %all-gather.2.cloned.1.call-start = ((), (), s32[]{:S(2)}) async-start(), calls=%async_computation.2 | async-start | bytes 6684672 | tf_op jit(solution)/shard_map/all_gather | solution.py:115
  9.2 1.2 copy-start.3
  9.2 1.4 %copy-start.5 = (bf16[4,768]{1,0:T(4,128)(2,1)S(1)}, bf16[4,768]{1,0:T(4,128)(2,1)}, u32[]{:S(2)}) copy-start(bf16[4,768]{1,0:T(4,128)(2,1)} %param.13) | copy-start | bytes 18436
  9.3 9.7 %copy-start.1 = (bf16[128,768]{1,0:T(8,128)(2,1)S(1)}, bf16[128,768]{1,0:T(8,128)(2,1)}, u32[]{:S(2)}) copy-start(bf16[128,768]{1,0:T(8,128)(2,1)} %param.8) | copy-start | bytes 589828
  9.5 9.8 %copy-start.4 = (bf16[4,768]{1,0:T(4,128)(2,1)S(1)}, bf16[4,768]{1,0:T(4,128)(2,1)}, u32[]{:S(2)}) copy-start(bf16[4,768]{1,0:T(4,128)(2,1)} %param.11) | copy-start | bytes 18436
  11.4 41.7 %all-to-all-start = ((bf16[16,2,4,768]{3,2,1,0:T(4,128)(2,1)}), bf16[16,2,4,768]{3,2,1,0:T(4,128)(2,1)S(1)}, u32[]{:S(2)}, u32[]{:S(2)}) async-start(bf16[16,2,4,768]{3,2,1,0:T(4,128)(2,1)} %broadcast_in_dim.10), calls=%async_computation | async-start | bytes 393216 | tf_op jit(solution)/shard_map/all_to_all | solution.py:117
  19.2 21.7 %copy-start.6 = (s32[6,1,64]{2,1,0:T(1,128)S(1)}, s32[6,1,64]{2,1,0:T(1,128)}, u32[]{:S(2)}) copy-start(s32[6,1,64]{2,1,0:T(1,128)} %param.15) | copy-start | bytes 4612
  96.2 33.1 %all-to-all-start.1 = ((bf16[16,224,128]{2,1,0:T(8,128)(2,1)}), bf16[16,224,128]{2,1,0:T(8,128)(2,1)S(1)}, u32[]{:S(2)}, u32[]{:S(2)}) async-start(bf16[16,224,128]{2,1,0:T(8,128)(2,1)} %bitcast.33), calls=%async_computation.1 | async-start | bytes 1835008 | tf_op jit(solution)/shard_map/all_to_all | solution.py:150
Sparse Core Ops, SparseCore 0:
  10.5 69.6 all-gather.1
